TPU v7x, 512 devices: a whole 4x4x16 slice. The times are simulated.
512 devices in a mesh: req: 8 (over x, core), gx: 8 (over z_lo), gy: 8 (over y, z_hi).
Axes of the slice: x: 4, y: 4, z: 16 (z_hi: 2, z_lo: 8; z = z_hi * 8 + z_lo), core: 2. Of those that a mesh axis runs over, the one named last changes fastest.
Arguments:
- hidden: bfloat16 [6144, 4096], P(('req', 'gx'), 'gy')
- ln_gain: float32 [4096], P('gy'), may hold values from 0.25 to 1.75
- w_qkv: bfloat16 [4096, 32, 384], P('gy', 'gx'), may hold values from -0.09375 to 0.09375
- w_out: bfloat16 [4096, 4096], P('gx', 'gy'), may hold values from -0.375 to 0.375
- kv_cache: bfloat16 [16, 2176, 2, 4096], P('req', 'gy', None, 'gx')
- cache_len: int32 [16], P('req'), may hold values from 0 to 1792, as said below
Outputs:
- mixed: bfloat16 [6144, 4096], P(('req', 'gx'), 'gy')
- cache_out: bfloat16 [16, 2176, 2, 4096], P('req', 'gy', None, 'gx')
Inputs may be any that keep to these rules, and one draw needn't show every extreme that they name: `cache_len`: cached lengths are heavy-tailed; some request has exactly 1792.
All inputs are finite; a program needn't handle non-finite values.
Results may differ from a plain program's by a relative error of at most 0.04.
Values may be sent and summed in bfloat16 or wider, within the bound.
No kernel may reach another device: no remote copies, remote signals or barrier semaphores. Data moves between devices by JAX's collectives and lax.ppermute only.
A program may use at most 64 MiB of HBM per device.

v0:
```python
import math

import jax
import jax.numpy as jnp
from jax import lax
from jax.sharding import PartitionSpec as P

D = 4096


norm_eps = 1e-05
floor_score = -1e30


def partial_attend(query, keys, values, valid, distance, slopes, scale):
    scores = jnp.einsum("chd,phd->chp", query, keys, preferred_element_type=jnp.float32) * scale
    scores = scores - slopes[None, :, None] * distance.astype(jnp.float32)[:, None, :]
    scores = jnp.where(valid[:, None, :], scores, floor_score)
    highest = jnp.max(scores, axis=-1)
    weights = jnp.where(valid[:, None, :], jnp.exp(scores - highest[..., None]), 0.0)
    totals = jnp.sum(weights, axis=-1)
    accum = jnp.einsum(
        "chp,phd->chd", weights.astype(jnp.bfloat16), values, preferred_element_type=jnp.float32
    )
    return (highest, totals, accum)


def write_cache(fresh_rows, cache_block, positions, length, group):
    offset = positions - length
    inside = (offset >= 0) & (offset < group)
    taken = jnp.take(fresh_rows, jnp.clip(offset, 0, group - 1), axis=0)
    return jnp.where(inside[:, None, None], taken, cache_block)


def shards(hidden, ln_gain, w_qkv, w_out, kv_cache, cache_len):
    hidden_f = hidden.astype(jnp.float32)
    sums = lax.psum((jnp.sum(hidden_f, axis=1), jnp.sum(hidden_f * hidden_f, axis=1)), "gy")
    mean = sums[0] / D
    var = sums[1] / D - mean * mean
    normed = (
        (hidden_f - mean[:, None]) * lax.rsqrt(var + norm_eps)[:, None] * ln_gain[None, :]
    ).astype(jnp.bfloat16)
    local_heads = w_qkv.shape[1]
    head_size = w_qkv.shape[2] // 3
    weight_flat = w_qkv.reshape(w_qkv.shape[0], local_heads * 3 * head_size)
    partial_value = jnp.dot(
        lax.all_gather(normed, "gx", axis=0, tiled=True),
        weight_flat,
        preferred_element_type=jnp.float32,
    )
    requests = cache_len.shape[0]
    all_rows = partial_value.shape[0]
    group = all_rows // requests
    width_local = local_heads * head_size
    block = kv_cache.shape[1]
    positions = lax.axis_index("gy") * block + jnp.arange(block, dtype=jnp.int32)
    head_ids = lax.axis_index("gx") * local_heads + jnp.arange(local_heads, dtype=jnp.int32)
    all_heads = local_heads * lax.axis_size("gx")
    slopes = jnp.exp2(-8.0 * (head_ids + 1).astype(jnp.float32) / all_heads)
    scale = 1.0 / math.sqrt(head_size)
    steps_c = jnp.arange(group, dtype=jnp.int32)
    tops_list = []
    totals_list = []
    accum_list = []
    caches = []
    qkv = lax.psum(partial_value.astype(jnp.bfloat16), "gy")
    qkv = qkv.reshape(requests, group, local_heads, 3 * head_size)
    fresh = jnp.stack(
        [
            qkv[:, :, :, head_size : 2 * head_size].reshape(requests, group, width_local),
            qkv[:, :, :, 2 * head_size :].reshape(requests, group, width_local),
        ],
        axis=2,
    )
    for request in range(requests):
        length = cache_len[request]
        updated = write_cache(fresh[request], kv_cache[request], positions, length, group)
        caches.append(updated)
        keys = updated[:, 0].reshape(block, local_heads, head_size)
        values = updated[:, 1].reshape(block, local_heads, head_size)
        distance = (length + steps_c)[:, None] - positions[None, :]
        part_top, part_total, part_accum = partial_attend(
            qkv[request, :, :, :head_size], keys, values, distance >= 0, distance, slopes, scale
        )
        tops_list.append(part_top)
        totals_list.append(part_total)
        accum_list.append(part_accum)
    tops = jnp.stack(tops_list)
    totals = jnp.stack(totals_list)
    accums = jnp.stack(accum_list)
    overall = lax.pmax(tops, "gy")
    factor = jnp.exp(tops - overall)
    joined_totals, joined_accums = (
        lax.psum((totals * factor).astype(jnp.bfloat16), "gy").astype(jnp.float32),
        lax.psum((accums * factor[..., None]).astype(jnp.bfloat16), "gy").astype(jnp.float32),
    )
    attn = (
        (joined_accums / joined_totals[..., None])
        .astype(jnp.bfloat16)
        .reshape(requests * group, width_local)
    )
    projected = lax.psum_scatter(
        jnp.dot(attn, w_out, preferred_element_type=jnp.float32).astype(jnp.bfloat16),
        "gx",
        scatter_dimension=0,
        tiled=True,
    ).astype(jnp.float32)
    mixed = (projected + hidden_f).astype(jnp.bfloat16)
    return (mixed, jnp.stack(caches))


def solution(mesh):
    in_specs = (
        P(("req", "gx"), "gy"),
        P("gy"),
        P("gy", "gx", None),
        P("gx", "gy"),
        P("req", "gy", None, "gx"),
        P("req"),
    )
    out_specs = (P(("req", "gx"), "gy"), P("req", "gy", None, "gx"))
    return jax.shard_map(shards, mesh=mesh, in_specs=in_specs, out_specs=out_specs, check_vma=False)
```

profile of v0, /device:TPU:6, one launch (start us, length us, event | category | flops | bytes accessed | tf_op | source)
XLA Modules:
  0.0 905.0 jit_solution(9160782233411214175)
XLA Ops:
  8.3 49.8 %all-reduce = (f32[96]{0:T(128)S(1)}, f32[96]{0:T(128)S(1)}) all-reduce(f32[96]{0:T(128)S(1)} %get-tuple-element.10, f32[96]{0:T(128)S(1)} %get-tuple-element.9), channel_id=1, replica_groups=mesh['req'=8,'gx'=8,'gy'=8] {'gy'}, use_global_device_ids=true, to_apply=%region_3.0 | all-reduce | flops 192 | bytes 1536 | tf_op jit(solution)/shard_map/psum | solution.py:37
  59.1 48.9 %all_gather.3 = bf16[768,512]{1,0:T(8,128)(2,1)S(1)} all-gather(bf16[96,512]{1,0:T(8,128)(2,1)S(1)} %fusion.30), channel_id=1, replica_groups=mesh['req'=8,'gx'=8,'gy'=8] {'gx'}, dimensions={0}, use_global_device_ids=true | all-gather | bytes 884736 | tf_op jit(solution)/shard_map/all_gather | solution.py:47
  108.0 1.7 copy.38
  109.7 2.8 convolution_convert_fusion
  112.5 4.1 reshape.154
  116.6 1.7 copy.24
  126.1 392.3 %all-reduce.4.cloned.1.call-done = bf16[2,384,4,384]{3,1,2,0:T(8,128)(2,1)} async-done(((bf16[2,384,4,384]{3,1,2,0:T(8,128)(2,1)}), bf16[2,384,4,384]{3,1,2,0:T(8,128)(2,1)}) %all-reduce.4.cloned.1.call-update) | async-done | bytes 2359312 | tf_op jit(solution)/shard_map/psum | solution.py:66
  518.4 1.5 fusion.37
  521.0 3.5 copy.27
  525.7 4.8 copy.28
  530.5 5.4 fusion.19
  535.9 3.0 gather_fusion
  538.9 3.5 gather_fusion.1
  542.4 5.5 broadcast_select_fusion.1
  547.9 2.3 slice_reduce_fusion.3
  550.3 2.3 slice_reduce_fusion.1
  552.6 1.5 fusion.39
  555.4 1.5 fusion.40
  557.8 70.5 %pmax.7 = f32[2,384,4]{1,2,0:T(4,128)S(1)} all-reduce(f32[2,384,4]{1,2,0:T(4,128)S(1)} %pad_maximum_fusion.2), channel_id=1, replica_groups=mesh['req'=8,'gx'=8,'gy'=8] {'gy'}, use_global_device_ids=true, to_apply=%region_7.9 | all-reduce | flops 3072 | bytes 24576 | tf_op jit(solution)/shard_map/pmax | solution.py:91
  629.4 40.7 %psum.39 = bf16[2,384,4]{1,2,0:T(4,128)(2,1)S(1)} all-reduce(bf16[2,384,4]{1,2,0:T(4,128)(2,1)S(1)} %get-tuple-element.13), channel_id=1, replica_groups=mesh['req'=8,'gx'=8,'gy'=8] {'gy'}, use_global_device_ids=true, to_apply=%region_11.13 | all-reduce | flops 3072 | bytes 12288 | tf_op jit(solution)/shard_map/psum | solution.py:94
  670.1 161.4 %all-reduce.6.cloned.1.call-done = bf16[2,384,4,128]{1,3,2,0:T(8,128)(2,1)} async-done(((bf16[2,384,4,128]{1,3,2,0:T(8,128)(2,1)}), bf16[2,384,4,128]{1,3,2,0:T(8,128)(2,1)}) %all-reduce.6.cloned.1.call-update) | async-done | bytes 786448 | tf_op jit(solution)/shard_map/psum | solution.py:95
  834.9 2.6 pad_maximum_fusion
  837.5 59.4 %reduce-scatter.2.cloned.1.call-done = bf16[96,512]{1,0:T(8,128)(2,1)} async-done(((bf16[768,512]{1,0:T(8,128)(2,1)}), bf16[96,512]{1,0:T(8,128)(2,1)}) %reduce-scatter.2.cloned.1.call-update) | async-done | bytes 98320 | tf_op jit(solution)/shard_map/reduce_scatter | solution.py:102
  896.9 1.6 fusion.32
  (43 shorter events, 18.7 us)
Async XLA Ops:
  7.2 826.2 %copy-start = (bf16[512,512]{1,0:T(8,128)(2,1)S(1)}, bf16[512,512]{1,0:T(8,128)(2,1)}, u32[]{:S(2)}) copy-start(bf16[512,512]{1,0:T(8,128)(2,1)} %param.11) | copy-start | bytes 1572868
  7.2 511.2 %all-reduce.4.cloned.1.call-start = ((), (), s32[]{:S(2)}) async-start(), calls=%async_computation.1 | async-start | bytes 4718592 | tf_op jit(solution)/shard_map/psum | solution.py:66
  118.3 0.7 copy-start.4
  118.4 713.1 %all-reduce.6.cloned.1.call-start = ((), (), s32[]{:S(2)}) async-start(), calls=%async_computation.2 | async-start | bytes 1572864 | tf_op jit(solution)/shard_map/psum | solution.py:95
  547.9 4.6 copy-start.3
  554.4 1.0 copy-start.2
  629.3 267.6 %reduce-scatter.2.cloned.1.call-start = ((), (), s32[]{:S(2)}) async-start(), calls=%async_computation.3 | async-start | bytes 884736 | tf_op jit(solution)/shard_map/reduce_scatter | solution.py:102
  834.9 62.0 %copy-start.1 = (bf16[96,512]{1,0:T(8,128)(2,1)S(1)}, bf16[96,512]{1,0:T(8,128)(2,1)}, u32[]{:S(2)}) copy-start(bf16[96,512]{1,0:T(8,128)(2,1)} %param.8) | copy-start | bytes 294916
Sparse Core Ops, SparseCore 0:
  118.5 399.8 all-reduce.3
  629.5 202.0 all-reduce.5
  835.0 61.8 reduce-scatter.1
where the time goes:
time: 906 us; the launch traced here: 905 us
  waiting for transfers between devices  613 us (68%)
  blocking collectives  210 us (23%)
  local copies, waits for them, and re-layouts  32.9 us (4%)
  other arithmetic  26.6 us (3%)
  between operations  14 us (2%)
    psum x1, waiting for transfers between devices, shards(): qkv = lax.psum(partial_value.astype(jnp.bfloat16), 'gy')  392 us
    psum x1, waiting for transfers between devices, shards(): lax.psum((accums * factor[..., None]).astype(jnp.bfloat16), 'gy')  161 us
    pmax x1, blocking collectives, shards(): overall = lax.pmax(tops, 'gy')  70.5 us
    reduce_scatter x1, waiting for transfers between devices, shards(): lax.psum_scatter(jnp.dot(attn, w_out, preferred_element_type=jnp.float32)...  59.4 us
    psum x1, blocking collectives, shards(): lax.psum((jnp.sum(hidden_f, axis=1), jnp.sum(hidden_f * hidden_f, axis=1)...  49.8 us
    all_gather x1, blocking collectives, shards(): lax.all_gather(normed, 'gx', axis=0, tiled=True)  48.9 us
    psum x1, blocking collectives, shards(): lax.psum((totals * factor).astype(jnp.bfloat16), 'gy').astype(jnp.float32)  40.7 us
  transfers between devices with their start and end apart: 3, of which 3 were waited for; matrix products, arithmetic and copies ran while one was open for 1% of the time, Pallas kernels for 0%

commit v1 on v0

--- a/solution.py
+++ b/solution.py
@@ -3,6 +3,7 @@
 import jax
 import jax.numpy as jnp
 from jax import lax
+from jax.sharding import Mesh
 from jax.sharding import PartitionSpec as P
 
 D = 4096
@@ -10,6 +11,31 @@
 
 norm_eps = 1e-05
 floor_score = -1e30
+
+
+GY = ("gyy", "gyz")
+
+
+def gy_index():
+    return lax.axis_index("gyy") * lax.axis_size("gyz") + lax.axis_index("gyz")
+
+
+def gy_sum(x):
+    return lax.psum(lax.psum(x, "gyy"), "gyz")
+
+
+def gy_max(x):
+    return lax.pmax(lax.pmax(x, "gyz"), "gyy")
+
+
+def gy_sum_rows(x, twice):
+    part = lax.psum_scatter(x, "gyy", scatter_dimension=0, tiled=True)
+    if twice:
+        part = lax.psum_scatter(part, "gyz", scatter_dimension=0, tiled=True)
+        part = lax.all_gather(part, "gyz", axis=0, tiled=True)
+    else:
+        part = lax.psum(part, "gyz")
+    return lax.all_gather(part, "gyy", axis=0, tiled=True)
 
 
 def partial_attend(query, keys, values, valid, distance, slopes, scale):
@@ -34,7 +60,7 @@
 
 def shards(hidden, ln_gain, w_qkv, w_out, kv_cache, cache_len):
     hidden_f = hidden.astype(jnp.float32)
-    sums = lax.psum((jnp.sum(hidden_f, axis=1), jnp.sum(hidden_f * hidden_f, axis=1)), "gy")
+    sums = gy_sum((jnp.sum(hidden_f, axis=1), jnp.sum(hidden_f * hidden_f, axis=1)))
     mean = sums[0] / D
     var = sums[1] / D - mean * mean
     normed = (
@@ -53,7 +79,7 @@
     group = all_rows // requests
     width_local = local_heads * head_size
     block = kv_cache.shape[1]
-    positions = lax.axis_index("gy") * block + jnp.arange(block, dtype=jnp.int32)
+    positions = gy_index() * block + jnp.arange(block, dtype=jnp.int32)
     head_ids = lax.axis_index("gx") * local_heads + jnp.arange(local_heads, dtype=jnp.int32)
     all_heads = local_heads * lax.axis_size("gx")
     slopes = jnp.exp2(-8.0 * (head_ids + 1).astype(jnp.float32) / all_heads)
@@ -63,7 +89,7 @@
     totals_list = []
     accum_list = []
     caches = []
-    qkv = lax.psum(partial_value.astype(jnp.bfloat16), "gy")
+    qkv = gy_sum_rows(partial_value.astype(jnp.bfloat16), True)
     qkv = qkv.reshape(requests, group, local_heads, 3 * head_size)
     fresh = jnp.stack(
         [
@@ -88,12 +114,19 @@
     tops = jnp.stack(tops_list)
     totals = jnp.stack(totals_list)
     accums = jnp.stack(accum_list)
-    overall = lax.pmax(tops, "gy")
+    overall = gy_max(tops)
     factor = jnp.exp(tops - overall)
-    joined_totals, joined_accums = (
-        lax.psum((totals * factor).astype(jnp.bfloat16), "gy").astype(jnp.float32),
-        lax.psum((accums * factor[..., None]).astype(jnp.bfloat16), "gy").astype(jnp.float32),
+    rows = requests * group
+    packed = jnp.concatenate(
+        [
+            (accums * factor[..., None]).astype(jnp.bfloat16).reshape(rows, width_local),
+            (totals * factor).astype(jnp.bfloat16).reshape(rows, local_heads),
+        ],
+        axis=1,
     )
+    packed = gy_sum_rows(packed, False).astype(jnp.float32)
+    joined_accums = packed[:, :width_local].reshape(accums.shape)
+    joined_totals = packed[:, width_local:].reshape(totals.shape)
     attn = (
         (joined_accums / joined_totals[..., None])
         .astype(jnp.bfloat16)
@@ -110,13 +143,18 @@
 
 
 def solution(mesh):
+    n_gy = mesh.shape["gy"]
+    split = Mesh(
+        mesh.devices.reshape(mesh.shape["req"], mesh.shape["gx"], n_gy // 2, 2),
+        ("req", "gx") + GY,
+    )
     in_specs = (
-        P(("req", "gx"), "gy"),
-        P("gy"),
-        P("gy", "gx", None),
-        P("gx", "gy"),
-        P("req", "gy", None, "gx"),
+        P(("req", "gx"), GY),
+        P(GY),
+        P(GY, "gx", None),
+        P("gx", GY),
+        P("req", GY, None, "gx"),
         P("req"),
     )
-    out_specs = (P(("req", "gx"), "gy"), P("req", "gy", None, "gx"))
-    return jax.shard_map(shards, mesh=mesh, in_specs=in_specs, out_specs=out_specs, check_vma=False)
+    out_specs = (P(("req", "gx"), GY), P("req", GY, None, "gx"))
+    return jax.shard_map(shards, mesh=split, in_specs=in_specs, out_specs=out_specs, check_vma=False)

time: 906 us -> 532 us (0.59)
  waiting for transfers between devices: 613 us -> 270 us
  blocking collectives: 210 us -> 169 us
    psum x2 -> x1, waiting for transfers between devices: 554 us -> 71.8 us  [gy_sum_rows(): part = lax.psum(part, 'gyz')]
    reduce_scatter x0 -> x3, waiting for transfers between devices: none -> 116 us  [the longest x2 59.2 us: gy_sum_rows(): part = lax.psum_scatter(x, 'gyy', scatter_dimension=0, tiled=True)]
    psum x2, blocking collectives: 90.6 us -> 27.4 us  [gy_sum(): return lax.psum(lax.psum(x, 'gyy'), 'gyz')]
    all_gather x0 -> x2, blocking collectives: none -> 48.6 us  [the longest x1 34.1 us: gy_sum_rows(): part = lax.all_gather(part, 'gyz', axis=0, tiled=True)]
    pmax x1 -> x2, blocking collectives: 70.5 us -> 43.7 us  [gy_max(): return lax.pmax(lax.pmax(x, 'gyz'), 'gyy')]
    all_gather x0 -> x1, waiting for transfers between devices: none -> 26.3 us  [gy_sum_rows(): return lax.all_gather(part, 'gyy', axis=0, tiled=True)]
  transfers between devices with their start and end apart: 3 -> 6, of which waited for: 3 -> 6; matrix products, arithmetic and copies ran while one was open for 1% -> 2% of each run, Pallas kernels for 0% -> 0%
where the time goes in v1:
time: 532 us; the launch traced here: 531 us
  waiting for transfers between devices  270 us (51%)
  blocking collectives  169 us (32%)
  local copies, waits for them, and re-layouts  38.9 us (7%)
  other arithmetic  30.5 us (6%)
  between operations  14.4 us (3%)
  matrix products  7.5 us (1%)
    psum x1, waiting for transfers between devices, gy_sum_rows(): part = lax.psum(part, 'gyz')  71.8 us
    reduce_scatter x2, waiting for transfers between devices, gy_sum_rows(): part = lax.psum_scatter(x, 'gyy', scatter_dimension=0, tiled=True)  59.2 us
    reduce_scatter x1, waiting for transfers between devices, gy_sum_rows(): part = lax.psum_scatter(part, 'gyz', scatter_dimension=0, tiled=True)  56.5 us
    reduce_scatter x1, waiting for transfers between devices, shards(): lax.psum_scatter(jnp.dot(attn, w_out, preferred_element_type=jnp.float32)...  55.8 us
    all_gather x1, blocking collectives, shards(): lax.all_gather(normed, 'gx', axis=0, tiled=True)  49.5 us
    pmax x2, blocking collectives, gy_max(): return lax.pmax(lax.pmax(x, 'gyz'), 'gyy')  43.7 us
    all_gather x1, blocking collectives, gy_sum_rows(): part = lax.all_gather(part, 'gyz', axis=0, tiled=True)  34.1 us
    psum x2, blocking collectives, gy_sum(): return lax.psum(lax.psum(x, 'gyy'), 'gyz')  27.4 us
  transfers between devices with their start and end apart: 6, of which 6 were waited for; matrix products, arithmetic and copies ran while one was open for 2% of the time, Pallas kernels for 0%

profile of v1, /device:TPU:6, one launch (start us, length us, event | category | flops | bytes accessed | tf_op | source)
XLA Modules:
  0.0 530.6 jit_solution(7304780923316092833)
XLA Ops:
  8.3 10.7 %all-reduce = (f32[96]{0:T(128)S(1)}, f32[96]{0:T(128)S(1)}) all-reduce(f32[96]{0:T(128)S(1)} %get-tuple-element.8, f32[96]{0:T(128)S(1)} %get-tuple-element.7), channel_id=1, replica_groups=mesh['req'=8,'gx'=8,'gyy'=4,'gyz'=2] {'gyy'}, use_global_device_ids=true, to_apply=%region_4.0 | all-reduce | flops 192 | bytes 1536 | tf_op jit(solution)/shard_map/psum | solution.py:24
  19.0 16.7 %all-reduce.1 = (f32[96]{0:T(128)S(1)}, f32[96]{0:T(128)S(1)}) all-reduce(f32[96]{0:T(128)S(1)} %get-tuple-element.9, f32[96]{0:T(128)S(1)} %get-tuple-element.10), channel_id=1, replica_groups=mesh['req'=8,'gx'=8,'gyy'=4,'gyz'=2] {'gyz'}, use_global_device_ids=true, to_apply=%region_5.0 | all-reduce | flops 192 | bytes 1536 | tf_op jit(solution)/shard_map/psum | solution.py:24
  36.8 49.5 %all_gather.12 = bf16[768,512]{1,0:T(8,128)(2,1)S(1)} all-gather(bf16[96,512]{1,0:T(8,128)(2,1)S(1)} %fusion.30), channel_id=1, replica_groups=mesh['req'=8,'gx'=8,'gyy'=4,'gyz'=2] {'gx'}, dimensions={0}, use_global_device_ids=true | all-gather | bytes 884736 | tf_op jit(solution)/shard_map/all_gather | solution.py:73
  87.9 2.8 convolution_convert_fusion
  90.7 38.5 %reduce-scatter.5.cloned.1.call-done = bf16[192,1536]{1,0:T(8,128)(2,1)} async-done(((bf16[768,1536]{1,0:T(8,128)(2,1)}), bf16[192,1536]{1,0:T(8,128)(2,1)}) %reduce-scatter.5.cloned.1.call-update) | async-done | bytes 589840 | tf_op jit(solution)/shard_map/reduce_scatter | solution.py:32
  129.3 56.5 %reduce-scatter.7.cloned.1.call-done = bf16[96,1536]{1,0:T(8,128)(2,1)} async-done(((bf16[192,1536]{1,0:T(8,128)(2,1)}), bf16[96,1536]{1,0:T(8,128)(2,1)}) %reduce-scatter.7.cloned.1.call-update) | async-done | bytes 294928 | tf_op jit(solution)/shard_map/reduce_scatter | solution.py:34
  185.8 34.1 %all_gather.13 = bf16[192,1536]{1,0:T(8,128)(2,1)} all-gather(bf16[96,1536]{1,0:T(8,128)(2,1)} %reduce-scatter.7.cloned.1.call-done), channel_id=1, replica_groups=mesh['req'=8,'gx'=8,'gyy'=4,'gyz'=2] {'gyz'}, dimensions={0}, use_global_device_ids=true | all-gather | bytes 884736 | tf_op jit(solution)/shard_map/all_gather | solution.py:35
  229.3 26.3 %all-gather.2.cloned.1.call-done = bf16[768,1536]{1,0:T(8,128)(2,1)} async-done(((bf16[192,1536]{1,0:T(8,128)(2,1)}), bf16[768,1536]{1,0:T(8,128)(2,1)}) %all-gather.2.cloned.1.call-update) | async-done | bytes 2359312 | tf_op jit(solution)/shard_map/all_gather | solution.py:38
  255.6 4.1 reshape.162
  264.9 3.5 copy.21
  269.7 4.8 copy.20
  274.5 5.4 %fusion.19 = (bf16[384,2,512]{2,1,0:T(2,128)(2,1)}, bf16[384,2,512]{2,1,0:T(2,128)(2,1)S(1)}) fusion(bf16[2,384,1,512]{3,2,1,0:T(2,128)(2,1)S(1)} %copy.21, bf16[2,384,1,512]{3,2,1,0:T(2,128)(2,1)} %copy.20), kind=kLoop, calls=%fused_computation.38 | loop fusion | flops 3145728 | bytes 3145728 | tf_op jit(solution)/shard_map/squeeze | solution.py:103
  279.9 3.0 gather_fusion
  282.9 3.9 gather_fusion.1
  286.8 5.7 %broadcast_select_fusion.1 = (bf16[272,2,512]{2,1,0:T(2,128)(2,1)S(1)}, bf16[272,2,512]{2,1,0:T(2,128)(2,1)S(1)}) fusion(pred[272]{0:T(512)(128)(4,1)S(1)} %copy-done.14, bf16[272,2,512]{2,1,0:T(2,128)(2,1)S(1)} %gather_fusion, pred[272]{0:T(512)(128)(4,1)S(1)} %copy-done.16, bf16[2,272,2,512]{3,2,1,0:T(2,128)(2,1)} %param.12, ...), kind=kLoop, calls=%fused_computation.24 | loop fusion | flops 1114112 | bytes 3343424 | tf_op jit(solution)/shard_map/jit(_where)/select_n | solution.py:58
  292.6 3.0 slice_reduce_fusion.1
  295.5 3.0 slice_reduce_fusion.3
  303.5 27.5 %pmax.14 = f32[2,384,4]{1,2,0:T(4,128)} all-reduce(f32[2,384,4]{1,2,0:T(4,128)} %pad_maximum_fusion.3), channel_id=1, replica_groups=mesh['req'=8,'gx'=8,'gyy'=4,'gyz'=2] {'gyz'}, use_global_device_ids=true, to_apply=%region_10.12 | all-reduce | flops 3072 | bytes 24576 | tf_op jit(solution)/shard_map/pmax | solution.py:28
  331.0 16.2 %pmax.15 = f32[2,384,4]{1,2,0:T(4,128)} all-reduce(f32[2,384,4]{1,2,0:T(4,128)} %pmax.14), channel_id=1, replica_groups=mesh['req'=8,'gx'=8,'gyy'=4,'gyz'=2] {'gyy'}, use_global_device_ids=true, to_apply=%region_11.13 | all-reduce | flops 3072 | bytes 24576 | tf_op jit(solution)/shard_map/pmax | solution.py:28
  353.8 20.7 %reduce-scatter.9.cloned.1.call-done = bf16[192,516]{1,0:T(8,128)(2,1)} async-done(((bf16[768,516]{1,0:T(8,128)(2,1)}), bf16[192,516]{1,0:T(8,128)(2,1)}) %reduce-scatter.9.cloned.1.call-update) | async-done | bytes 198160 | tf_op jit(solution)/shard_map/reduce_scatter | solution.py:32
  374.6 71.8 %all-reduce.4.cloned.1.call-done = bf16[192,516]{1,0:T(8,128)(2,1)} async-done(((bf16[192,516]{1,0:T(8,128)(2,1)}), bf16[192,516]{1,0:T(8,128)(2,1)}) %all-reduce.4.cloned.1.call-update) | async-done | bytes 198160 | tf_op jit(solution)/shard_map/psum | solution.py:37
  446.5 14.6 %all_gather.15 = bf16[768,516]{1,0:T(8,128)(2,1)S(1)} all-gather(bf16[192,516]{1,0:T(8,128)(2,1)} %all-reduce.4.cloned.1.call-done), channel_id=1, replica_groups=mesh['req'=8,'gx'=8,'gyy'=4,'gyz'=2] {'gyy'}, dimensions={0}, use_global_device_ids=true | all-gather | bytes 990720 | tf_op jit(solution)/shard_map/all_gather | solution.py:38
  463.7 2.6 pad_maximum_fusion
  466.3 55.8 %reduce-scatter.11.cloned.1.call-done = bf16[96,512]{1,0:T(8,128)(2,1)} async-done(((bf16[768,512]{1,0:T(8,128)(2,1)}), bf16[96,512]{1,0:T(8,128)(2,1)}) %reduce-scatter.11.cloned.1.call-update) | async-done | bytes 98320 | tf_op jit(solution)/shard_map/reduce_scatter | solution.py:135
  (87 shorter events, 35.4 us)
Async XLA Ops:
  7.2 455.0 %copy-start = (bf16[512,512]{1,0:T(8,128)(2,1)S(1)}, bf16[512,512]{1,0:T(8,128)(2,1)}, u32[]{:S(2)}) copy-start(bf16[512,512]{1,0:T(8,128)(2,1)} %param.11) | copy-start | bytes 1572868
  7.2 122.0 %reduce-scatter.5.cloned.1.call-start = ((), (), s32[]{:S(2)}) async-start(), calls=%async_computation.4 | async-start | bytes 2949120 | tf_op jit(solution)/shard_map/reduce_scatter | solution.py:32
  90.7 129.8 %copy-start.17 = (s32[2]{0:T(128)S(1)}, s32[2]{0:T(128)}, u32[]{:S(2)}) copy-start(s32[2]{0:T(128)} %param.13) | copy-start | bytes 28
  90.7 95.1 %reduce-scatter.7.cloned.1.call-start = ((), (), s32[]{:S(2)}) async-start(), calls=%async_computation.5 | async-start | bytes 884736 | tf_op jit(solution)/shard_map/reduce_scatter | solution.py:34
  129.2 126.4 %all-gather.2.cloned.1.call-start = ((), (), s32[]{:S(2)}) async-start(), calls=%async_computation.6 | async-start | bytes 2949120 | tf_op jit(solution)/shard_map/all_gather | solution.py:38
  219.9 154.7 %reduce-scatter.9.cloned.1.call-start = ((), (), s32[]{:S(2)}) async-start(), calls=%async_computation.7 | async-start | bytes 1228800 | tf_op jit(solution)/shard_map/reduce_scatter | solution.py:32
  262.6 5.8 %copy-start.3 = (bf16[2,384,4,128]{3,2,1,0:T(4,128)(2,1)S(1)}, bf16[2,384,4,128]{3,2,1,0:T(4,128)(2,1)}, u32[]{:S(2)}) copy-start(bf16[2,384,4,128]{3,2,1,0:T(4,128)(2,1)} %get-tuple-element.19) | copy-start | bytes 2359300
  279.9 6.9 %copy-start.13 = (pred[272]{0:T(512)(128)(4,1)S(1)}, pred[272]{0:T(512)(128)(4,1)}, u32[]{:S(2)}) copy-start(pred[272]{0:T(512)(128)(4,1)} %get-tuple-element.39) | copy-start | bytes 820
  279.9 6.9 %copy-start.14 = (pred[272]{0:T(512)(128)(4,1)S(1)}, pred[272]{0:T(512)(128)(4,1)}, u32[]{:S(2)}) copy-start(pred[272]{0:T(512)(128)(4,1)} %get-tuple-element.40) | copy-start | bytes 820
  279.9 6.9 %copy-start.15 = (pred[272]{0:T(512)(128)(4,1)S(1)}, pred[272]{0:T(512)(128)(4,1)}, u32[]{:S(2)}) copy-start(pred[272]{0:T(512)(128)(4,1)} %get-tuple-element.37) | copy-start | bytes 820
  279.9 6.9 %copy-start.16 = (pred[272]{0:T(512)(128)(4,1)S(1)}, pred[272]{0:T(512)(128)(4,1)}, u32[]{:S(2)}) copy-start(pred[272]{0:T(512)(128)(4,1)} %get-tuple-element.38) | copy-start | bytes 820
  292.5 6.0 %copy-start.5 = (pred[384,272]{0,1:T(8,128)(4,1)S(1)}, pred[384,272]{0,1:T(8,128)(4,1)}, u32[]{:S(2)}) copy-start(pred[384,272]{0,1:T(8,128)(4,1)} %get-tuple-element.24) | copy-start | bytes 313348
  292.5 6.0 %copy-start.9 = (f32[384,272]{0,1:T(8,128)S(1)}, f32[384,272]{0,1:T(8,128)}, u32[]{:S(2)}) copy-start(f32[384,272]{0,1:T(8,128)} %get-tuple-element.26) | copy-start | bytes 1253380
  292.5 6.0 %copy-start.11 = (bf16[1,384,4,128]{3,2,1,0:T(4,128)(2,1)S(1)}, bf16[1,384,4,128]{3,2,1,0:T(4,128)(2,1)}, u32[]{:S(2)}) copy-start(bf16[1,384,4,128]{3,2,1,0:T(4,128)(2,1)} %get-tuple-element.18) | copy-start | bytes 1179652
  292.6 6.0 %copy-start.18 = (f32[4]{0:T(128)S(1)}, f32[4]{0:T(128)}, u32[]{:S(2)}) copy-start(f32[4]{0:T(128)} %multiply_exponential_fusion) | copy-start | bytes 52
  299.1 1.0 copy-start.8
  299.1 1.1 copy-start.10
  300.8 1.2 copy-start.1
  349.3 1.6 copy-start.2
  349.3 1.6 copy-start.4
  351.8 0.9 copy-start.7
  353.8 92.7 %all-reduce.4.cloned.1.call-start = ((), (), s32[]{:S(2)}) async-start(), calls=%async_computation.8 | async-start | bytes 491520 | tf_op jit(solution)/shard_map/psum | solution.py:37
  374.6 147.6 %reduce-scatter.11.cloned.1.call-start = ((), (), s32[]{:S(2)}) async-start(), calls=%async_computation.9 | async-start | bytes 884736 | tf_op jit(solution)/shard_map/reduce_scatter | solution.py:135
  463.7 58.5 %copy-start.6 = (bf16[96,512]{1,0:T(8,128)(2,1)S(1)}, bf16[96,512]{1,0:T(8,128)(2,1)}, u32[]{:S(2)}) copy-start(bf16[96,512]{1,0:T(8,128)(2,1)} %param.8) | copy-start | bytes 294916
  (1 other events, 0.7 us)
Sparse Core Ops, SparseCore 0:
  90.8 38.3 reduce-scatter.4
  132.0 53.6 reduce-scatter.6
  220.0 35.5 all-gather.1
  353.9 20.6 reduce-scatter.8
  377.3 69.1 all-reduce.3
  463.8 58.2 reduce-scatter.10

commit v2 on v1

--- a/solution.py
+++ b/solution.py
@@ -20,22 +20,51 @@
     return lax.axis_index("gyy") * lax.axis_size("gyz") + lax.axis_index("gyz")
 
 
+def shift(x, axis, step):
+    n = lax.axis_size(axis)
+    return lax.ppermute(x, axis, [(i, (i + step) % n) for i in range(n)])
+
+
+def swap_combine(x, axis, op):
+    wide = x.astype(jnp.float32) if op is jnp.add else x
+    total = wide
+    for step in range(1, lax.axis_size(axis)):
+        total = op(total, shift(x, axis, step).astype(wide.dtype))
+    return total
+
+
+def ring_scatter_sum(x, axis):
+    n = lax.axis_size(axis)
+    me = lax.axis_index(axis)
+    rows = x.shape[0] // n
+    total = lax.dynamic_slice_in_dim(x, me * rows, rows).astype(jnp.float32)
+    for step in range(1, n):
+        block = lax.dynamic_slice_in_dim(x, ((me + step) % n) * rows, rows)
+        total = total + shift(block, axis, step).astype(jnp.float32)
+    return total
+
+
+def ring_gather(x, axis):
+    n = lax.axis_size(axis)
+    me = lax.axis_index(axis)
+    stacked = jnp.stack([x] + [shift(x, axis, step) for step in range(1, n)])
+    order = (me - jnp.arange(n, dtype=jnp.int32)) % n
+    taken = jnp.take(stacked, order, axis=0)
+    return taken.reshape((n * x.shape[0],) + x.shape[1:])
+
+
 def gy_sum(x):
-    return lax.psum(lax.psum(x, "gyy"), "gyz")
+    return swap_combine(swap_combine(x, "gyz", jnp.add), "gyy", jnp.add)
 
 
 def gy_max(x):
-    return lax.pmax(lax.pmax(x, "gyz"), "gyy")
+    return swap_combine(swap_combine(x, "gyz", jnp.maximum), "gyy", jnp.maximum)
 
 
-def gy_sum_rows(x, twice):
-    part = lax.psum_scatter(x, "gyy", scatter_dimension=0, tiled=True)
-    if twice:
-        part = lax.psum_scatter(part, "gyz", scatter_dimension=0, tiled=True)
-        part = lax.all_gather(part, "gyz", axis=0, tiled=True)
-    else:
-        part = lax.psum(part, "gyz")
-    return lax.all_gather(part, "gyy", axis=0, tiled=True)
+def gy_sum_rows(x):
+    part = ring_scatter_sum(x, "gyy").astype(x.dtype)
+    part = swap_combine(part, "gyz", jnp.add).astype(x.dtype)
+    return ring_gather(part, "gyy")
 
 
 def partial_attend(query, keys, values, valid, distance, slopes, scale):
@@ -60,7 +89,7 @@
 
 def shards(hidden, ln_gain, w_qkv, w_out, kv_cache, cache_len):
     hidden_f = hidden.astype(jnp.float32)
-    sums = gy_sum((jnp.sum(hidden_f, axis=1), jnp.sum(hidden_f * hidden_f, axis=1)))
+    sums = gy_sum(jnp.stack([jnp.sum(hidden_f, axis=1), jnp.sum(hidden_f * hidden_f, axis=1)]))
     mean = sums[0] / D
     var = sums[1] / D - mean * mean
     normed = (
@@ -70,7 +99,7 @@
     head_size = w_qkv.shape[2] // 3
     weight_flat = w_qkv.reshape(w_qkv.shape[0], local_heads * 3 * head_size)
     partial_value = jnp.dot(
-        lax.all_gather(normed, "gx", axis=0, tiled=True),
+        ring_gather(normed, "gx"),
         weight_flat,
         preferred_element_type=jnp.float32,
     )
@@ -89,7 +118,7 @@
     totals_list = []
     accum_list = []
     caches = []
-    qkv = gy_sum_rows(partial_value.astype(jnp.bfloat16), True)
+    qkv = gy_sum_rows(partial_value.astype(jnp.bfloat16))
     qkv = qkv.reshape(requests, group, local_heads, 3 * head_size)
     fresh = jnp.stack(
         [
@@ -124,7 +153,7 @@
         ],
         axis=1,
     )
-    packed = gy_sum_rows(packed, False).astype(jnp.float32)
+    packed = gy_sum_rows(packed).astype(jnp.float32)
     joined_accums = packed[:, :width_local].reshape(accums.shape)
     joined_totals = packed[:, width_local:].reshape(totals.shape)
     attn = (
@@ -132,12 +161,9 @@
         .astype(jnp.bfloat16)
         .reshape(requests * group, width_local)
     )
-    projected = lax.psum_scatter(
-        jnp.dot(attn, w_out, preferred_element_type=jnp.float32).astype(jnp.bfloat16),
-        "gx",
-        scatter_dimension=0,
-        tiled=True,
-    ).astype(jnp.float32)
+    projected = ring_scatter_sum(
+        jnp.dot(attn, w_out, preferred_element_type=jnp.float32).astype(jnp.bfloat16), "gx"
+    )
     mixed = (projected + hidden_f).astype(jnp.bfloat16)
     return (mixed, jnp.stack(caches))
 

time: 532 us -> 393 us (0.74)
  starting transfers between devices: 0.24 us -> 213 us
  waiting for transfers between devices: 270 us -> 93 us
  blocking collectives: 169 us -> 0 us
  between operations: 14.4 us -> 1.71 us
    ppermute x0 -> x36, starting transfers between devices: none -> 213 us  [shift(): return lax.ppermute(x, axis, [(i, (i + step) % n) for i in range(n)])]
    reduce_scatter x4 -> x0, waiting for transfers between devices: 172 us -> none  [the longest x2 59.2 us: gy_sum_rows(): part = lax.psum_scatter(x, 'gyy', scatter_dimension=0, tiled=True)]
    all_gather x3 -> x0, blocking collectives: 98.1 us -> none  [the longest x1 49.5 us: shards(): lax.all_gather(normed, 'gx', axis=0, tiled=True)]
    ppermute x0 -> x36, waiting for transfers between devices: none -> 93 us  [shift(): return lax.ppermute(x, axis, [(i, (i + step) % n) for i in range(n)])]
    psum x1 -> x0, waiting for transfers between devices: 71.8 us -> none  [gy_sum_rows(): part = lax.psum(part, 'gyz')]
    pmax x2 -> x0, blocking collectives: 43.7 us -> none  [gy_max(): return lax.pmax(lax.pmax(x, 'gyz'), 'gyy')]
    psum x2 -> x0, blocking collectives: 27.4 us -> none  [gy_sum(): return lax.psum(lax.psum(x, 'gyy'), 'gyz')]
    all_gather x1 -> x0, waiting for transfers between devices: 26.3 us -> none  [gy_sum_rows(): return lax.all_gather(part, 'gyy', axis=0, tiled=True)]
  transfers between devices with their start and end apart: 6 -> 36, of which waited for: 6 -> 17; matrix products, arithmetic and copies ran while one was open for 2% -> 4% of each run, Pallas kernels for 0% -> 0%
where the time goes in v2:
time: 393 us; the launch traced here: 388 us
  starting transfers between devices  213 us (54%)
  waiting for transfers between devices  93 us (24%)
  local copies, waits for them, and re-layouts  41.8 us (11%)
  other arithmetic  30.4 us (8%)
  matrix products  7.59 us (2%)
    ppermute x36, starting transfers between devices, shift(): return lax.ppermute(x, axis, [(i, (i + step) % n) for i in range(n)])  213 us
    ppermute x36, waiting for transfers between devices, shift(): return lax.ppermute(x, axis, [(i, (i + step) % n) for i in range(n)])  93 us
    gather x4, local copies, waits for them, and re-layouts, ring_gather(): taken = jnp.take(stacked, order, axis=0)  8.47 us
    another operation x2, local copies, waits for them, and re-layouts, shards(): jnp.stack([qkv[:, :, :, head_size:2 * head_size].reshape(requests, group,...  8.29 us
  transfers between devices with their start and end apart: 36, of which 17 were waited for; matrix products, arithmetic and copies ran while one was open for 4% of the time, Pallas kernels for 0%

profile of v2, /device:TPU:6, one launch (start us, length us, event | category | flops | bytes accessed | tf_op | source)
XLA Modules:
  0.0 387.9 jit_solution(6840681588322417602)
XLA Ops:
  1.8 15.7 %collective-permute-start = (f32[2,96]{1,0:T(2,128)S(1)}, f32[2,96]{1,0:T(2,128)S(1)}, u32[]{:S(2)}, u32[]{:S(2)}) collective-permute-start(f32[2,96]{1,0:T(2,128)S(1)} %pad_maximum_fusion.5), channel_id=1, source_target_pairs={{0,1},{1,0},{2,3},{3,2},{4,5},{5,4},{6,7},{7,6},{8,9},{9,8},{10,11... | collective-permute-start | bytes 2312 | tf_op jit(solution)/shard_map/ppermute | solution.py:25
  22.5 4.8 %collective-permute-start.2 = (f32[2,96]{1,0:T(2,128)S(1)}, f32[2,96]{1,0:T(2,128)S(1)}, u32[]{:S(2)}, u32[]{:S(2)}) collective-permute-start(f32[2,96]{1,0:T(2,128)S(1)} %fusion.51), channel_id=1, source_target_pairs={{0,4},{2,6},{4,0},{6,2},{1,5},{3,7},{5,1},{7,3},{8,12},{10,14},{12... | collective-permute-start | bytes 2312 | tf_op jit(solution)/shard_map/ppermute | solution.py:25
  40.0 7.4 %collective-permute-start.6 = (bf16[96,512]{1,0:T(8,128)(2,1)S(1)}, bf16[96,512]{1,0:T(8,128)(2,1)S(1)}, u32[]{:S(2)}, u32[]{:S(2)}) collective-permute-start(bf16[96,512]{1,0:T(8,128)(2,1)S(1)} %get-tuple-element.14), channel_id=1, source_target_pairs={{0,24},{8,32},{16,40},{24,48},{32,56},{40,0},{48,8},{56,16},{1,25}... | collective-permute-start | bytes 294920 | tf_op jit(solution)/shard_map/ppermute | solution.py:25
  51.1 7.4 %collective-permute-start.8 = (bf16[96,512]{1,0:T(8,128)(2,1)S(1)}, bf16[96,512]{1,0:T(8,128)(2,1)S(1)}, u32[]{:S(2)}, u32[]{:S(2)}) collective-permute-start(bf16[96,512]{1,0:T(8,128)(2,1)S(1)} %get-tuple-element.14), channel_id=1, source_target_pairs={{0,40},{8,48},{16,56},{24,0},{32,8},{40,16},{48,24},{56,32},{1,41}... | collective-permute-start | bytes 294920 | tf_op jit(solution)/shard_map/ppermute | solution.py:25
  87.7 17.5 %collective-permute-done.11 = bf16[192,1536]{1,0:T(8,128)(2,1)S(1)} collective-permute-done((bf16[192,1536]{1,0:T(8,128)(2,1)}, bf16[192,1536]{1,0:T(8,128)(2,1)S(1)}, u32[]{:S(2)}, u32[]{:S(2)}) %collective-permute-start.11) | collective-permute-done | bytes 589856 | tf_op jit(solution)/shard_map/ppermute | solution.py:25
  109.6 8.5 %collective-permute-start.14 = (bf16[192,1536]{1,0:T(8,128)(2,1)S(1)}, bf16[192,1536]{1,0:T(8,128)(2,1)S(1)}, u32[]{:S(2)}, u32[]{:S(2)}) collective-permute-start(bf16[192,1536]{1,0:T(8,128)(2,1)S(1)} %add_convert_fusion.1), channel_id=1, source_target_pairs={{0,1},{1,0},{2,3},{3,2},{4,5},{5,4},{6,7},{7,6},{8,9},{9,8},{10,11... | collective-permute-start | bytes 1769480 | tf_op jit(solution)/shard_map/ppermute | solution.py:25
  120.6 17.8 %collective-permute-done.14 = bf16[192,1536]{1,0:T(8,128)(2,1)S(1)} collective-permute-done((bf16[192,1536]{1,0:T(8,128)(2,1)S(1)}, bf16[192,1536]{1,0:T(8,128)(2,1)S(1)}, u32[]{:S(2)}, u32[]{:S(2)}) %collective-permute-start.14) | collective-permute-done | bytes 589856 | tf_op jit(solution)/shard_map/ppermute | solution.py:25
  138.6 8.4 %collective-permute-start.15 = (bf16[192,1536]{1,0:T(8,128)(2,1)S(1)}, bf16[192,1536]{1,0:T(8,128)(2,1)S(1)}, u32[]{:S(2)}, u32[]{:S(2)}) collective-permute-start(bf16[192,1536]{1,0:T(8,128)(2,1)S(1)} %add_convert_fusion), channel_id=1, source_target_pairs={{0,2},{2,4},{4,6},{6,0},{1,3},{3,5},{5,7},{7,1},{8,10},{10,12},{12... | collective-permute-start | bytes 1769480 | tf_op jit(solution)/shard_map/ppermute | solution.py:25
  148.9 4.8 %collective-permute-start.17 = (bf16[192,1536]{1,0:T(8,128)(2,1)S(1)}, bf16[192,1536]{1,0:T(8,128)(2,1)S(1)}, u32[]{:S(2)}, u32[]{:S(2)}) collective-permute-start(bf16[192,1536]{1,0:T(8,128)(2,1)S(1)} %add_convert_fusion), channel_id=1, source_target_pairs={{0,6},{2,0},{4,2},{6,4},{1,7},{3,1},{5,3},{7,5},{8,14},{10,8},{12,... | collective-permute-start | bytes 1769480 | tf_op jit(solution)/shard_map/ppermute | solution.py:25
  155.8 4.9 %collective-permute-done.15 = bf16[192,1536]{1,0:T(8,128)(2,1)S(1)} collective-permute-done((bf16[192,1536]{1,0:T(8,128)(2,1)S(1)}, bf16[192,1536]{1,0:T(8,128)(2,1)S(1)}, u32[]{:S(2)}, u32[]{:S(2)}) %collective-permute-start.15) | collective-permute-done | bytes 589856 | tf_op jit(solution)/shard_map/ppermute | solution.py:25
  160.7 10.7 %collective-permute-done.16 = bf16[192,1536]{1,0:T(8,128)(2,1)S(1)} collective-permute-done((bf16[192,1536]{1,0:T(8,128)(2,1)S(1)}, bf16[192,1536]{1,0:T(8,128)(2,1)S(1)}, u32[]{:S(2)}, u32[]{:S(2)}) %collective-permute-start.16) | collective-permute-done | bytes 589856 | tf_op jit(solution)/shard_map/ppermute | solution.py:25
  191.1 4.8 %copy.29 = bf16[2,384,1,512]{3,2,1,0:T(2,128)(2,1)} copy(bf16[2,384,1,512]{1,3,0,2:T(8,128)(2,1)} %bitcast.146) | data formatting | bytes 1572864 | tf_op jit(solution)/shard_map/stack;reshape | solution.py:123
  195.8 5.4 %fusion.20 = (bf16[384,2,512]{2,1,0:T(2,128)(2,1)S(1)}, bf16[384,2,512]{2,1,0:T(2,128)(2,1)}) fusion(bf16[2,384,1,512]{3,2,1,0:T(2,128)(2,1)} %copy.29, bf16[2,384,1,512]{3,2,1,0:T(2,128)(2,1)S(1)} %copy.28), kind=kLoop, calls=%fused_computation.55 | loop fusion | flops 3145728 | bytes 3145728 | tf_op jit(solution)/shard_map/squeeze | solution.py:132
  208.2 5.7 %broadcast_select_fusion.1 = (bf16[272,2,512]{2,1,0:T(2,128)(2,1)S(1)}, bf16[272,2,512]{2,1,0:T(2,128)(2,1)S(1)}) fusion(pred[272]{0:T(512)(128)(4,1)S(1)} %get-tuple-element.49, bf16[272,2,512]{2,1,0:T(2,128)(2,1)} %gather_fusion.3, pred[272]{0:T(512)(128)(4,1)S(1)} %get-tuple-element.47, bf16[2,272,2,512]{3,2,1,0:T(2,128)(2,1)} %param.12, ...), kind=kLoop, calls=%fused_computation.35 | loop fusion | flops 1114112 | bytes 3343424 | tf_op jit(solution)/shard_map/jit(_where)/select_n | solution.py:87
  221.8 8.5 %collective-permute-start.18 = (f32[2,384,4]{1,2,0:T(4,128)S(1)}, f32[2,384,4]{1,2,0:T(4,128)S(1)}, u32[]{:S(2)}, u32[]{:S(2)}) collective-permute-start(f32[2,384,4]{1,2,0:T(4,128)S(1)} %pad_maximum_fusion.4), channel_id=1, source_target_pairs={{0,1},{1,0},{2,3},{3,2},{4,5},{5,4},{6,7},{7,6},{8,9},{9,8},{10,11... | collective-permute-start | bytes 36872 | tf_op jit(solution)/shard_map/ppermute | solution.py:25
  236.1 5.1 %collective-permute-start.19 = (f32[2,384,4]{1,2,0:T(4,128)S(1)}, f32[2,384,4]{1,2,0:T(4,128)S(1)}, u32[]{:S(2)}, u32[]{:S(2)}) collective-permute-start(f32[2,384,4]{1,2,0:T(4,128)S(1)} %fusion.52), channel_id=1, source_target_pairs={{0,2},{2,4},{4,6},{6,0},{1,3},{3,5},{5,7},{7,1},{8,10},{10,12},{12... | collective-permute-start | bytes 36872 | tf_op jit(solution)/shard_map/ppermute | solution.py:25
  253.3 6.4 %collective-permute-start.23 = (bf16[192,516]{1,0:T(8,128)(2,1)S(1)}, bf16[192,516]{1,0:T(8,128)(2,1)S(1)}, u32[]{:S(2)}, u32[]{:S(2)}) collective-permute-start(bf16[192,516]{1,0:T(8,128)(2,1)S(1)} %get-tuple-element.25), channel_id=1, source_target_pairs={{0,4},{2,6},{4,0},{6,2},{1,5},{3,7},{5,1},{7,3},{8,12},{10,14},{12... | collective-permute-start | bytes 594440 | tf_op jit(solution)/shard_map/ppermute | solution.py:25
  268.5 6.9 %collective-permute-start.25 = (bf16[192,516]{1,0:T(8,128)(2,1)S(1)}, bf16[192,516]{1,0:T(8,128)(2,1)S(1)}, u32[]{:S(2)}, u32[]{:S(2)}) collective-permute-start(bf16[192,516]{1,0:T(8,128)(2,1)S(1)} %add_convert_fusion.3), channel_id=1, source_target_pairs={{0,1},{1,0},{2,3},{3,2},{4,5},{5,4},{6,7},{7,6},{8,9},{9,8},{10,11... | collective-permute-start | bytes 594440 | tf_op jit(solution)/shard_map/ppermute | solution.py:25
  275.4 9.9 %collective-permute-done.25 = bf16[192,516]{1,0:T(8,128)(2,1)S(1)} collective-permute-done((bf16[192,516]{1,0:T(8,128)(2,1)S(1)}, bf16[192,516]{1,0:T(8,128)(2,1)S(1)}, u32[]{:S(2)}, u32[]{:S(2)}) %collective-permute-start.25) | collective-permute-done | bytes 198176 | tf_op jit(solution)/shard_map/ppermute | solution.py:25
  287.7 4.8 %collective-permute-start.27 = (bf16[192,516]{1,0:T(8,128)(2,1)S(1)}, bf16[192,516]{1,0:T(8,128)(2,1)S(1)}, u32[]{:S(2)}, u32[]{:S(2)}) collective-permute-start(bf16[192,516]{1,0:T(8,128)(2,1)S(1)} %add_convert_fusion.2), channel_id=1, source_target_pairs={{0,4},{2,6},{4,0},{6,2},{1,5},{3,7},{5,1},{7,3},{8,12},{10,14},{12... | collective-permute-start | bytes 594440 | tf_op jit(solution)/shard_map/ppermute | solution.py:25
  307.1 35.3 %collective-permute-start.29 = (bf16[96,512]{1,0:T(8,128)(2,1)S(1)}, bf16[96,512]{1,0:T(8,128)(2,1)S(1)}, u32[]{:S(2)}, u32[]{:S(2)}) collective-permute-start(bf16[96,512]{1,0:T(8,128)(2,1)S(1)} %get-tuple-element.27), channel_id=1, source_target_pairs={{0,8},{8,16},{16,24},{24,32},{32,40},{40,48},{48,56},{56,0},{1,9},... | collective-permute-start | bytes 294920 | tf_op jit(solution)/shard_map/ppermute | solution.py:25
  344.6 6.6 %collective-permute-start.31 = (bf16[96,512]{1,0:T(8,128)(2,1)S(1)}, bf16[96,512]{1,0:T(8,128)(2,1)S(1)}, u32[]{:S(2)}, u32[]{:S(2)}) collective-permute-start(bf16[96,512]{1,0:T(8,128)(2,1)S(1)} %get-tuple-element.32), channel_id=1, source_target_pairs={{0,24},{8,32},{16,40},{24,48},{32,56},{40,0},{48,8},{56,16},{1,25}... | collective-permute-start | bytes 294920 | tf_op jit(solution)/shard_map/ppermute | solution.py:25
  351.2 15.2 %collective-permute-start.32 = (bf16[96,512]{1,0:T(8,128)(2,1)S(1)}, bf16[96,512]{1,0:T(8,128)(2,1)S(1)}, u32[]{:S(2)}, u32[]{:S(2)}) collective-permute-start(bf16[96,512]{1,0:T(8,128)(2,1)S(1)} %get-tuple-element.31), channel_id=1, source_target_pairs={{0,32},{8,40},{16,48},{24,56},{32,0},{40,8},{48,16},{56,24},{1,33}... | collective-permute-start | bytes 294920 | tf_op jit(solution)/shard_map/ppermute | solution.py:25
  366.5 7.8 %collective-permute-start.33 = (bf16[96,512]{1,0:T(8,128)(2,1)S(1)}, bf16[96,512]{1,0:T(8,128)(2,1)S(1)}, u32[]{:S(2)}, u32[]{:S(2)}) collective-permute-start(bf16[96,512]{1,0:T(8,128)(2,1)S(1)} %get-tuple-element.30), channel_id=1, source_target_pairs={{0,40},{8,48},{16,56},{24,0},{32,8},{40,16},{48,24},{56,32},{1,41}... | collective-permute-start | bytes 294920 | tf_op jit(solution)/shard_map/ppermute | solution.py:25
  (161 shorter events, 155.8 us)
Async XLA Ops:
  1.8 17.3 %collective-permute-start = (f32[2,96]{1,0:T(2,128)S(1)}, f32[2,96]{1,0:T(2,128)S(1)}, u32[]{:S(2)}, u32[]{:S(2)}) collective-permute-start(f32[2,96]{1,0:T(2,128)S(1)} %pad_maximum_fusion.5), channel_id=1, source_target_pairs={{0,1},{1,0},{2,3},{3,2},{4,5},{5,4},{6,7},{7,6},{8,9},{9,8},{10,11... | collective-permute-start | bytes 2312 | tf_op jit(solution)/shard_map/ppermute | solution.py:25
  19.0 14.4 %collective-permute-start.1 = (f32[2,96]{1,0:T(2,128)S(1)}, f32[2,96]{1,0:T(2,128)S(1)}, u32[]{:S(2)}, u32[]{:S(2)}) collective-permute-start(f32[2,96]{1,0:T(2,128)S(1)} %fusion.51), channel_id=1, source_target_pairs={{0,2},{2,4},{4,6},{6,0},{1,3},{3,5},{5,7},{7,1},{8,10},{10,12},{12... | collective-permute-start | bytes 2312 | tf_op jit(solution)/shard_map/ppermute | solution.py:25
  33.7 24.8 %collective-permute-start.4 = (bf16[96,512]{1,0:T(8,128)(2,1)S(1)}, bf16[96,512]{1,0:T(8,128)(2,1)S(1)}, u32[]{:S(2)}, u32[]{:S(2)}) collective-permute-start(bf16[96,512]{1,0:T(8,128)(2,1)S(1)} %get-tuple-element.14), channel_id=1, source_target_pairs={{0,8},{8,16},{16,24},{24,32},{32,40},{40,48},{48,56},{56,0},{1,9},... | collective-permute-start | bytes 294920 | tf_op jit(solution)/shard_map/ppermute | solution.py:25
  36.6 26.5 %collective-permute-start.5 = (bf16[96,512]{1,0:T(8,128)(2,1)S(1)}, bf16[96,512]{1,0:T(8,128)(2,1)S(1)}, u32[]{:S(2)}, u32[]{:S(2)}) collective-permute-start(bf16[96,512]{1,0:T(8,128)(2,1)S(1)} %get-tuple-element.14), channel_id=1, source_target_pairs={{0,16},{8,24},{16,32},{24,40},{32,48},{40,56},{48,0},{56,8},{1,17}... | collective-permute-start | bytes 294920 | tf_op jit(solution)/shard_map/ppermute | solution.py:25
  40.0 26.0 %collective-permute-start.6 = (bf16[96,512]{1,0:T(8,128)(2,1)S(1)}, bf16[96,512]{1,0:T(8,128)(2,1)S(1)}, u32[]{:S(2)}, u32[]{:S(2)}) collective-permute-start(bf16[96,512]{1,0:T(8,128)(2,1)S(1)} %get-tuple-element.14), channel_id=1, source_target_pairs={{0,24},{8,32},{16,40},{24,48},{32,56},{40,0},{48,8},{56,16},{1,25}... | collective-permute-start | bytes 294920 | tf_op jit(solution)/shard_map/ppermute | solution.py:25
  47.4 18.7 %collective-permute-start.7 = (bf16[96,512]{1,0:T(8,128)(2,1)S(1)}, bf16[96,512]{1,0:T(8,128)(2,1)S(1)}, u32[]{:S(2)}, u32[]{:S(2)}) collective-permute-start(bf16[96,512]{1,0:T(8,128)(2,1)S(1)} %get-tuple-element.14), channel_id=1, source_target_pairs={{0,32},{8,40},{16,48},{24,56},{32,0},{40,8},{48,16},{56,24},{1,33}... | collective-permute-start | bytes 294920 | tf_op jit(solution)/shard_map/ppermute | solution.py:25
  51.1 15.0 %collective-permute-start.8 = (bf16[96,512]{1,0:T(8,128)(2,1)S(1)}, bf16[96,512]{1,0:T(8,128)(2,1)S(1)}, u32[]{:S(2)}, u32[]{:S(2)}) collective-permute-start(bf16[96,512]{1,0:T(8,128)(2,1)S(1)} %get-tuple-element.14), channel_id=1, source_target_pairs={{0,40},{8,48},{16,56},{24,0},{32,8},{40,16},{48,24},{56,32},{1,41}... | collective-permute-start | bytes 294920 | tf_op jit(solution)/shard_map/ppermute | solution.py:25
  75.6 29.7 %collective-permute-start.11 = (bf16[192,1536]{1,0:T(8,128)(2,1)}, bf16[192,1536]{1,0:T(8,128)(2,1)S(1)}, u32[]{:S(2)}, u32[]{:S(2)}) collective-permute-start(bf16[192,1536]{1,0:T(8,128)(2,1)} %get-tuple-element.19), channel_id=1, source_target_pairs={{0,2},{2,4},{4,6},{6,0},{1,3},{3,5},{5,7},{7,1},{8,10},{10,12},{12... | collective-permute-start | bytes 1769480 | tf_op jit(solution)/shard_map/ppermute | solution.py:25
  78.2 27.1 %collective-permute-start.12 = (bf16[192,1536]{1,0:T(8,128)(2,1)}, bf16[192,1536]{1,0:T(8,128)(2,1)}, u32[]{:S(2)}, u32[]{:S(2)}) collective-permute-start(bf16[192,1536]{1,0:T(8,128)(2,1)} %get-tuple-element.21), channel_id=1, source_target_pairs={{0,4},{2,6},{4,0},{6,2},{1,5},{3,7},{5,1},{7,3},{8,12},{10,14},{12... | collective-permute-start | bytes 1769480 | tf_op jit(solution)/shard_map/ppermute | solution.py:25
  82.3 25.6 %collective-permute-start.13 = (bf16[192,1536]{1,0:T(8,128)(2,1)}, bf16[192,1536]{1,0:T(8,128)(2,1)}, u32[]{:S(2)}, u32[]{:S(2)}) collective-permute-start(bf16[192,1536]{1,0:T(8,128)(2,1)} %get-tuple-element.20), channel_id=1, source_target_pairs={{0,6},{2,0},{4,2},{6,4},{1,7},{3,1},{5,3},{7,5},{8,14},{10,8},{12,... | collective-permute-start | bytes 1769480 | tf_op jit(solution)/shard_map/ppermute | solution.py:25
  109.6 28.8 %collective-permute-start.14 = (bf16[192,1536]{1,0:T(8,128)(2,1)S(1)}, bf16[192,1536]{1,0:T(8,128)(2,1)S(1)}, u32[]{:S(2)}, u32[]{:S(2)}) collective-permute-start(bf16[192,1536]{1,0:T(8,128)(2,1)S(1)} %add_convert_fusion.1), channel_id=1, source_target_pairs={{0,1},{1,0},{2,3},{3,2},{4,5},{5,4},{6,7},{7,6},{8,9},{9,8},{10,11... | collective-permute-start | bytes 1769480 | tf_op jit(solution)/shard_map/ppermute | solution.py:25
  138.6 22.1 %collective-permute-start.15 = (bf16[192,1536]{1,0:T(8,128)(2,1)S(1)}, bf16[192,1536]{1,0:T(8,128)(2,1)S(1)}, u32[]{:S(2)}, u32[]{:S(2)}) collective-permute-start(bf16[192,1536]{1,0:T(8,128)(2,1)S(1)} %add_convert_fusion), channel_id=1, source_target_pairs={{0,2},{2,4},{4,6},{6,0},{1,3},{3,5},{5,7},{7,1},{8,10},{10,12},{12... | collective-permute-start | bytes 1769480 | tf_op jit(solution)/shard_map/ppermute | solution.py:25
  147.0 24.4 %collective-permute-start.16 = (bf16[192,1536]{1,0:T(8,128)(2,1)S(1)}, bf16[192,1536]{1,0:T(8,128)(2,1)S(1)}, u32[]{:S(2)}, u32[]{:S(2)}) collective-permute-start(bf16[192,1536]{1,0:T(8,128)(2,1)S(1)} %add_convert_fusion), channel_id=1, source_target_pairs={{0,4},{2,6},{4,0},{6,2},{1,5},{3,7},{5,1},{7,3},{8,12},{10,14},{12... | collective-permute-start | bytes 1769480 | tf_op jit(solution)/shard_map/ppermute | solution.py:25
  148.9 25.2 %collective-permute-start.17 = (bf16[192,1536]{1,0:T(8,128)(2,1)S(1)}, bf16[192,1536]{1,0:T(8,128)(2,1)S(1)}, u32[]{:S(2)}, u32[]{:S(2)}) collective-permute-start(bf16[192,1536]{1,0:T(8,128)(2,1)S(1)} %add_convert_fusion), channel_id=1, source_target_pairs={{0,6},{2,0},{4,2},{6,4},{1,7},{3,1},{5,3},{7,5},{8,14},{10,8},{12,... | collective-permute-start | bytes 1769480 | tf_op jit(solution)/shard_map/ppermute | solution.py:25
  221.8 14.3 %collective-permute-start.18 = (f32[2,384,4]{1,2,0:T(4,128)S(1)}, f32[2,384,4]{1,2,0:T(4,128)S(1)}, u32[]{:S(2)}, u32[]{:S(2)}) collective-permute-start(f32[2,384,4]{1,2,0:T(4,128)S(1)} %pad_maximum_fusion.4), channel_id=1, source_target_pairs={{0,1},{1,0},{2,3},{3,2},{4,5},{5,4},{6,7},{7,6},{8,9},{9,8},{10,11... | collective-permute-start | bytes 36872 | tf_op jit(solution)/shard_map/ppermute | solution.py:25
  236.1 12.5 %collective-permute-start.19 = (f32[2,384,4]{1,2,0:T(4,128)S(1)}, f32[2,384,4]{1,2,0:T(4,128)S(1)}, u32[]{:S(2)}, u32[]{:S(2)}) collective-permute-start(f32[2,384,4]{1,2,0:T(4,128)S(1)} %fusion.52), channel_id=1, source_target_pairs={{0,2},{2,4},{4,6},{6,0},{1,3},{3,5},{5,7},{7,1},{8,10},{10,12},{12... | collective-permute-start | bytes 36872 | tf_op jit(solution)/shard_map/ppermute | solution.py:25
  268.5 16.8 %collective-permute-start.25 = (bf16[192,516]{1,0:T(8,128)(2,1)S(1)}, bf16[192,516]{1,0:T(8,128)(2,1)S(1)}, u32[]{:S(2)}, u32[]{:S(2)}) collective-permute-start(bf16[192,516]{1,0:T(8,128)(2,1)S(1)} %add_convert_fusion.3), channel_id=1, source_target_pairs={{0,1},{1,0},{2,3},{3,2},{4,5},{5,4},{6,7},{7,6},{8,9},{9,8},{10,11... | collective-permute-start | bytes 594440 | tf_op jit(solution)/shard_map/ppermute | solution.py:25
  285.3 12.4 %collective-permute-start.26 = (bf16[192,516]{1,0:T(8,128)(2,1)S(1)}, bf16[192,516]{1,0:T(8,128)(2,1)S(1)}, u32[]{:S(2)}, u32[]{:S(2)}) collective-permute-start(bf16[192,516]{1,0:T(8,128)(2,1)S(1)} %add_convert_fusion.2), channel_id=1, source_target_pairs={{0,2},{2,4},{4,6},{6,0},{1,3},{3,5},{5,7},{7,1},{8,10},{10,12},{12... | collective-permute-start | bytes 594440 | tf_op jit(solution)/shard_map/ppermute | solution.py:25
  307.1 67.2 %collective-permute-start.29 = (bf16[96,512]{1,0:T(8,128)(2,1)S(1)}, bf16[96,512]{1,0:T(8,128)(2,1)S(1)}, u32[]{:S(2)}, u32[]{:S(2)}) collective-permute-start(bf16[96,512]{1,0:T(8,128)(2,1)S(1)} %get-tuple-element.27), channel_id=1, source_target_pairs={{0,8},{8,16},{16,24},{24,32},{32,40},{40,48},{48,56},{56,0},{1,9},... | collective-permute-start | bytes 294920 | tf_op jit(solution)/shard_map/ppermute | solution.py:25
  342.5 33.8 %collective-permute-start.30 = (bf16[96,512]{1,0:T(8,128)(2,1)S(1)}, bf16[96,512]{1,0:T(8,128)(2,1)S(1)}, u32[]{:S(2)}, u32[]{:S(2)}) collective-permute-start(bf16[96,512]{1,0:T(8,128)(2,1)S(1)} %get-tuple-element.33), channel_id=1, source_target_pairs={{0,16},{8,24},{16,32},{24,40},{32,48},{40,56},{48,0},{56,8},{1,17}... | collective-permute-start | bytes 294920 | tf_op jit(solution)/shard_map/ppermute | solution.py:25
  344.6 38.6 %collective-permute-start.31 = (bf16[96,512]{1,0:T(8,128)(2,1)S(1)}, bf16[96,512]{1,0:T(8,128)(2,1)S(1)}, u32[]{:S(2)}, u32[]{:S(2)}) collective-permute-start(bf16[96,512]{1,0:T(8,128)(2,1)S(1)} %get-tuple-element.32), channel_id=1, source_target_pairs={{0,24},{8,32},{16,40},{24,48},{32,56},{40,0},{48,8},{56,16},{1,25}... | collective-permute-start | bytes 294920 | tf_op jit(solution)/shard_map/ppermute | solution.py:25
  351.2 31.9 %collective-permute-start.32 = (bf16[96,512]{1,0:T(8,128)(2,1)S(1)}, bf16[96,512]{1,0:T(8,128)(2,1)S(1)}, u32[]{:S(2)}, u32[]{:S(2)}) collective-permute-start(bf16[96,512]{1,0:T(8,128)(2,1)S(1)} %get-tuple-element.31), channel_id=1, source_target_pairs={{0,32},{8,40},{16,48},{24,56},{32,0},{40,8},{48,16},{56,24},{1,33}... | collective-permute-start | bytes 294920 | tf_op jit(solution)/shard_map/ppermute | solution.py:25
  366.5 16.7 %collective-permute-start.33 = (bf16[96,512]{1,0:T(8,128)(2,1)S(1)}, bf16[96,512]{1,0:T(8,128)(2,1)S(1)}, u32[]{:S(2)}, u32[]{:S(2)}) collective-permute-start(bf16[96,512]{1,0:T(8,128)(2,1)S(1)} %get-tuple-element.30), channel_id=1, source_target_pairs={{0,40},{8,48},{16,56},{24,0},{32,8},{40,16},{48,24},{56,32},{1,41}... | collective-permute-start | bytes 294920 | tf_op jit(solution)/shard_map/ppermute | solution.py:25
  374.3 12.8 %collective-permute-start.34 = (bf16[96,512]{1,0:T(8,128)(2,1)S(1)}, bf16[96,512]{1,0:T(8,128)(2,1)S(1)}, u32[]{:S(2)}, u32[]{:S(2)}) collective-permute-start(bf16[96,512]{1,0:T(8,128)(2,1)S(1)} %get-tuple-element.29), channel_id=1, source_target_pairs={{0,48},{8,56},{16,0},{24,8},{32,16},{40,24},{48,32},{56,40},{1,49}... | collective-permute-start | bytes 294920 | tf_op jit(solution)/shard_map/ppermute | solution.py:25
  (27 other events, 606.9 us)

commit v3 on v2

--- a/solution.py
+++ b/solution.py
@@ -53,6 +53,36 @@
     return taken.reshape((n * x.shape[0],) + x.shape[1:])
 
 
+def merge(parts, heads):
+    top = parts[0][1]
+    for _, high in parts[1:]:
+        top = jnp.maximum(top, high)
+    total = 0.0
+    for block, high in parts:
+        factor = jnp.exp(high - top)
+        wide = jnp.repeat(factor, block.shape[1] // heads - 1, axis=1)
+        total = total + block.astype(jnp.float32) * jnp.concatenate([wide, factor], axis=1)
+    return total, top
+
+
+def attend_combine(packed, tops, heads):
+    n = lax.axis_size("gyy")
+    me = lax.axis_index("gyy")
+    rows = packed.shape[0] // n
+    parts = []
+    for step in range(n):
+        block = lax.dynamic_slice_in_dim(packed, ((me + step) % n) * rows, rows)
+        high = lax.dynamic_slice_in_dim(tops, ((me + step) % n) * rows, rows)
+        parts.append((block, high) if step == 0 else shift((block, high), "gyy", step))
+    total, top = merge(parts, heads)
+    own = (total.astype(packed.dtype), top)
+    total, _ = merge([own, shift(own, "gyz", 1)], heads)
+    width = total.shape[1] - heads
+    sums = total[:, :width].reshape(rows, heads, width // heads)
+    attn = (sums / total[:, width:, None]).astype(packed.dtype).reshape(rows, width)
+    return ring_gather(attn, "gyy")
+
+
 def gy_sum(x):
     return swap_combine(swap_combine(x, "gyz", jnp.add), "gyy", jnp.add)
 
@@ -89,17 +119,19 @@
 
 def shards(hidden, ln_gain, w_qkv, w_out, kv_cache, cache_len):
     hidden_f = hidden.astype(jnp.float32)
-    sums = gy_sum(jnp.stack([jnp.sum(hidden_f, axis=1), jnp.sum(hidden_f * hidden_f, axis=1)]))
-    mean = sums[0] / D
-    var = sums[1] / D - mean * mean
+    gathered = ring_gather(hidden, "gx").astype(jnp.float32)
+    sums = gy_sum(jnp.stack([jnp.sum(hidden_f, axis=1), jnp.sum(hidden_f * hidden_f, axis=1)], axis=1))
+    sums = ring_gather(sums, "gx")
+    mean = sums[:, 0] / D
+    var = sums[:, 1] / D - mean * mean
     normed = (
-        (hidden_f - mean[:, None]) * lax.rsqrt(var + norm_eps)[:, None] * ln_gain[None, :]
+        (gathered - mean[:, None]) * lax.rsqrt(var + norm_eps)[:, None] * ln_gain[None, :]
     ).astype(jnp.bfloat16)
     local_heads = w_qkv.shape[1]
     head_size = w_qkv.shape[2] // 3
     weight_flat = w_qkv.reshape(w_qkv.shape[0], local_heads * 3 * head_size)
     partial_value = jnp.dot(
-        ring_gather(normed, "gx"),
+        normed,
         weight_flat,
         preferred_element_type=jnp.float32,
     )
@@ -143,24 +175,15 @@
     tops = jnp.stack(tops_list)
     totals = jnp.stack(totals_list)
     accums = jnp.stack(accum_list)
-    overall = gy_max(tops)
-    factor = jnp.exp(tops - overall)
     rows = requests * group
     packed = jnp.concatenate(
         [
-            (accums * factor[..., None]).astype(jnp.bfloat16).reshape(rows, width_local),
-            (totals * factor).astype(jnp.bfloat16).reshape(rows, local_heads),
+            accums.astype(jnp.bfloat16).reshape(rows, width_local),
+            totals.astype(jnp.bfloat16).reshape(rows, local_heads),
         ],
         axis=1,
     )
-    packed = gy_sum_rows(packed).astype(jnp.float32)
-    joined_accums = packed[:, :width_local].reshape(accums.shape)
-    joined_totals = packed[:, width_local:].reshape(totals.shape)
-    attn = (
-        (joined_accums / joined_totals[..., None])
-        .astype(jnp.bfloat16)
-        .reshape(requests * group, width_local)
-    )
+    attn = attend_combine(packed, tops.reshape(rows, local_heads), local_heads)
     projected = ring_scatter_sum(
         jnp.dot(attn, w_out, preferred_element_type=jnp.float32).astype(jnp.bfloat16), "gx"
     )

time: 393 us -> 418 us (1.064)
  waiting for transfers between devices: 93 us -> 107 us
  starting transfers between devices: 213 us -> 223 us
    ppermute x36 -> x43, waiting for transfers between devices: 93 us -> 107 us  [shift(): return lax.ppermute(x, axis, [(i, (i + step) % n) for i in range(n)])]
    ppermute x36 -> x43, starting transfers between devices: 213 us -> 223 us  [shift(): return lax.ppermute(x, axis, [(i, (i + step) % n) for i in range(n)])]
    unnamed x38 -> x53, local copies, waits for them, and re-layouts: 6.81 us -> 10.1 us
    gather x4 -> x7, local copies, waits for them, and re-layouts: 8.47 us -> 8.12 us  [ring_gather(): taken = jnp.take(stacked, order, axis=0)]
  transfers between devices with their start and end apart: 36 -> 43, of which waited for: 17 -> 24; matrix products, arithmetic and copies ran while one was open for 4% -> 5% of each run, Pallas kernels for 0% -> 0%
where the time goes in v3:
time: 418 us; the launch traced here: 415 us
  starting transfers between devices  223 us (53%)
  waiting for transfers between devices  107 us (26%)
  local copies, waits for them, and re-layouts  45.8 us (11%)
  other arithmetic  30.9 us (7%)
  matrix products  7.46 us (2%)
    ppermute x43, starting transfers between devices, shift(): return lax.ppermute(x, axis, [(i, (i + step) % n) for i in range(n)])  223 us
    ppermute x43, waiting for transfers between devices, shift(): return lax.ppermute(x, axis, [(i, (i + step) % n) for i in range(n)])  107 us
    unnamed x53, local copies, waits for them, and re-layouts  10.1 us
  transfers between devices with their start and end apart: 43, of which 24 were waited for; matrix products, arithmetic and copies ran while one was open for 5% of the time, Pallas kernels for 0%

profile of v3, /device:TPU:6, one launch (start us, length us, event | category | flops | bytes accessed | tf_op | source)
XLA Modules:
  0.0 415.4 jit_solution(4136581523727281751)
XLA Ops:
  10.8 13.0 %collective-permute-start.7 = (f32[96,2]{0,1:T(2,128)S(1)}, f32[96,2]{0,1:T(2,128)S(1)}, u32[]{:S(2)}, u32[]{:S(2)}) collective-permute-start(f32[96,2]{0,1:T(2,128)S(1)} %pad_maximum_fusion.7), channel_id=1, source_target_pairs={{0,1},{1,0},{2,3},{3,2},{4,5},{5,4},{6,7},{7,6},{8,9},{9,8},{10,11... | collective-permute-start | bytes 2312 | tf_op jit(solution)/shard_map/ppermute | solution.py:25
  36.4 7.4 %collective-permute-start.2 = (bf16[96,512]{1,0:T(8,128)(2,1)}, bf16[96,512]{1,0:T(8,128)(2,1)S(1)}, u32[]{:S(2)}, u32[]{:S(2)}) collective-permute-start(bf16[96,512]{1,0:T(8,128)(2,1)} %param.8), channel_id=1, source_target_pairs={{0,24},{8,32},{16,40},{24,48},{32,56},{40,0},{48,8},{56,16},{1,25}... | collective-permute-start | bytes 294920 | tf_op jit(solution)/shard_map/ppermute | solution.py:25
  52.6 7.1 %collective-permute-done.11 = f32[96,2]{0,1:T(2,128)S(1)} collective-permute-done((f32[96,2]{0,1:T(2,128)S(1)}, f32[96,2]{0,1:T(2,128)S(1)}, u32[]{:S(2)}, u32[]{:S(2)}) %collective-permute-start.11) | collective-permute-done | bytes 800 | tf_op jit(solution)/shard_map/ppermute | solution.py:25
  61.6 9.2 %collective-permute-done.12 = f32[96,2]{0,1:T(2,128)S(1)} collective-permute-done((f32[96,2]{0,1:T(2,128)S(1)}, f32[96,2]{0,1:T(2,128)S(1)}, u32[]{:S(2)}, u32[]{:S(2)}) %collective-permute-start.12) | collective-permute-done | bytes 800 | tf_op jit(solution)/shard_map/ppermute | solution.py:25
  72.8 8.3 %collective-permute-done.13 = f32[96,2]{0,1:T(2,128)S(1)} collective-permute-done((f32[96,2]{0,1:T(2,128)S(1)}, f32[96,2]{0,1:T(2,128)S(1)}, u32[]{:S(2)}, u32[]{:S(2)}) %collective-permute-start.13) | collective-permute-done | bytes 800 | tf_op jit(solution)/shard_map/ppermute | solution.py:25
  83.1 7.4 %collective-permute-done.14 = f32[96,2]{0,1:T(2,128)S(1)} collective-permute-done((f32[96,2]{0,1:T(2,128)S(1)}, f32[96,2]{0,1:T(2,128)S(1)}, u32[]{:S(2)}, u32[]{:S(2)}) %collective-permute-start.14) | collective-permute-done | bytes 800 | tf_op jit(solution)/shard_map/ppermute | solution.py:25
  92.4 5.3 %collective-permute-done.15 = f32[96,2]{0,1:T(2,128)S(1)} collective-permute-done((f32[96,2]{0,1:T(2,128)S(1)}, f32[96,2]{0,1:T(2,128)S(1)}, u32[]{:S(2)}, u32[]{:S(2)}) %collective-permute-start.15) | collective-permute-done | bytes 800 | tf_op jit(solution)/shard_map/ppermute | solution.py:25
  104.1 6.2 %collective-permute-start.17 = (f32[96,2]{0,1:T(2,128)S(1)}, f32[96,2]{0,1:T(2,128)S(1)}, u32[]{:S(2)}, u32[]{:S(2)}) collective-permute-start(f32[96,2]{0,1:T(2,128)S(1)} %get-tuple-element.16), channel_id=1, source_target_pairs={{0,56},{8,0},{16,8},{24,16},{32,24},{40,32},{48,40},{56,48},{1,57}... | collective-permute-start | bytes 2312 | tf_op jit(solution)/shard_map/ppermute | solution.py:25
  120.9 6.2 %collective-permute-start.6 = (bf16[96,512]{1,0:T(8,128)(2,1)S(1)}, bf16[96,512]{1,0:T(8,128)(2,1)S(1)}, u32[]{:S(2)}, u32[]{:S(2)}) collective-permute-start(bf16[96,512]{1,0:T(8,128)(2,1)S(1)} %copy-done.2), channel_id=1, source_target_pairs={{0,56},{8,0},{16,8},{24,16},{32,24},{40,32},{48,40},{56,48},{1,57}... | collective-permute-start | bytes 294920 | tf_op jit(solution)/shard_map/ppermute | solution.py:25
  149.0 8.8 %collective-permute-done.18 = bf16[192,1536]{1,0:T(8,128)(2,1)S(1)} collective-permute-done((bf16[192,1536]{1,0:T(8,128)(2,1)}, bf16[192,1536]{1,0:T(8,128)(2,1)S(1)}, u32[]{:S(2)}, u32[]{:S(2)}) %collective-permute-start.18) | collective-permute-done | bytes 589856 | tf_op jit(solution)/shard_map/ppermute | solution.py:25
  162.1 10.0 %collective-permute-start.21 = (bf16[192,1536]{1,0:T(8,128)(2,1)S(1)}, bf16[192,1536]{1,0:T(8,128)(2,1)S(1)}, u32[]{:S(2)}, u32[]{:S(2)}) collective-permute-start(bf16[192,1536]{1,0:T(8,128)(2,1)S(1)} %add_convert_fusion.1), channel_id=1, source_target_pairs={{0,1},{1,0},{2,3},{3,2},{4,5},{5,4},{6,7},{7,6},{8,9},{9,8},{10,11... | collective-permute-start | bytes 1769480 | tf_op jit(solution)/shard_map/ppermute | solution.py:25
  174.8 20.3 %collective-permute-done.21 = bf16[192,1536]{1,0:T(8,128)(2,1)S(1)} collective-permute-done((bf16[192,1536]{1,0:T(8,128)(2,1)S(1)}, bf16[192,1536]{1,0:T(8,128)(2,1)S(1)}, u32[]{:S(2)}, u32[]{:S(2)}) %collective-permute-start.21) | collective-permute-done | bytes 589856 | tf_op jit(solution)/shard_map/ppermute | solution.py:25
  208.2 7.3 %collective-permute-done.23 = bf16[192,1536]{1,0:T(8,128)(2,1)S(1)} collective-permute-done((bf16[192,1536]{1,0:T(8,128)(2,1)S(1)}, bf16[192,1536]{1,0:T(8,128)(2,1)S(1)}, u32[]{:S(2)}, u32[]{:S(2)}) %collective-permute-start.23) | collective-permute-done | bytes 589856 | tf_op jit(solution)/shard_map/ppermute | solution.py:25
  239.2 5.4 %fusion.18 = (bf16[384,2,512]{2,1,0:T(2,128)(2,1)S(1)}, bf16[384,2,512]{2,1,0:T(2,128)(2,1)}) fusion(bf16[2,384,1,512]{3,2,1,0:T(2,128)(2,1)} %copy.49, bf16[2,384,1,512]{3,2,1,0:T(2,128)(2,1)S(1)} %copy.48), kind=kLoop, calls=%fused_computation.55 | loop fusion | flops 3145728 | bytes 3145728 | tf_op jit(solution)/shard_map/squeeze | solution.py:164
  251.1 5.5 %broadcast_select_fusion.1 = (bf16[272,2,512]{2,1,0:T(2,128)(2,1)S(1)}, bf16[272,2,512]{2,1,0:T(2,128)(2,1)S(1)}) fusion(pred[272]{0:T(512)(128)(4,1)S(1)} %get-tuple-element.60, bf16[272,2,512]{2,1,0:T(2,128)(2,1)S(1)} %gather_fusion.4, pred[272]{0:T(512)(128)(4,1)S(1)} %get-tuple-element.58, bf16[2,272,2,512]{3,2,1,0:T(2,128)(2,1)} %param.12, ...), kind=kLoop, calls=%fused_computation.35 | loop fusion | flops 1114112 | bytes 3343424 | tf_op jit(solution)/shard_map/jit(_where)/select_n | solution.py:117
  270.7 5.5 %collective-permute-start.26 = (f32[192,4]{1,0:T(8,128)}, f32[192,4]{1,0:T(8,128)}, u32[]{:S(2)}, u32[]{:S(2)}) collective-permute-start(f32[192,4]{1,0:T(8,128)} %copy.62), channel_id=1, source_target_pairs={{0,4},{2,6},{4,0},{6,2},{1,5},{3,7},{5,1},{7,3},{8,12},{10,14},{12... | collective-permute-start | bytes 9224 | tf_op jit(solution)/shard_map/ppermute | solution.py:25
  305.3 10.1 %collective-permute-start.32 = (bf16[192,516]{1,0:T(8,128)(2,1)S(1)}, bf16[192,516]{1,0:T(8,128)(2,1)S(1)}, u32[]{:S(2)}, u32[]{:S(2)}) collective-permute-start(bf16[192,516]{1,0:T(8,128)(2,1)S(1)} %fusion.22), channel_id=1, source_target_pairs={{0,1},{1,0},{2,3},{3,2},{4,5},{5,4},{6,7},{7,6},{8,9},{9,8},{10,11... | collective-permute-start | bytes 594440 | tf_op jit(solution)/shard_map/ppermute | solution.py:25
  316.0 7.1 %collective-permute-done.32 = bf16[192,516]{1,0:T(8,128)(2,1)S(1)} collective-permute-done((bf16[192,516]{1,0:T(8,128)(2,1)S(1)}, bf16[192,516]{1,0:T(8,128)(2,1)S(1)}, u32[]{:S(2)}, u32[]{:S(2)}) %collective-permute-start.32) | collective-permute-done | bytes 198176 | tf_op jit(solution)/shard_map/ppermute | solution.py:25
  326.8 5.2 %collective-permute-start.34 = (bf16[192,512]{1,0:T(8,128)(2,1)S(1)}, bf16[192,512]{1,0:T(8,128)(2,1)S(1)}, u32[]{:S(2)}, u32[]{:S(2)}) collective-permute-start(bf16[192,512]{1,0:T(8,128)(2,1)S(1)} %fusion.24), channel_id=1, source_target_pairs={{0,4},{2,6},{4,0},{6,2},{1,5},{3,7},{5,1},{7,3},{8,12},{10,14},{12... | collective-permute-start | bytes 589832 | tf_op jit(solution)/shard_map/ppermute | solution.py:25
  341.1 10.7 %collective-permute-start.36 = (bf16[96,512]{1,0:T(8,128)(2,1)S(1)}, bf16[96,512]{1,0:T(8,128)(2,1)S(1)}, u32[]{:S(2)}, u32[]{:S(2)}) collective-permute-start(bf16[96,512]{1,0:T(8,128)(2,1)S(1)} %get-tuple-element.29), channel_id=1, source_target_pairs={{0,8},{8,16},{16,24},{24,32},{32,40},{40,48},{48,56},{56,0},{1,9},... | collective-permute-start | bytes 294920 | tf_op jit(solution)/shard_map/ppermute | solution.py:25
  351.9 8.6 %collective-permute-start.37 = (bf16[96,512]{1,0:T(8,128)(2,1)S(1)}, bf16[96,512]{1,0:T(8,128)(2,1)S(1)}, u32[]{:S(2)}, u32[]{:S(2)}) collective-permute-start(bf16[96,512]{1,0:T(8,128)(2,1)S(1)} %get-tuple-element.35), channel_id=1, source_target_pairs={{0,16},{8,24},{16,32},{24,40},{32,48},{40,56},{48,0},{56,8},{1,17}... | collective-permute-start | bytes 294920 | tf_op jit(solution)/shard_map/ppermute | solution.py:25
  360.5 30.0 %collective-permute-start.38 = (bf16[96,512]{1,0:T(8,128)(2,1)S(1)}, bf16[96,512]{1,0:T(8,128)(2,1)S(1)}, u32[]{:S(2)}, u32[]{:S(2)}) collective-permute-start(bf16[96,512]{1,0:T(8,128)(2,1)S(1)} %get-tuple-element.34), channel_id=1, source_target_pairs={{0,24},{8,32},{16,40},{24,48},{32,56},{40,0},{48,8},{56,16},{1,25}... | collective-permute-start | bytes 294920 | tf_op jit(solution)/shard_map/ppermute | solution.py:25
  392.5 7.8 %collective-permute-start.40 = (bf16[96,512]{1,0:T(8,128)(2,1)S(1)}, bf16[96,512]{1,0:T(8,128)(2,1)S(1)}, u32[]{:S(2)}, u32[]{:S(2)}) collective-permute-start(bf16[96,512]{1,0:T(8,128)(2,1)S(1)} %get-tuple-element.32), channel_id=1, source_target_pairs={{0,40},{8,48},{16,56},{24,0},{32,8},{40,16},{48,24},{56,32},{1,41}... | collective-permute-start | bytes 294920 | tf_op jit(solution)/shard_map/ppermute | solution.py:25
  400.3 7.8 %collective-permute-start.41 = (bf16[96,512]{1,0:T(8,128)(2,1)S(1)}, bf16[96,512]{1,0:T(8,128)(2,1)S(1)}, u32[]{:S(2)}, u32[]{:S(2)}) collective-permute-start(bf16[96,512]{1,0:T(8,128)(2,1)S(1)} %get-tuple-element.31), channel_id=1, source_target_pairs={{0,48},{8,56},{16,0},{24,8},{32,16},{40,24},{48,32},{56,40},{1,49}... | collective-permute-start | bytes 294920 | tf_op jit(solution)/shard_map/ppermute | solution.py:25
  (206 shorter events, 193.0 us)
Async XLA Ops:
  0.6 116.0 %collective-permute-start = (bf16[96,512]{1,0:T(8,128)(2,1)}, bf16[96,512]{1,0:T(8,128)(2,1)S(1)}, u32[]{:S(2)}, u32[]{:S(2)}) collective-permute-start(bf16[96,512]{1,0:T(8,128)(2,1)} %param.8), channel_id=1, source_target_pairs={{0,8},{8,16},{16,24},{24,32},{32,40},{40,48},{48,56},{56,0},{1,9},... | collective-permute-start | bytes 294920 | tf_op jit(solution)/shard_map/ppermute | solution.py:25
  4.6 116.3 %collective-permute-start.1 = (bf16[96,512]{1,0:T(8,128)(2,1)}, bf16[96,512]{1,0:T(8,128)(2,1)S(1)}, u32[]{:S(2)}, u32[]{:S(2)}) collective-permute-start(bf16[96,512]{1,0:T(8,128)(2,1)} %param.8), channel_id=1, source_target_pairs={{0,16},{8,24},{16,32},{24,40},{32,48},{40,56},{48,0},{56,8},{1,17}... | collective-permute-start | bytes 294920 | tf_op jit(solution)/shard_map/ppermute | solution.py:25
  10.8 14.6 %collective-permute-start.7 = (f32[96,2]{0,1:T(2,128)S(1)}, f32[96,2]{0,1:T(2,128)S(1)}, u32[]{:S(2)}, u32[]{:S(2)}) collective-permute-start(f32[96,2]{0,1:T(2,128)S(1)} %pad_maximum_fusion.7), channel_id=1, source_target_pairs={{0,1},{1,0},{2,3},{3,2},{4,5},{5,4},{6,7},{7,6},{8,9},{9,8},{10,11... | collective-permute-start | bytes 2312 | tf_op jit(solution)/shard_map/ppermute | solution.py:25
  30.4 13.5 %collective-permute-start.8 = (f32[96,2]{0,1:T(2,128)S(1)}, f32[96,2]{0,1:T(2,128)S(1)}, u32[]{:S(2)}, u32[]{:S(2)}) collective-permute-start(f32[96,2]{0,1:T(2,128)S(1)} %fusion.53), channel_id=1, source_target_pairs={{0,2},{2,4},{4,6},{6,0},{1,3},{3,5},{5,7},{7,1},{8,10},{10,12},{12... | collective-permute-start | bytes 2312 | tf_op jit(solution)/shard_map/ppermute | solution.py:25
  32.3 15.3 %collective-permute-start.9 = (f32[96,2]{0,1:T(2,128)S(1)}, f32[96,2]{0,1:T(2,128)S(1)}, u32[]{:S(2)}, u32[]{:S(2)}) collective-permute-start(f32[96,2]{0,1:T(2,128)S(1)} %fusion.53), channel_id=1, source_target_pairs={{0,4},{2,6},{4,0},{6,2},{1,5},{3,7},{5,1},{7,3},{8,12},{10,14},{12... | collective-permute-start | bytes 2312 | tf_op jit(solution)/shard_map/ppermute | solution.py:25
  36.4 90.7 %collective-permute-start.2 = (bf16[96,512]{1,0:T(8,128)(2,1)}, bf16[96,512]{1,0:T(8,128)(2,1)S(1)}, u32[]{:S(2)}, u32[]{:S(2)}) collective-permute-start(bf16[96,512]{1,0:T(8,128)(2,1)} %param.8), channel_id=1, source_target_pairs={{0,24},{8,32},{16,40},{24,48},{32,56},{40,0},{48,8},{56,16},{1,25}... | collective-permute-start | bytes 294920 | tf_op jit(solution)/shard_map/ppermute | solution.py:25
  43.9 83.3 %collective-permute-start.3 = (bf16[96,512]{1,0:T(8,128)(2,1)}, bf16[96,512]{1,0:T(8,128)(2,1)S(1)}, u32[]{:S(2)}, u32[]{:S(2)}) collective-permute-start(bf16[96,512]{1,0:T(8,128)(2,1)} %param.8), channel_id=1, source_target_pairs={{0,32},{8,40},{16,48},{24,56},{32,0},{40,8},{48,16},{56,24},{1,33}... | collective-permute-start | bytes 294920 | tf_op jit(solution)/shard_map/ppermute | solution.py:25
  111.6 15.6 %collective-permute-start.4 = (bf16[96,512]{1,0:T(8,128)(2,1)S(1)}, bf16[96,512]{1,0:T(8,128)(2,1)S(1)}, u32[]{:S(2)}, u32[]{:S(2)}) collective-permute-start(bf16[96,512]{1,0:T(8,128)(2,1)S(1)} %copy-done.2), channel_id=1, source_target_pairs={{0,40},{8,48},{16,56},{24,0},{32,8},{40,16},{48,24},{56,32},{1,41}... | collective-permute-start | bytes 294920 | tf_op jit(solution)/shard_map/ppermute | solution.py:25
  135.3 22.5 %collective-permute-start.18 = (bf16[192,1536]{1,0:T(8,128)(2,1)}, bf16[192,1536]{1,0:T(8,128)(2,1)S(1)}, u32[]{:S(2)}, u32[]{:S(2)}) collective-permute-start(bf16[192,1536]{1,0:T(8,128)(2,1)} %get-tuple-element.21), channel_id=1, source_target_pairs={{0,2},{2,4},{4,6},{6,0},{1,3},{3,5},{5,7},{7,1},{8,10},{10,12},{12... | collective-permute-start | bytes 1769480 | tf_op jit(solution)/shard_map/ppermute | solution.py:25
  139.1 18.7 %collective-permute-start.19 = (bf16[192,1536]{1,0:T(8,128)(2,1)}, bf16[192,1536]{1,0:T(8,128)(2,1)}, u32[]{:S(2)}, u32[]{:S(2)}) collective-permute-start(bf16[192,1536]{1,0:T(8,128)(2,1)} %get-tuple-element.23), channel_id=1, source_target_pairs={{0,4},{2,6},{4,0},{6,2},{1,5},{3,7},{5,1},{7,3},{8,12},{10,14},{12... | collective-permute-start | bytes 1769480 | tf_op jit(solution)/shard_map/ppermute | solution.py:25
  141.6 18.7 %collective-permute-start.20 = (bf16[192,1536]{1,0:T(8,128)(2,1)}, bf16[192,1536]{1,0:T(8,128)(2,1)}, u32[]{:S(2)}, u32[]{:S(2)}) collective-permute-start(bf16[192,1536]{1,0:T(8,128)(2,1)} %get-tuple-element.22), channel_id=1, source_target_pairs={{0,6},{2,0},{4,2},{6,4},{1,7},{3,1},{5,3},{7,5},{8,14},{10,8},{12,... | collective-permute-start | bytes 1769480 | tf_op jit(solution)/shard_map/ppermute | solution.py:25
  162.1 33.0 %collective-permute-start.21 = (bf16[192,1536]{1,0:T(8,128)(2,1)S(1)}, bf16[192,1536]{1,0:T(8,128)(2,1)S(1)}, u32[]{:S(2)}, u32[]{:S(2)}) collective-permute-start(bf16[192,1536]{1,0:T(8,128)(2,1)S(1)} %add_convert_fusion.1), channel_id=1, source_target_pairs={{0,1},{1,0},{2,3},{3,2},{4,5},{5,4},{6,7},{7,6},{8,9},{9,8},{10,11... | collective-permute-start | bytes 1769480 | tf_op jit(solution)/shard_map/ppermute | solution.py:25
  195.2 13.0 %collective-permute-start.22 = (bf16[192,1536]{1,0:T(8,128)(2,1)S(1)}, bf16[192,1536]{1,0:T(8,128)(2,1)S(1)}, u32[]{:S(2)}, u32[]{:S(2)}) collective-permute-start(bf16[192,1536]{1,0:T(8,128)(2,1)S(1)} %add_convert_fusion), channel_id=1, source_target_pairs={{0,2},{2,4},{4,6},{6,0},{1,3},{3,5},{5,7},{7,1},{8,10},{10,12},{12... | collective-permute-start | bytes 1769480 | tf_op jit(solution)/shard_map/ppermute | solution.py:25
  198.3 17.2 %collective-permute-start.23 = (bf16[192,1536]{1,0:T(8,128)(2,1)S(1)}, bf16[192,1536]{1,0:T(8,128)(2,1)S(1)}, u32[]{:S(2)}, u32[]{:S(2)}) collective-permute-start(bf16[192,1536]{1,0:T(8,128)(2,1)S(1)} %add_convert_fusion), channel_id=1, source_target_pairs={{0,4},{2,6},{4,0},{6,2},{1,5},{3,7},{5,1},{7,3},{8,12},{10,14},{12... | collective-permute-start | bytes 1769480 | tf_op jit(solution)/shard_map/ppermute | solution.py:25
  203.3 14.1 %collective-permute-start.24 = (bf16[192,1536]{1,0:T(8,128)(2,1)S(1)}, bf16[192,1536]{1,0:T(8,128)(2,1)S(1)}, u32[]{:S(2)}, u32[]{:S(2)}) collective-permute-start(bf16[192,1536]{1,0:T(8,128)(2,1)S(1)} %add_convert_fusion), channel_id=1, source_target_pairs={{0,6},{2,0},{4,2},{6,4},{1,7},{3,1},{5,3},{7,5},{8,14},{10,8},{12,... | collective-permute-start | bytes 1769480 | tf_op jit(solution)/shard_map/ppermute | solution.py:25
  267.5 12.5 %collective-permute-start.25 = (f32[192,4]{1,0:T(8,128)}, f32[192,4]{1,0:T(8,128)}, u32[]{:S(2)}, u32[]{:S(2)}) collective-permute-start(f32[192,4]{1,0:T(8,128)} %copy.61), channel_id=1, source_target_pairs={{0,2},{2,4},{4,6},{6,0},{1,3},{3,5},{5,7},{7,1},{8,10},{10,12},{12... | collective-permute-start | bytes 9224 | tf_op jit(solution)/shard_map/ppermute | solution.py:25
  285.2 15.8 %collective-permute-start.31 = (f32[192,4]{1,0:T(8,128)S(1)}, f32[192,4]{1,0:T(8,128)S(1)}, u32[]{:S(2)}, u32[]{:S(2)}) collective-permute-start(f32[192,4]{1,0:T(8,128)S(1)} %get-tuple-element.14), channel_id=1, source_target_pairs={{0,1},{1,0},{2,3},{3,2},{4,5},{5,4},{6,7},{7,6},{8,9},{9,8},{10,11... | collective-permute-start | bytes 9224 | tf_op jit(solution)/shard_map/ppermute | solution.py:25
  290.1 12.8 %collective-permute-start.28 = (bf16[192,516]{1,0:T(8,128)(2,1)S(1)}, bf16[192,516]{1,0:T(8,128)(2,1)S(1)}, u32[]{:S(2)}, u32[]{:S(2)}) collective-permute-start(bf16[192,516]{1,0:T(8,128)(2,1)S(1)} %get-tuple-element.26), channel_id=1, source_target_pairs={{0,2},{2,4},{4,6},{6,0},{1,3},{3,5},{5,7},{7,1},{8,10},{10,12},{12... | collective-permute-start | bytes 594440 | tf_op jit(solution)/shard_map/ppermute | solution.py:25
  305.3 17.9 %collective-permute-start.32 = (bf16[192,516]{1,0:T(8,128)(2,1)S(1)}, bf16[192,516]{1,0:T(8,128)(2,1)S(1)}, u32[]{:S(2)}, u32[]{:S(2)}) collective-permute-start(bf16[192,516]{1,0:T(8,128)(2,1)S(1)} %fusion.22), channel_id=1, source_target_pairs={{0,1},{1,0},{2,3},{3,2},{4,5},{5,4},{6,7},{7,6},{8,9},{9,8},{10,11... | collective-permute-start | bytes 594440 | tf_op jit(solution)/shard_map/ppermute | solution.py:25
  341.1 59.2 %collective-permute-start.36 = (bf16[96,512]{1,0:T(8,128)(2,1)S(1)}, bf16[96,512]{1,0:T(8,128)(2,1)S(1)}, u32[]{:S(2)}, u32[]{:S(2)}) collective-permute-start(bf16[96,512]{1,0:T(8,128)(2,1)S(1)} %get-tuple-element.29), channel_id=1, source_target_pairs={{0,8},{8,16},{16,24},{24,32},{32,40},{40,48},{48,56},{56,0},{1,9},... | collective-permute-start | bytes 294920 | tf_op jit(solution)/shard_map/ppermute | solution.py:25
  351.9 56.3 %collective-permute-start.37 = (bf16[96,512]{1,0:T(8,128)(2,1)S(1)}, bf16[96,512]{1,0:T(8,128)(2,1)S(1)}, u32[]{:S(2)}, u32[]{:S(2)}) collective-permute-start(bf16[96,512]{1,0:T(8,128)(2,1)S(1)} %get-tuple-element.35), channel_id=1, source_target_pairs={{0,16},{8,24},{16,32},{24,40},{32,48},{40,56},{48,0},{56,8},{1,17}... | collective-permute-start | bytes 294920 | tf_op jit(solution)/shard_map/ppermute | solution.py:25
  360.5 52.2 %collective-permute-start.38 = (bf16[96,512]{1,0:T(8,128)(2,1)S(1)}, bf16[96,512]{1,0:T(8,128)(2,1)S(1)}, u32[]{:S(2)}, u32[]{:S(2)}) collective-permute-start(bf16[96,512]{1,0:T(8,128)(2,1)S(1)} %get-tuple-element.34), channel_id=1, source_target_pairs={{0,24},{8,32},{16,40},{24,48},{32,56},{40,0},{48,8},{56,16},{1,25}... | collective-permute-start | bytes 294920 | tf_op jit(solution)/shard_map/ppermute | solution.py:25
  390.5 22.2 %collective-permute-start.39 = (bf16[96,512]{1,0:T(8,128)(2,1)S(1)}, bf16[96,512]{1,0:T(8,128)(2,1)S(1)}, u32[]{:S(2)}, u32[]{:S(2)}) collective-permute-start(bf16[96,512]{1,0:T(8,128)(2,1)S(1)} %get-tuple-element.33), channel_id=1, source_target_pairs={{0,32},{8,40},{16,48},{24,56},{32,0},{40,8},{48,16},{56,24},{1,33}... | collective-permute-start | bytes 294920 | tf_op jit(solution)/shard_map/ppermute | solution.py:25
  392.5 20.2 %collective-permute-start.40 = (bf16[96,512]{1,0:T(8,128)(2,1)S(1)}, bf16[96,512]{1,0:T(8,128)(2,1)S(1)}, u32[]{:S(2)}, u32[]{:S(2)}) collective-permute-start(bf16[96,512]{1,0:T(8,128)(2,1)S(1)} %get-tuple-element.32), channel_id=1, source_target_pairs={{0,40},{8,48},{16,56},{24,0},{32,8},{40,16},{48,24},{56,32},{1,41}... | collective-permute-start | bytes 294920 | tf_op jit(solution)/shard_map/ppermute | solution.py:25
  (33 other events, 728.5 us)

commit v4 on v3

--- a/solution.py
+++ b/solution.py
@@ -53,7 +53,22 @@
     return taken.reshape((n * x.shape[0],) + x.shape[1:])
 
 
+def split3(x):
+    pieces = []
+    for _ in range(3):
+        piece = x.astype(jnp.bfloat16)
+        pieces.append(piece)
+        x = x - piece.astype(jnp.float32)
+    return jnp.concatenate(pieces, axis=1)
+
+
+def join3(x, heads):
+    wide = x.astype(jnp.float32)
+    return wide[:, :heads] + wide[:, heads : 2 * heads] + wide[:, 2 * heads :]
+
+
 def merge(parts, heads):
+    parts = [(block[:, : -3 * heads], join3(block[:, -3 * heads :], heads)) for block in parts]
     top = parts[0][1]
     for _, high in parts[1:]:
         top = jnp.maximum(top, high)
@@ -69,13 +84,13 @@
     n = lax.axis_size("gyy")
     me = lax.axis_index("gyy")
     rows = packed.shape[0] // n
+    packed = jnp.concatenate([packed, split3(tops)], axis=1)
     parts = []
     for step in range(n):
         block = lax.dynamic_slice_in_dim(packed, ((me + step) % n) * rows, rows)
-        high = lax.dynamic_slice_in_dim(tops, ((me + step) % n) * rows, rows)
-        parts.append((block, high) if step == 0 else shift((block, high), "gyy", step))
+        parts.append(block if step == 0 else shift(block, "gyy", step))
     total, top = merge(parts, heads)
-    own = (total.astype(packed.dtype), top)
+    own = jnp.concatenate([total.astype(packed.dtype), split3(top)], axis=1)
     total, _ = merge([own, shift(own, "gyz", 1)], heads)
     width = total.shape[1] - heads
     sums = total[:, :width].reshape(rows, heads, width // heads)
@@ -91,10 +106,22 @@
     return swap_combine(swap_combine(x, "gyz", jnp.maximum), "gyy", jnp.maximum)
 
 
+def exchange_scatter_sum(x, axis):
+    n = lax.axis_size(axis)
+    split = x.reshape((n, x.shape[0] // n) + x.shape[1:])
+    return jnp.sum(lax.all_to_all(split, axis, 0, 0).astype(jnp.float32), axis=0)
+
+
+def exchange_gather(x, axis):
+    n = lax.axis_size(axis)
+    copies = jnp.broadcast_to(x[None], (n,) + x.shape)
+    return lax.all_to_all(copies, axis, 0, 0).reshape((n * x.shape[0],) + x.shape[1:])
+
+
 def gy_sum_rows(x):
-    part = ring_scatter_sum(x, "gyy").astype(x.dtype)
+    part = exchange_scatter_sum(x, "gyy").astype(x.dtype)
     part = swap_combine(part, "gyz", jnp.add).astype(x.dtype)
-    return ring_gather(part, "gyy")
+    return exchange_gather(part, "gyy")
 
 
 def partial_attend(query, keys, values, valid, distance, slopes, scale):
@@ -119,19 +146,17 @@
 
 def shards(hidden, ln_gain, w_qkv, w_out, kv_cache, cache_len):
     hidden_f = hidden.astype(jnp.float32)
-    gathered = ring_gather(hidden, "gx").astype(jnp.float32)
-    sums = gy_sum(jnp.stack([jnp.sum(hidden_f, axis=1), jnp.sum(hidden_f * hidden_f, axis=1)], axis=1))
-    sums = ring_gather(sums, "gx")
-    mean = sums[:, 0] / D
-    var = sums[:, 1] / D - mean * mean
+    sums = gy_sum(jnp.stack([jnp.sum(hidden_f, axis=1), jnp.sum(hidden_f * hidden_f, axis=1)]))
+    mean = sums[0] / D
+    var = sums[1] / D - mean * mean
     normed = (
-        (gathered - mean[:, None]) * lax.rsqrt(var + norm_eps)[:, None] * ln_gain[None, :]
+        (hidden_f - mean[:, None]) * lax.rsqrt(var + norm_eps)[:, None] * ln_gain[None, :]
     ).astype(jnp.bfloat16)
     local_heads = w_qkv.shape[1]
     head_size = w_qkv.shape[2] // 3
     weight_flat = w_qkv.reshape(w_qkv.shape[0], local_heads * 3 * head_size)
     partial_value = jnp.dot(
-        normed,
+        ring_gather(normed, "gx"),
         weight_flat,
         preferred_element_type=jnp.float32,
     )

time: 418 us -> 364 us (0.87)
  the two profiles are of different devices: /device:TPU:6 before, /device:TPU:1 now
where the time goes in v4:
time: 364 us; the launch traced here: 362 us
  starting transfers between devices  180 us (49%)
  waiting for transfers between devices  68.6 us (19%)
  local copies, waits for them, and re-layouts  47.6 us (13%)
  blocking collectives  31.5 us (9%)
  other arithmetic  29 us (8%)
  matrix products  4.07 us (1%)
    ppermute x26, starting transfers between devices, shift(): return lax.ppermute(x, axis, [(i, (i + step) % n) for i in range(n)])  176 us
    ppermute x26, waiting for transfers between devices, shift(): return lax.ppermute(x, axis, [(i, (i + step) % n) for i in range(n)])  54.1 us
    all_to_all x1, blocking collectives, exchange_scatter_sum(): lax.all_to_all(split, axis, 0, 0).astype(jnp.float32)  31.5 us
    all_to_all x1, waiting for transfers between devices, exchange_gather(): lax.all_to_all(copies, axis, 0, 0).reshape((n * x.shape[0],) + x.shape[1:])  14.5 us
    another operation x2, local copies, waits for them, and re-layouts, shards(): jnp.stack([qkv[:, :, :, head_size:2 * head_size].reshape(requests, group,...  8.27 us
    unnamed x44, local copies, waits for them, and re-layouts  7.35 us
  transfers between devices with their start and end apart: 27, of which 12 were waited for; matrix products, arithmetic and copies ran while one was open for 5% of the time, Pallas kernels for 0%

profile of v4, /device:TPU:1, one launch (start us, length us, event | category | flops | bytes accessed | tf_op | source)
XLA Modules:
  0.0 362.5 jit_solution(7321941750399935498)
XLA Ops:
  1.8 16.3 %collective-permute-start = (f32[2,96]{1,0:T(2,128)S(1)}, f32[2,96]{1,0:T(2,128)S(1)}, u32[]{:S(2)}, u32[]{:S(2)}) collective-permute-start(f32[2,96]{1,0:T(2,128)S(1)} %pad_maximum_fusion.7), channel_id=1, source_target_pairs={{0,1},{1,0},{2,3},{3,2},{4,5},{5,4},{6,7},{7,6},{8,9},{9,8},{10,11... | collective-permute-start | bytes 2312 | tf_op jit(solution)/shard_map/ppermute | solution.py:25
  19.0 4.6 %collective-permute-start.3 = (f32[2,96]{1,0:T(2,128)S(1)}, f32[2,96]{1,0:T(2,128)S(1)}, u32[]{:S(2)}, u32[]{:S(2)}) collective-permute-start(f32[2,96]{1,0:T(2,128)S(1)} %fusion.53), channel_id=1, source_target_pairs={{0,6},{2,0},{4,2},{6,4},{1,7},{3,1},{5,3},{7,5},{8,14},{10,8},{12,... | collective-permute-start | bytes 2312 | tf_op jit(solution)/shard_map/ppermute | solution.py:25
  35.2 3.1 collective-permute-start.5
  38.3 6.5 %collective-permute-start.6 = (bf16[96,512]{1,0:T(8,128)(2,1)S(1)}, bf16[96,512]{1,0:T(8,128)(2,1)S(1)}, u32[]{:S(2)}, u32[]{:S(2)}) collective-permute-start(bf16[96,512]{1,0:T(8,128)(2,1)S(1)} %get-tuple-element.14), channel_id=1, source_target_pairs={{0,24},{8,32},{16,40},{24,48},{32,56},{40,0},{48,8},{56,16},{1,25}... | collective-permute-start | bytes 294920 | tf_op jit(solution)/shard_map/ppermute | solution.py:25
  44.8 4.0 %collective-permute-start.7 = (bf16[96,512]{1,0:T(8,128)(2,1)S(1)}, bf16[96,512]{1,0:T(8,128)(2,1)S(1)}, u32[]{:S(2)}, u32[]{:S(2)}) collective-permute-start(bf16[96,512]{1,0:T(8,128)(2,1)S(1)} %get-tuple-element.14), channel_id=1, source_target_pairs={{0,32},{8,40},{16,48},{24,56},{32,0},{40,8},{48,16},{56,24},{1,33}... | collective-permute-start | bytes 294920 | tf_op jit(solution)/shard_map/ppermute | solution.py:25
  48.9 6.5 %collective-permute-start.8 = (bf16[96,512]{1,0:T(8,128)(2,1)S(1)}, bf16[96,512]{1,0:T(8,128)(2,1)S(1)}, u32[]{:S(2)}, u32[]{:S(2)}) collective-permute-start(bf16[96,512]{1,0:T(8,128)(2,1)S(1)} %get-tuple-element.14), channel_id=1, source_target_pairs={{0,40},{8,48},{16,56},{24,0},{32,8},{40,16},{48,24},{56,32},{1,41}... | collective-permute-start | bytes 294920 | tf_op jit(solution)/shard_map/ppermute | solution.py:25
  55.4 4.3 %collective-permute-start.9 = (bf16[96,512]{1,0:T(8,128)(2,1)S(1)}, bf16[96,512]{1,0:T(8,128)(2,1)S(1)}, u32[]{:S(2)}, u32[]{:S(2)}) collective-permute-start(bf16[96,512]{1,0:T(8,128)(2,1)S(1)} %get-tuple-element.14), channel_id=1, source_target_pairs={{0,48},{8,56},{16,0},{24,8},{32,16},{40,24},{48,32},{56,40},{1,49}... | collective-permute-start | bytes 294920 | tf_op jit(solution)/shard_map/ppermute | solution.py:25
  70.8 31.5 %all_to_all.10 = bf16[4,192,1536]{2,1,0:T(8,128)(2,1)S(1)} all-to-all(bf16[4,192,1536]{2,1,0:T(8,128)(2,1)S(1)} %bitcast.168), channel_id=1, replica_groups=mesh['req'=8,'gx'=8,'gyy'=4,'gyz'=2] {'gyy'}, dimensions={0} | all-to-all | bytes 4718592 | tf_op jit(solution)/shard_map/all_to_all | solution.py:112
  102.9 7.9 %collective-permute-start.11 = (bf16[192,1536]{1,0:T(8,128)(2,1)S(1)}, bf16[192,1536]{1,0:T(8,128)(2,1)S(1)}, u32[]{:S(2)}, u32[]{:S(2)}) collective-permute-start(bf16[192,1536]{1,0:T(8,128)(2,1)S(1)} %reduce_sum.50), channel_id=1, source_target_pairs={{0,1},{1,0},{2,3},{3,2},{4,5},{5,4},{6,7},{7,6},{8,9},{9,8},{10,11... | collective-permute-start | bytes 1769480 | tf_op jit(solution)/shard_map/ppermute | solution.py:25
  110.8 16.2 %collective-permute-done.11 = bf16[192,1536]{1,0:T(8,128)(2,1)S(1)} collective-permute-done((bf16[192,1536]{1,0:T(8,128)(2,1)S(1)}, bf16[192,1536]{1,0:T(8,128)(2,1)S(1)}, u32[]{:S(2)}, u32[]{:S(2)}) %collective-permute-start.11) | collective-permute-done | bytes 589856 | tf_op jit(solution)/shard_map/ppermute | solution.py:25
  128.8 3.8 %all-to-all-start.1 = ((bf16[4,192,1536]{2,1,0:T(8,128)(2,1)}), bf16[4,192,1536]{2,1,0:T(8,128)(2,1)S(1)}, u32[]{:S(2)}, u32[]{:S(2)}) async-start(bf16[4,192,1536]{2,1,0:T(8,128)(2,1)} %broadcast_in_dim.124), calls=%async_computation.1 | async-start | bytes 4718592 | tf_op jit(solution)/shard_map/all_to_all | solution.py:118
  142.0 14.5 %all-to-all-done.1 = bf16[4,192,1536]{2,1,0:T(8,128)(2,1)S(1)} async-done(((bf16[4,192,1536]{2,1,0:T(8,128)(2,1)}), bf16[4,192,1536]{2,1,0:T(8,128)(2,1)S(1)}, u32[]{:S(2)}, u32[]{:S(2)}) %all-to-all-start.1) | async-done | bytes 2359328 | tf_op jit(solution)/shard_map/all_to_all | solution.py:118
  164.1 3.5 copy.76
  168.9 4.8 %copy.75 = bf16[2,384,1,512]{3,2,1,0:T(2,128)(2,1)} copy(bf16[2,384,1,512]{1,3,0,2:T(8,128)(2,1)} %bitcast.167) | data formatting | bytes 1572864 | tf_op jit(solution)/shard_map/stack;reshape | solution.py:180
  173.7 5.4 %fusion.18 = (bf16[384,2,512]{2,1,0:T(2,128)(2,1)}, bf16[384,2,512]{2,1,0:T(2,128)(2,1)S(1)}) fusion(bf16[2,384,1,512]{3,2,1,0:T(2,128)(2,1)S(1)} %copy.76, bf16[2,384,1,512]{3,2,1,0:T(2,128)(2,1)} %copy.75), kind=kLoop, calls=%fused_computation.41 | loop fusion | flops 3145728 | bytes 3145728 | tf_op jit(solution)/shard_map/squeeze | solution.py:189
  182.1 3.9 %gather_fusion.3 = bf16[272,2,512]{2,1,0:T(2,128)(2,1)} fusion(bf16[384,2,512]{2,1,0:T(2,128)(2,1)S(1)} %get-tuple-element.16, s32[1024]{0:T(1024)S(1)} %pad_clamp_fusion.1), kind=kCustom, calls=%fused_computation.1.clone | custom fusion | bytes 1115200 | tf_op jit(solution)/shard_map/jit(_take)/gather | solution.py:143
  186.0 5.7 %broadcast_select_fusion.1 = (bf16[272,2,512]{2,1,0:T(2,128)(2,1)S(1)}, bf16[272,2,512]{2,1,0:T(2,128)(2,1)S(1)}) fusion(pred[272]{0:T(512)(128)(4,1)S(1)} %copy-done.10, bf16[272,2,512]{2,1,0:T(2,128)(2,1)S(1)} %gather_fusion.2, pred[272]{0:T(512)(128)(4,1)S(1)} %copy-done.12, bf16[2,272,2,512]{3,2,1,0:T(2,128)(2,1)} %param.12, ...), kind=kLoop, calls=%fused_computation.25 | loop fusion | flops 1114112 | bytes 3343424 | tf_op jit(solution)/shard_map/jit(_where)/select_n | solution.py:144
  213.5 3.2 collective-permute-done.13
  221.7 4.3 %collective-permute-start.15 = (bf16[192,528]{1,0:T(8,128)(2,1)S(1)}, bf16[192,528]{1,0:T(8,128)(2,1)S(1)}, u32[]{:S(2)}, u32[]{:S(2)}) collective-permute-start(bf16[192,528]{1,0:T(8,128)(2,1)S(1)} %pad_maximum_fusion.4), channel_id=1, source_target_pairs={{0,1},{1,0},{2,3},{3,2},{4,5},{5,4},{6,7},{7,6},{8,9},{9,8},{10,11... | collective-permute-start | bytes 608264 | tf_op jit(solution)/shard_map/ppermute | solution.py:25
  226.4 11.0 %collective-permute-done.15 = bf16[192,528]{1,0:T(8,128)(2,1)S(1)} collective-permute-done((bf16[192,528]{1,0:T(8,128)(2,1)S(1)}, bf16[192,528]{1,0:T(8,128)(2,1)S(1)}, u32[]{:S(2)}, u32[]{:S(2)}) %collective-permute-start.15) | collective-permute-done | bytes 202784 | tf_op jit(solution)/shard_map/ppermute | solution.py:25
  253.6 73.2 %collective-permute-start.25 = (bf16[96,512]{1,0:T(8,128)(2,1)S(1)}, bf16[96,512]{1,0:T(8,128)(2,1)S(1)}, u32[]{:S(2)}, u32[]{:S(2)}) collective-permute-start(bf16[96,512]{1,0:T(8,128)(2,1)S(1)} %get-tuple-element.27), channel_id=1, source_target_pairs={{0,56},{8,0},{16,8},{24,16},{32,24},{40,32},{48,40},{56,48},{1,57}... | collective-permute-start | bytes 294920 | tf_op jit(solution)/shard_map/ppermute | solution.py:25
  330.6 6.4 %collective-permute-start.22 = (bf16[96,512]{1,0:T(8,128)(2,1)S(1)}, bf16[96,512]{1,0:T(8,128)(2,1)S(1)}, u32[]{:S(2)}, u32[]{:S(2)}) collective-permute-start(bf16[96,512]{1,0:T(8,128)(2,1)S(1)} %get-tuple-element.30), channel_id=1, source_target_pairs={{0,32},{8,40},{16,48},{24,56},{32,0},{40,8},{48,16},{56,24},{1,33}... | collective-permute-start | bytes 294920 | tf_op jit(solution)/shard_map/ppermute | solution.py:25
  339.0 4.3 %collective-permute-start.20 = (bf16[96,512]{1,0:T(8,128)(2,1)S(1)}, bf16[96,512]{1,0:T(8,128)(2,1)S(1)}, u32[]{:S(2)}, u32[]{:S(2)}) collective-permute-start(bf16[96,512]{1,0:T(8,128)(2,1)S(1)} %get-tuple-element.32), channel_id=1, source_target_pairs={{0,16},{8,24},{16,32},{24,40},{32,48},{40,56},{48,0},{56,8},{1,17}... | collective-permute-start | bytes 294920 | tf_op jit(solution)/shard_map/ppermute | solution.py:25
  349.0 12.7 %collective-permute-done.22 = bf16[96,512]{1,0:T(8,128)(2,1)S(1)} collective-permute-done((bf16[96,512]{1,0:T(8,128)(2,1)S(1)}, bf16[96,512]{1,0:T(8,128)(2,1)S(1)}, u32[]{:S(2)}, u32[]{:S(2)}) %collective-permute-start.22) | collective-permute-done | bytes 98336 | tf_op jit(solution)/shard_map/ppermute | solution.py:25
  (167 shorter events, 103.1 us)
Async XLA Ops:
  1.8 17.2 %collective-permute-start = (f32[2,96]{1,0:T(2,128)S(1)}, f32[2,96]{1,0:T(2,128)S(1)}, u32[]{:S(2)}, u32[]{:S(2)}) collective-permute-start(f32[2,96]{1,0:T(2,128)S(1)} %pad_maximum_fusion.7), channel_id=1, source_target_pairs={{0,1},{1,0},{2,3},{3,2},{4,5},{5,4},{6,7},{7,6},{8,9},{9,8},{10,11... | collective-permute-start | bytes 2312 | tf_op jit(solution)/shard_map/ppermute | solution.py:25
  19.0 11.2 %collective-permute-start.3 = (f32[2,96]{1,0:T(2,128)S(1)}, f32[2,96]{1,0:T(2,128)S(1)}, u32[]{:S(2)}, u32[]{:S(2)}) collective-permute-start(f32[2,96]{1,0:T(2,128)S(1)} %fusion.53), channel_id=1, source_target_pairs={{0,6},{2,0},{4,2},{6,4},{1,7},{3,1},{5,3},{7,5},{8,14},{10,8},{12,... | collective-permute-start | bytes 2312 | tf_op jit(solution)/shard_map/ppermute | solution.py:25
  32.5 22.8 %collective-permute-start.4 = (bf16[96,512]{1,0:T(8,128)(2,1)S(1)}, bf16[96,512]{1,0:T(8,128)(2,1)S(1)}, u32[]{:S(2)}, u32[]{:S(2)}) collective-permute-start(bf16[96,512]{1,0:T(8,128)(2,1)S(1)} %get-tuple-element.14), channel_id=1, source_target_pairs={{0,8},{8,16},{16,24},{24,32},{32,40},{40,48},{48,56},{56,0},{1,9},... | collective-permute-start | bytes 294920 | tf_op jit(solution)/shard_map/ppermute | solution.py:25
  35.2 25.1 %collective-permute-start.5 = (bf16[96,512]{1,0:T(8,128)(2,1)S(1)}, bf16[96,512]{1,0:T(8,128)(2,1)S(1)}, u32[]{:S(2)}, u32[]{:S(2)}) collective-permute-start(bf16[96,512]{1,0:T(8,128)(2,1)S(1)} %get-tuple-element.14), channel_id=1, source_target_pairs={{0,16},{8,24},{16,32},{24,40},{32,48},{40,56},{48,0},{56,8},{1,17}... | collective-permute-start | bytes 294920 | tf_op jit(solution)/shard_map/ppermute | solution.py:25
  38.3 25.3 %collective-permute-start.6 = (bf16[96,512]{1,0:T(8,128)(2,1)S(1)}, bf16[96,512]{1,0:T(8,128)(2,1)S(1)}, u32[]{:S(2)}, u32[]{:S(2)}) collective-permute-start(bf16[96,512]{1,0:T(8,128)(2,1)S(1)} %get-tuple-element.14), channel_id=1, source_target_pairs={{0,24},{8,32},{16,40},{24,48},{32,56},{40,0},{48,8},{56,16},{1,25}... | collective-permute-start | bytes 294920 | tf_op jit(solution)/shard_map/ppermute | solution.py:25
  44.8 19.7 %collective-permute-start.7 = (bf16[96,512]{1,0:T(8,128)(2,1)S(1)}, bf16[96,512]{1,0:T(8,128)(2,1)S(1)}, u32[]{:S(2)}, u32[]{:S(2)}) collective-permute-start(bf16[96,512]{1,0:T(8,128)(2,1)S(1)} %get-tuple-element.14), channel_id=1, source_target_pairs={{0,32},{8,40},{16,48},{24,56},{32,0},{40,8},{48,16},{56,24},{1,33}... | collective-permute-start | bytes 294920 | tf_op jit(solution)/shard_map/ppermute | solution.py:25
  48.9 16.3 %collective-permute-start.8 = (bf16[96,512]{1,0:T(8,128)(2,1)S(1)}, bf16[96,512]{1,0:T(8,128)(2,1)S(1)}, u32[]{:S(2)}, u32[]{:S(2)}) collective-permute-start(bf16[96,512]{1,0:T(8,128)(2,1)S(1)} %get-tuple-element.14), channel_id=1, source_target_pairs={{0,40},{8,48},{16,56},{24,0},{32,8},{40,16},{48,24},{56,32},{1,41}... | collective-permute-start | bytes 294920 | tf_op jit(solution)/shard_map/ppermute | solution.py:25
  55.4 10.8 %collective-permute-start.9 = (bf16[96,512]{1,0:T(8,128)(2,1)S(1)}, bf16[96,512]{1,0:T(8,128)(2,1)S(1)}, u32[]{:S(2)}, u32[]{:S(2)}) collective-permute-start(bf16[96,512]{1,0:T(8,128)(2,1)S(1)} %get-tuple-element.14), channel_id=1, source_target_pairs={{0,48},{8,56},{16,0},{24,8},{32,16},{40,24},{48,32},{56,40},{1,49}... | collective-permute-start | bytes 294920 | tf_op jit(solution)/shard_map/ppermute | solution.py:25
  102.9 24.2 %collective-permute-start.11 = (bf16[192,1536]{1,0:T(8,128)(2,1)S(1)}, bf16[192,1536]{1,0:T(8,128)(2,1)S(1)}, u32[]{:S(2)}, u32[]{:S(2)}) collective-permute-start(bf16[192,1536]{1,0:T(8,128)(2,1)S(1)} %reduce_sum.50), channel_id=1, source_target_pairs={{0,1},{1,0},{2,3},{3,2},{4,5},{5,4},{6,7},{7,6},{8,9},{9,8},{10,11... | collective-permute-start | bytes 1769480 | tf_op jit(solution)/shard_map/ppermute | solution.py:25
  128.8 27.7 %all-to-all-start.1 = ((bf16[4,192,1536]{2,1,0:T(8,128)(2,1)}), bf16[4,192,1536]{2,1,0:T(8,128)(2,1)S(1)}, u32[]{:S(2)}, u32[]{:S(2)}) async-start(bf16[4,192,1536]{2,1,0:T(8,128)(2,1)} %broadcast_in_dim.124), calls=%async_computation.1 | async-start | bytes 4718592 | tf_op jit(solution)/shard_map/all_to_all | solution.py:118
  205.3 8.0 %collective-permute-start.14 = (bf16[192,528]{1,0:T(8,128)(2,1)}, bf16[192,528]{1,0:T(8,128)(2,1)S(1)}, u32[]{:S(2)}, u32[]{:S(2)}) collective-permute-start(bf16[192,528]{1,0:T(8,128)(2,1)} %get-tuple-element.24), channel_id=1, source_target_pairs={{0,6},{2,0},{4,2},{6,4},{1,7},{3,1},{5,3},{7,5},{8,14},{10,8},{12,... | collective-permute-start | bytes 608264 | tf_op jit(solution)/shard_map/ppermute | solution.py:25
  208.2 8.4 %collective-permute-start.13 = (bf16[192,528]{1,0:T(8,128)(2,1)S(1)}, bf16[192,528]{1,0:T(8,128)(2,1)S(1)}, u32[]{:S(2)}, u32[]{:S(2)}) collective-permute-start(bf16[192,528]{1,0:T(8,128)(2,1)S(1)} %get-tuple-element.25), channel_id=1, source_target_pairs={{0,4},{2,6},{4,0},{6,2},{1,5},{3,7},{5,1},{7,3},{8,12},{10,14},{12... | collective-permute-start | bytes 608264 | tf_op jit(solution)/shard_map/ppermute | solution.py:25
  211.3 8.2 %collective-permute-start.12 = (bf16[192,528]{1,0:T(8,128)(2,1)S(1)}, bf16[192,528]{1,0:T(8,128)(2,1)S(1)}, u32[]{:S(2)}, u32[]{:S(2)}) collective-permute-start(bf16[192,528]{1,0:T(8,128)(2,1)S(1)} %get-tuple-element.23), channel_id=1, source_target_pairs={{0,2},{2,4},{4,6},{6,0},{1,3},{3,5},{5,7},{7,1},{8,10},{10,12},{12... | collective-permute-start | bytes 608264 | tf_op jit(solution)/shard_map/ppermute | solution.py:25
  221.7 15.7 %collective-permute-start.15 = (bf16[192,528]{1,0:T(8,128)(2,1)S(1)}, bf16[192,528]{1,0:T(8,128)(2,1)S(1)}, u32[]{:S(2)}, u32[]{:S(2)}) collective-permute-start(bf16[192,528]{1,0:T(8,128)(2,1)S(1)} %pad_maximum_fusion.4), channel_id=1, source_target_pairs={{0,1},{1,0},{2,3},{3,2},{4,5},{5,4},{6,7},{7,6},{8,9},{9,8},{10,11... | collective-permute-start | bytes 608264 | tf_op jit(solution)/shard_map/ppermute | solution.py:25
  238.7 8.2 %collective-permute-start.18 = (bf16[192,512]{1,0:T(8,128)(2,1)S(1)}, bf16[192,512]{1,0:T(8,128)(2,1)S(1)}, u32[]{:S(2)}, u32[]{:S(2)}) collective-permute-start(bf16[192,512]{1,0:T(8,128)(2,1)S(1)} %fusion.24), channel_id=1, source_target_pairs={{0,6},{2,0},{4,2},{6,4},{1,7},{3,1},{5,3},{7,5},{8,14},{10,8},{12,... | collective-permute-start | bytes 589832 | tf_op jit(solution)/shard_map/ppermute | solution.py:25
  241.5 7.9 %collective-permute-start.17 = (bf16[192,512]{1,0:T(8,128)(2,1)S(1)}, bf16[192,512]{1,0:T(8,128)(2,1)S(1)}, u32[]{:S(2)}, u32[]{:S(2)}) collective-permute-start(bf16[192,512]{1,0:T(8,128)(2,1)S(1)} %fusion.24), channel_id=1, source_target_pairs={{0,4},{2,6},{4,0},{6,2},{1,5},{3,7},{5,1},{7,3},{8,12},{10,14},{12... | collective-permute-start | bytes 589832 | tf_op jit(solution)/shard_map/ppermute | solution.py:25
  244.4 7.6 %collective-permute-start.16 = (bf16[192,512]{1,0:T(8,128)(2,1)S(1)}, bf16[192,512]{1,0:T(8,128)(2,1)S(1)}, u32[]{:S(2)}, u32[]{:S(2)}) collective-permute-start(bf16[192,512]{1,0:T(8,128)(2,1)S(1)} %fusion.24), channel_id=1, source_target_pairs={{0,2},{2,4},{4,6},{6,0},{1,3},{3,5},{5,7},{7,1},{8,10},{10,12},{12... | collective-permute-start | bytes 589832 | tf_op jit(solution)/shard_map/ppermute | solution.py:25
  253.6 85.4 %collective-permute-start.25 = (bf16[96,512]{1,0:T(8,128)(2,1)S(1)}, bf16[96,512]{1,0:T(8,128)(2,1)S(1)}, u32[]{:S(2)}, u32[]{:S(2)}) collective-permute-start(bf16[96,512]{1,0:T(8,128)(2,1)S(1)} %get-tuple-element.27), channel_id=1, source_target_pairs={{0,56},{8,0},{16,8},{24,16},{32,24},{40,32},{48,40},{56,48},{1,57}... | collective-permute-start | bytes 294920 | tf_op jit(solution)/shard_map/ppermute | solution.py:25
  326.8 16.4 %collective-permute-start.24 = (bf16[96,512]{1,0:T(8,128)(2,1)S(1)}, bf16[96,512]{1,0:T(8,128)(2,1)S(1)}, u32[]{:S(2)}, u32[]{:S(2)}) collective-permute-start(bf16[96,512]{1,0:T(8,128)(2,1)S(1)} %get-tuple-element.28), channel_id=1, source_target_pairs={{0,48},{8,56},{16,0},{24,8},{32,16},{40,24},{48,32},{56,40},{1,49}... | collective-permute-start | bytes 294920 | tf_op jit(solution)/shard_map/ppermute | solution.py:25
  328.7 20.2 %collective-permute-start.23 = (bf16[96,512]{1,0:T(8,128)(2,1)S(1)}, bf16[96,512]{1,0:T(8,128)(2,1)S(1)}, u32[]{:S(2)}, u32[]{:S(2)}) collective-permute-start(bf16[96,512]{1,0:T(8,128)(2,1)S(1)} %get-tuple-element.29), channel_id=1, source_target_pairs={{0,40},{8,48},{16,56},{24,0},{32,8},{40,16},{48,24},{56,32},{1,41}... | collective-permute-start | bytes 294920 | tf_op jit(solution)/shard_map/ppermute | solution.py:25
  330.6 31.0 %collective-permute-start.22 = (bf16[96,512]{1,0:T(8,128)(2,1)S(1)}, bf16[96,512]{1,0:T(8,128)(2,1)S(1)}, u32[]{:S(2)}, u32[]{:S(2)}) collective-permute-start(bf16[96,512]{1,0:T(8,128)(2,1)S(1)} %get-tuple-element.30), channel_id=1, source_target_pairs={{0,32},{8,40},{16,48},{24,56},{32,0},{40,8},{48,16},{56,24},{1,33}... | collective-permute-start | bytes 294920 | tf_op jit(solution)/shard_map/ppermute | solution.py:25
  337.0 24.6 %collective-permute-start.21 = (bf16[96,512]{1,0:T(8,128)(2,1)S(1)}, bf16[96,512]{1,0:T(8,128)(2,1)S(1)}, u32[]{:S(2)}, u32[]{:S(2)}) collective-permute-start(bf16[96,512]{1,0:T(8,128)(2,1)S(1)} %get-tuple-element.31), channel_id=1, source_target_pairs={{0,24},{8,32},{16,40},{24,48},{32,56},{40,0},{48,8},{56,16},{1,25}... | collective-permute-start | bytes 294920 | tf_op jit(solution)/shard_map/ppermute | solution.py:25
  339.0 22.7 %collective-permute-start.20 = (bf16[96,512]{1,0:T(8,128)(2,1)S(1)}, bf16[96,512]{1,0:T(8,128)(2,1)S(1)}, u32[]{:S(2)}, u32[]{:S(2)}) collective-permute-start(bf16[96,512]{1,0:T(8,128)(2,1)S(1)} %get-tuple-element.32), channel_id=1, source_target_pairs={{0,16},{8,24},{16,32},{24,40},{32,48},{40,56},{48,0},{56,8},{1,17}... | collective-permute-start | bytes 294920 | tf_op jit(solution)/shard_map/ppermute | solution.py:25
  343.2 18.4 %collective-permute-start.19 = (bf16[96,512]{1,0:T(8,128)(2,1)S(1)}, bf16[96,512]{1,0:T(8,128)(2,1)S(1)}, u32[]{:S(2)}, u32[]{:S(2)}) collective-permute-start(bf16[96,512]{1,0:T(8,128)(2,1)S(1)} %get-tuple-element.26), channel_id=1, source_target_pairs={{0,8},{8,16},{16,24},{24,32},{32,40},{40,48},{48,56},{56,0},{1,9},... | collective-permute-start | bytes 294920 | tf_op jit(solution)/shard_map/ppermute | solution.py:25
  (18 other events, 494.5 us)

commit v5 on v4

--- a/solution.py
+++ b/solution.py
@@ -51,6 +51,18 @@
     order = (me - jnp.arange(n, dtype=jnp.int32)) % n
     taken = jnp.take(stacked, order, axis=0)
     return taken.reshape((n * x.shape[0],) + x.shape[1:])
+
+
+def exchange_scatter_sum(x, axis):
+    n = lax.axis_size(axis)
+    split = x.reshape((n, x.shape[0] // n) + x.shape[1:])
+    return jnp.sum(lax.all_to_all(split, axis, 0, 0).astype(jnp.float32), axis=0)
+
+
+def exchange_gather(x, axis):
+    n = lax.axis_size(axis)
+    copies = jnp.broadcast_to(x[None], (n,) + x.shape)
+    return lax.all_to_all(copies, axis, 0, 0).reshape((n * x.shape[0],) + x.shape[1:])
 
 
 def split3(x):
@@ -85,37 +97,25 @@
     me = lax.axis_index("gyy")
     rows = packed.shape[0] // n
     packed = jnp.concatenate([packed, split3(tops)], axis=1)
-    parts = []
-    for step in range(n):
-        block = lax.dynamic_slice_in_dim(packed, ((me + step) % n) * rows, rows)
-        parts.append(block if step == 0 else shift(block, "gyy", step))
-    total, top = merge(parts, heads)
+    split = packed.reshape((n, rows) + packed.shape[1:])
+    received = lax.all_to_all(split, "gyy", 0, 0)
+    total, top = merge([received[j] for j in range(n)], heads)
     own = jnp.concatenate([total.astype(packed.dtype), split3(top)], axis=1)
     total, _ = merge([own, shift(own, "gyz", 1)], heads)
     width = total.shape[1] - heads
     sums = total[:, :width].reshape(rows, heads, width // heads)
     attn = (sums / total[:, width:, None]).astype(packed.dtype).reshape(rows, width)
-    return ring_gather(attn, "gyy")
+    return exchange_gather(attn, "gyy")
 
 
 def gy_sum(x):
-    return swap_combine(swap_combine(x, "gyz", jnp.add), "gyy", jnp.add)
+    n = lax.axis_size("gyy") * lax.axis_size("gyz")
+    copies = jnp.broadcast_to(x[None], (n,) + x.shape)
+    return jnp.sum(lax.all_to_all(copies, GY, 0, 0), axis=0)
 
 
 def gy_max(x):
     return swap_combine(swap_combine(x, "gyz", jnp.maximum), "gyy", jnp.maximum)
-
-
-def exchange_scatter_sum(x, axis):
-    n = lax.axis_size(axis)
-    split = x.reshape((n, x.shape[0] // n) + x.shape[1:])
-    return jnp.sum(lax.all_to_all(split, axis, 0, 0).astype(jnp.float32), axis=0)
-
-
-def exchange_gather(x, axis):
-    n = lax.axis_size(axis)
-    copies = jnp.broadcast_to(x[None], (n,) + x.shape)
-    return lax.all_to_all(copies, axis, 0, 0).reshape((n * x.shape[0],) + x.shape[1:])
 
 
 def gy_sum_rows(x):
@@ -156,7 +156,7 @@
     head_size = w_qkv.shape[2] // 3
     weight_flat = w_qkv.reshape(w_qkv.shape[0], local_heads * 3 * head_size)
     partial_value = jnp.dot(
-        ring_gather(normed, "gx"),
+        exchange_gather(normed, "gx"),
         weight_flat,
         preferred_element_type=jnp.float32,
     )
@@ -209,7 +209,7 @@
         axis=1,
     )
     attn = attend_combine(packed, tops.reshape(rows, local_heads), local_heads)
-    projected = ring_scatter_sum(
+    projected = exchange_scatter_sum(
         jnp.dot(attn, w_out, preferred_element_type=jnp.float32).astype(jnp.bfloat16), "gx"
     )
     mixed = (projected + hidden_f).astype(jnp.bfloat16)

time: 364 us -> 361 us (level)
  the two profiles are of different devices: /device:TPU:1 before, /device:TPU:6 now
where the time goes in v5:
time: 361 us; the launch traced here: 360 us
  waiting for transfers between devices  120 us (33%)
  starting transfers between devices  78.5 us (22%)
  blocking collectives  77.9 us (22%)
  local copies, waits for them, and re-layouts  43.8 us (12%)
  other arithmetic  30.6 us (8%)
  matrix products  7.58 us (2%)
    all_to_all x1, starting transfers between devices, exchange_scatter_sum(): lax.all_to_all(split, axis, 0, 0).astype(jnp.float32)  64.7 us
    all_to_all x2, waiting for transfers between devices, exchange_gather(): lax.all_to_all(copies, axis, 0, 0).reshape((n * x.shape[0],) + x.shape[1:])  45.7 us
    ppermute x2, waiting for transfers between devices, shift(): return lax.ppermute(x, axis, [(i, (i + step) % n) for i in range(n)])  39.3 us
    all_to_all x1, waiting for transfers between devices, exchange_scatter_sum(): lax.all_to_all(split, axis, 0, 0).astype(jnp.float32)  35.5 us
    all_to_all x1, blocking collectives, gy_sum(): return jnp.sum(lax.all_to_all(copies, GY, 0, 0), axis=0)  32.4 us
    all_to_all x1, blocking collectives, exchange_scatter_sum(): lax.all_to_all(split, axis, 0, 0).astype(jnp.float32)  20.4 us
    all_to_all x1, blocking collectives, attend_combine(): received = lax.all_to_all(split, 'gyy', 0, 0)  12.9 us
    all_to_all x1, blocking collectives, exchange_gather(): lax.all_to_all(copies, axis, 0, 0).reshape((n * x.shape[0],) + x.shape[1:])  12.1 us
  transfers between devices with their start and end apart: 5, of which 5 were waited for; matrix products, arithmetic and copies ran while one was open for 4% of the time, Pallas kernels for 0%

profile of v5, /device:TPU:6, one launch (start us, length us, event | category | flops | bytes accessed | tf_op | source)
XLA Modules:
  0.0 360.0 jit_solution(1123093246693661720)
XLA Ops:
  1.9 32.4 %all_to_all.35 = f32[8,2,96]{2,1,0:T(2,128)S(1)} all-to-all(f32[8,2,96]{2,1,0:T(2,128)S(1)} %broadcast_in_dim.112), channel_id=1, replica_groups=mesh['req'=8,'gx'=8,'gyy'=4,'gyz'=2] {'gyy','gyz'}, dimensions={0} | all-to-all | bytes 12288 | tf_op jit(solution)/shard_map/all_to_all | solution.py:114
  36.3 5.0 %all-to-all-start.1 = ((bf16[8,96,512]{2,1,0:T(8,128)(2,1)}), bf16[8,96,512]{2,1,0:T(8,128)(2,1)S(1)}, u32[]{:S(2)}, u32[]{:S(2)}) async-start(bf16[8,96,512]{2,1,0:T(8,128)(2,1)} %broadcast_in_dim.113), calls=%async_computation.1 | async-start | bytes 1572864 | tf_op jit(solution)/shard_map/all_to_all | solution.py:65
  42.7 37.1 %all-to-all-done.1 = bf16[8,96,512]{2,1,0:T(8,128)(2,1)S(1)} async-done(((bf16[8,96,512]{2,1,0:T(8,128)(2,1)}), bf16[8,96,512]{2,1,0:T(8,128)(2,1)S(1)}, u32[]{:S(2)}, u32[]{:S(2)}) %all-to-all-start.1) | async-done | bytes 786464 | tf_op jit(solution)/shard_map/all_to_all | solution.py:65
  79.9 2.8 convolution_convert_fusion
  82.7 20.4 %all_to_all.36 = bf16[4,192,1536]{2,1,0:T(8,128)(2,1)S(1)} all-to-all(bf16[4,192,1536]{2,1,0:T(8,128)(2,1)S(1)} %bitcast.148), channel_id=1, replica_groups=mesh['req'=8,'gx'=8,'gyy'=4,'gyz'=2] {'gyy'}, dimensions={0} | all-to-all | bytes 4718592 | tf_op jit(solution)/shard_map/all_to_all | solution.py:59
  103.7 2.8 collective-permute-start
  106.5 24.8 %collective-permute-done = bf16[192,1536]{1,0:T(8,128)(2,1)S(1)} collective-permute-done((bf16[192,1536]{1,0:T(8,128)(2,1)S(1)}, bf16[192,1536]{1,0:T(8,128)(2,1)S(1)}, u32[]{:S(2)}, u32[]{:S(2)}) %collective-permute-start) | collective-permute-done | bytes 589856 | tf_op jit(solution)/shard_map/ppermute | solution.py:25
  133.0 3.8 %all-to-all-start.3 = ((bf16[4,192,1536]{2,1,0:T(8,128)(2,1)}), bf16[4,192,1536]{2,1,0:T(8,128)(2,1)S(1)}, u32[]{:S(2)}, u32[]{:S(2)}) async-start(bf16[4,192,1536]{2,1,0:T(8,128)(2,1)} %broadcast_in_dim.114), calls=%async_computation.3 | async-start | bytes 4718592 | tf_op jit(solution)/shard_map/all_to_all | solution.py:65
  146.2 8.5 %all-to-all-done.3 = bf16[4,192,1536]{2,1,0:T(8,128)(2,1)S(1)} async-done(((bf16[4,192,1536]{2,1,0:T(8,128)(2,1)}), bf16[4,192,1536]{2,1,0:T(8,128)(2,1)S(1)}, u32[]{:S(2)}, u32[]{:S(2)}) %all-to-all-start.3) | async-done | bytes 2359328 | tf_op jit(solution)/shard_map/all_to_all | solution.py:65
  156.8 2.3 fusion.47
  162.3 3.5 copy.92
  167.1 4.8 %copy.91 = bf16[2,384,1,512]{3,2,1,0:T(2,128)(2,1)} copy(bf16[2,384,1,512]{1,3,0,2:T(8,128)(2,1)} %bitcast.147) | data formatting | bytes 1572864 | tf_op jit(solution)/shard_map/stack;reshape | solution.py:180
  171.8 5.4 %fusion.18 = (bf16[384,2,512]{2,1,0:T(2,128)(2,1)}, bf16[384,2,512]{2,1,0:T(2,128)(2,1)S(1)}) fusion(bf16[2,384,1,512]{3,2,1,0:T(2,128)(2,1)S(1)} %copy.92, bf16[2,384,1,512]{3,2,1,0:T(2,128)(2,1)} %copy.91), kind=kLoop, calls=%fused_computation.37 | loop fusion | flops 3145728 | bytes 3145728 | tf_op jit(solution)/shard_map/squeeze | solution.py:189
  177.3 3.0 gather_fusion
  180.3 3.9 %gather_fusion.1 = bf16[272,2,512]{2,1,0:T(2,128)(2,1)} fusion(bf16[384,2,512]{2,1,0:T(2,128)(2,1)S(1)} %get-tuple-element.14, s32[1024]{0:T(1024)S(1)} %pad_clamp_fusion), kind=kCustom, calls=%fused_computation.1.clone | custom fusion | bytes 1115200 | tf_op jit(solution)/shard_map/jit(_take)/gather | solution.py:143
  184.2 5.7 %broadcast_select_fusion.1 = (bf16[272,2,512]{2,1,0:T(2,128)(2,1)S(1)}, bf16[272,2,512]{2,1,0:T(2,128)(2,1)S(1)}) fusion(pred[272]{0:T(512)(128)(4,1)S(1)} %copy-done.17, bf16[272,2,512]{2,1,0:T(2,128)(2,1)S(1)} %gather_fusion, pred[272]{0:T(512)(128)(4,1)S(1)} %copy-done.19, bf16[2,272,2,512]{3,2,1,0:T(2,128)(2,1)} %param.12, ...), kind=kLoop, calls=%fused_computation.24 | loop fusion | flops 1114112 | bytes 3343424 | tf_op jit(solution)/shard_map/jit(_where)/select_n | solution.py:144
  189.9 3.0 slice_reduce_fusion.1
  192.9 3.0 slice_reduce_fusion.3
  209.1 12.9 %all_to_all.37 = bf16[4,192,528]{2,1,0:T(8,128)(2,1)S(1)} all-to-all(bf16[4,192,528]{2,1,0:T(8,128)(2,1)S(1)} %concatenate.29), channel_id=1, replica_groups=mesh['req'=8,'gx'=8,'gyy'=4,'gyz'=2] {'gyy'}, dimensions={0} | all-to-all | bytes 1622016 | tf_op jit(solution)/shard_map/all_to_all | solution.py:101
  227.0 14.5 %collective-permute-done.1 = bf16[192,528]{1,0:T(8,128)(2,1)S(1)} collective-permute-done((bf16[192,528]{1,0:T(8,128)(2,1)S(1)}, bf16[192,528]{1,0:T(8,128)(2,1)S(1)}, u32[]{:S(2)}, u32[]{:S(2)}) %collective-permute-start.1) | collective-permute-done | bytes 202784 | tf_op jit(solution)/shard_map/ppermute | solution.py:25
  242.9 12.1 %all_to_all.38 = bf16[4,192,512]{2,1,0:T(8,128)(2,1)S(1)} all-to-all(bf16[4,192,512]{2,1,0:T(8,128)(2,1)S(1)} %broadcast_in_dim.126), channel_id=1, replica_groups=mesh['req'=8,'gx'=8,'gyy'=4,'gyz'=2] {'gyy'}, dimensions={0} | all-to-all | bytes 1572864 | tf_op jit(solution)/shard_map/all_to_all | solution.py:65
  256.4 64.7 %all-to-all-start.6 = ((bf16[8,96,512]{2,1,0:T(8,128)(2,1)}), bf16[8,96,512]{2,1,0:T(8,128)(2,1)S(1)}, u32[]{:S(2)}, u32[]{:S(2)}) async-start(bf16[8,96,512]{2,1,0:T(8,128)(2,1)} %bitcast.30), calls=%async_computation.6 | async-start | bytes 1572864 | tf_op jit(solution)/shard_map/all_to_all | solution.py:59
  321.1 2.6 pad_maximum_fusion
  323.8 35.5 %all-to-all-done.6 = bf16[8,96,512]{2,1,0:T(8,128)(2,1)S(1)} async-done(((bf16[8,96,512]{2,1,0:T(8,128)(2,1)}), bf16[8,96,512]{2,1,0:T(8,128)(2,1)S(1)}, u32[]{:S(2)}, u32[]{:S(2)}) %all-to-all-start.6) | async-done | bytes 786464 | tf_op jit(solution)/shard_map/all_to_all | solution.py:59
  (125 shorter events, 44.3 us)
Async XLA Ops:
  0.6 254.3 %copy-start = (bf16[512,512]{1,0:T(8,128)(2,1)S(1)}, bf16[512,512]{1,0:T(8,128)(2,1)}, u32[]{:S(2)}) copy-start(bf16[512,512]{1,0:T(8,128)(2,1)} %param.11) | copy-start | bytes 1572868
  0.6 40.6 %copy-start.2 = (bf16[512,4,384]{2,1,0:T(4,128)(2,1)S(1)}, bf16[512,4,384]{2,1,0:T(4,128)(2,1)}, u32[]{:S(2)}) copy-start(bf16[512,4,384]{2,1,0:T(4,128)(2,1)} %param.10) | copy-start | bytes 4718596
  36.3 43.6 %all-to-all-start.1 = ((bf16[8,96,512]{2,1,0:T(8,128)(2,1)}), bf16[8,96,512]{2,1,0:T(8,128)(2,1)S(1)}, u32[]{:S(2)}, u32[]{:S(2)}) async-start(bf16[8,96,512]{2,1,0:T(8,128)(2,1)} %broadcast_in_dim.113), calls=%async_computation.1 | async-start | bytes 1572864 | tf_op jit(solution)/shard_map/all_to_all | solution.py:65
  103.7 27.6 %collective-permute-start = (bf16[192,1536]{1,0:T(8,128)(2,1)S(1)}, bf16[192,1536]{1,0:T(8,128)(2,1)S(1)}, u32[]{:S(2)}, u32[]{:S(2)}) collective-permute-start(bf16[192,1536]{1,0:T(8,128)(2,1)S(1)} %reduce_sum.69), channel_id=1, source_target_pairs={{0,1},{1,0},{2,3},{3,2},{4,5},{5,4},{6,7},{7,6},{8,9},{9,8},{10,11... | collective-permute-start | bytes 1769480 | tf_op jit(solution)/shard_map/ppermute | solution.py:25
  133.0 4.3 %copy-start.20 = (s32[2]{0:T(128)S(1)}, s32[2]{0:T(128)}, u32[]{:S(2)}) copy-start(s32[2]{0:T(128)} %param.13) | copy-start | bytes 28
  133.0 21.6 %all-to-all-start.3 = ((bf16[4,192,1536]{2,1,0:T(8,128)(2,1)}), bf16[4,192,1536]{2,1,0:T(8,128)(2,1)S(1)}, u32[]{:S(2)}, u32[]{:S(2)}) async-start(bf16[4,192,1536]{2,1,0:T(8,128)(2,1)} %broadcast_in_dim.114), calls=%async_computation.3 | async-start | bytes 4718592 | tf_op jit(solution)/shard_map/all_to_all | solution.py:65
  177.3 6.9 %copy-start.16 = (pred[272]{0:T(512)(128)(4,1)S(1)}, pred[272]{0:T(512)(128)(4,1)}, u32[]{:S(2)}) copy-start(pred[272]{0:T(512)(128)(4,1)} %get-tuple-element.49) | copy-start | bytes 820
  177.3 6.9 %copy-start.17 = (pred[272]{0:T(512)(128)(4,1)S(1)}, pred[272]{0:T(512)(128)(4,1)}, u32[]{:S(2)}) copy-start(pred[272]{0:T(512)(128)(4,1)} %get-tuple-element.50) | copy-start | bytes 820
  177.3 6.9 %copy-start.18 = (pred[272]{0:T(512)(128)(4,1)S(1)}, pred[272]{0:T(512)(128)(4,1)}, u32[]{:S(2)}) copy-start(pred[272]{0:T(512)(128)(4,1)} %get-tuple-element.47) | copy-start | bytes 820
  177.3 6.9 %copy-start.19 = (pred[272]{0:T(512)(128)(4,1)S(1)}, pred[272]{0:T(512)(128)(4,1)}, u32[]{:S(2)}) copy-start(pred[272]{0:T(512)(128)(4,1)} %get-tuple-element.48) | copy-start | bytes 820
  189.9 6.0 %copy-start.5 = (f32[384,272]{0,1:T(8,128)S(1)}, f32[384,272]{0,1:T(8,128)}, u32[]{:S(2)}) copy-start(f32[384,272]{0,1:T(8,128)} %get-tuple-element.38) | copy-start | bytes 1253380
  189.9 6.0 %copy-start.6 = (pred[384,272]{0,1:T(8,128)(4,1)S(1)}, pred[384,272]{0,1:T(8,128)(4,1)}, u32[]{:S(2)}) copy-start(pred[384,272]{0,1:T(8,128)(4,1)} %get-tuple-element.36) | copy-start | bytes 313348
  189.9 6.0 %copy-start.8 = (bf16[1,384,4,128]{3,2,1,0:T(4,128)(2,1)S(1)}, bf16[1,384,4,128]{3,2,1,0:T(4,128)(2,1)}, u32[]{:S(2)}) copy-start(bf16[1,384,4,128]{3,2,1,0:T(4,128)(2,1)} %get-tuple-element.16) | copy-start | bytes 1179652
  189.9 6.0 %copy-start.21 = (f32[4]{0:T(128)S(1)}, f32[4]{0:T(128)}, u32[]{:S(2)}) copy-start(f32[4]{0:T(128)} %multiply_exponential_fusion) | copy-start | bytes 52
  196.5 2.3 copy-start.12
  200.2 1.7 copy-start.10
  200.2 1.7 copy-start.13
  201.9 1.4 copy-start.1
  201.9 1.4 copy-start.15
  201.9 1.7 copy-start.9
  204.3 2.2 copy-start.11
  224.6 16.8 %collective-permute-start.1 = (bf16[192,528]{1,0:T(8,128)(2,1)S(1)}, bf16[192,528]{1,0:T(8,128)(2,1)S(1)}, u32[]{:S(2)}, u32[]{:S(2)}) collective-permute-start(bf16[192,528]{1,0:T(8,128)(2,1)S(1)} %pad_maximum_fusion.3), channel_id=1, source_target_pairs={{0,1},{1,0},{2,3},{3,2},{4,5},{5,4},{6,7},{7,6},{8,9},{9,8},{10,11... | collective-permute-start | bytes 608264 | tf_op jit(solution)/shard_map/ppermute | solution.py:25
  256.4 102.8 %all-to-all-start.6 = ((bf16[8,96,512]{2,1,0:T(8,128)(2,1)}), bf16[8,96,512]{2,1,0:T(8,128)(2,1)S(1)}, u32[]{:S(2)}, u32[]{:S(2)}) async-start(bf16[8,96,512]{2,1,0:T(8,128)(2,1)} %bitcast.30), calls=%async_computation.6 | async-start | bytes 1572864 | tf_op jit(solution)/shard_map/all_to_all | solution.py:59
  321.1 38.2 %copy-start.3 = (bf16[96,512]{1,0:T(8,128)(2,1)S(1)}, bf16[96,512]{1,0:T(8,128)(2,1)}, u32[]{:S(2)}) copy-start(bf16[96,512]{1,0:T(8,128)(2,1)} %param.8) | copy-start | bytes 294916
  (3 other events, 2.7 us)

commit v6 on v5

--- a/solution.py
+++ b/solution.py
@@ -156,7 +156,7 @@
     head_size = w_qkv.shape[2] // 3
     weight_flat = w_qkv.reshape(w_qkv.shape[0], local_heads * 3 * head_size)
     partial_value = jnp.dot(
-        exchange_gather(normed, "gx"),
+        ring_gather(normed, "gx"),
         weight_flat,
         preferred_element_type=jnp.float32,
     )
@@ -209,7 +209,7 @@
         axis=1,
     )
     attn = attend_combine(packed, tops.reshape(rows, local_heads), local_heads)
-    projected = exchange_scatter_sum(
+    projected = ring_scatter_sum(
         jnp.dot(attn, w_out, preferred_element_type=jnp.float32).astype(jnp.bfloat16), "gx"
     )
     mixed = (projected + hidden_f).astype(jnp.bfloat16)

time: 361 us -> 350 us (0.970)
  starting transfers between devices: 78.5 us -> 129 us
  blocking collectives: 77.9 us -> 41.8 us
  waiting for transfers between devices: 120 us -> 89.1 us
  local copies, waits for them, and re-layouts: 43.8 us -> 50.9 us
    ppermute x2 -> x16, starting transfers between devices: 5.01 us -> 104 us  [shift(): return lax.ppermute(x, axis, [(i, (i + step) % n) for i in range(n)])]
    all_to_all x1, starting transfers between devices: 64.7 us -> 17.7 us  [gy_sum(): return jnp.sum(lax.all_to_all(copies, GY, 0, 0), axis=0)]
    all_to_all x2 -> x0, blocking collectives: 44.5 us -> none  [the longest x1 32.4 us: gy_sum(): return jnp.sum(lax.all_to_all(copies, GY, 0, 0), axis=0)]
    all_to_all x2, waiting for transfers between devices: 45.7 us -> 22.1 us  [exchange_gather(): lax.all_to_all(copies, axis, 0, 0).reshape((n * x.shape[0],) + x.shape[1:])]
    all_to_all x1, waiting for transfers between devices: 35.5 us -> 13.2 us  [gy_sum(): return jnp.sum(lax.all_to_all(copies, GY, 0, 0), axis=0)]
    ppermute x2 -> x16, waiting for transfers between devices: 39.3 us -> 53.8 us  [shift(): return lax.ppermute(x, axis, [(i, (i + step) % n) for i in range(n)])]
    all_to_all x1, blocking collectives: 20.4 us -> 28.9 us  [exchange_scatter_sum(): lax.all_to_all(split, axis, 0, 0).astype(jnp.float32)]
    unnamed x51 -> x59, local copies, waits for them, and re-layouts: 3.08 us -> 7.22 us
  transfers between devices with their start and end apart: 5 -> 19, of which waited for: 5 -> 9; matrix products, arithmetic and copies ran while one was open for 4% -> 5% of each run, Pallas kernels for 0% -> 0%
where the time goes in v6:
time: 350 us; the launch traced here: 349 us
  starting transfers between devices  129 us (37%)
  waiting for transfers between devices  89.1 us (25%)
  local copies, waits for them, and re-layouts  50.9 us (15%)
  blocking collectives  41.8 us (12%)
  other arithmetic  30.5 us (9%)
  matrix products  5.31 us (2%)
    ppermute x16, starting transfers between devices, shift(): return lax.ppermute(x, axis, [(i, (i + step) % n) for i in range(n)])  104 us
    ppermute x16, waiting for transfers between devices, shift(): return lax.ppermute(x, axis, [(i, (i + step) % n) for i in range(n)])  53.8 us
    all_to_all x1, blocking collectives, exchange_scatter_sum(): lax.all_to_all(split, axis, 0, 0).astype(jnp.float32)  28.9 us
    all_to_all x2, waiting for transfers between devices, exchange_gather(): lax.all_to_all(copies, axis, 0, 0).reshape((n * x.shape[0],) + x.shape[1:])  22.1 us
    all_to_all x1, starting transfers between devices, gy_sum(): return jnp.sum(lax.all_to_all(copies, GY, 0, 0), axis=0)  17.7 us
    all_to_all x1, waiting for transfers between devices, gy_sum(): return jnp.sum(lax.all_to_all(copies, GY, 0, 0), axis=0)  13.2 us
    all_to_all x1, blocking collectives, attend_combine(): received = lax.all_to_all(split, 'gyy', 0, 0)  12.9 us
    another operation x2, local copies, waits for them, and re-layouts, shards(): jnp.stack([qkv[:, :, :, head_size:2 * head_size].reshape(requests, group,...  8.27 us
  transfers between devices with their start and end apart: 19, of which 9 were waited for; matrix products, arithmetic and copies ran while one was open for 5% of the time, Pallas kernels for 0%

profile of v6, /device:TPU:6, one launch (start us, length us, event | category | flops | bytes accessed | tf_op | source)
XLA Modules:
  0.0 348.5 jit_solution(7322052001526131118)
XLA Ops:
  2.4 17.7 %all-to-all-start = ((f32[8,2,96]{2,1,0:T(2,128)}), f32[8,2,96]{2,1,0:T(2,128)S(1)}, u32[]{:S(2)}, u32[]{:S(2)}) async-start(f32[8,2,96]{2,1,0:T(2,128)} %broadcast_in_dim.117), calls=%async_computation | async-start | bytes 16384 | tf_op jit(solution)/shard_map/all_to_all | solution.py:114
  21.8 13.2 %all-to-all-done = f32[8,2,96]{2,1,0:T(2,128)S(1)} async-done(((f32[8,2,96]{2,1,0:T(2,128)}), f32[8,2,96]{2,1,0:T(2,128)S(1)}, u32[]{:S(2)}, u32[]{:S(2)}) %all-to-all-start) | async-done | bytes 6176 | tf_op jit(solution)/shard_map/all_to_all | solution.py:114
  42.1 3.8 %collective-permute-start.2 = (bf16[96,512]{1,0:T(8,128)(2,1)S(1)}, bf16[96,512]{1,0:T(8,128)(2,1)S(1)}, u32[]{:S(2)}, u32[]{:S(2)}) collective-permute-start(bf16[96,512]{1,0:T(8,128)(2,1)S(1)} %get-tuple-element.14), channel_id=1, source_target_pairs={{0,24},{8,32},{16,40},{24,48},{32,56},{40,0},{48,8},{56,16},{1,25}... | collective-permute-start | bytes 294920 | tf_op jit(solution)/shard_map/ppermute | solution.py:25
  46.0 7.3 %collective-permute-start.3 = (bf16[96,512]{1,0:T(8,128)(2,1)S(1)}, bf16[96,512]{1,0:T(8,128)(2,1)S(1)}, u32[]{:S(2)}, u32[]{:S(2)}) collective-permute-start(bf16[96,512]{1,0:T(8,128)(2,1)S(1)} %get-tuple-element.14), channel_id=1, source_target_pairs={{0,32},{8,40},{16,48},{24,56},{32,0},{40,8},{48,16},{56,24},{1,33}... | collective-permute-start | bytes 294920 | tf_op jit(solution)/shard_map/ppermute | solution.py:25
  56.2 6.4 %collective-permute-start.5 = (bf16[96,512]{1,0:T(8,128)(2,1)S(1)}, bf16[96,512]{1,0:T(8,128)(2,1)S(1)}, u32[]{:S(2)}, u32[]{:S(2)}) collective-permute-start(bf16[96,512]{1,0:T(8,128)(2,1)S(1)} %get-tuple-element.14), channel_id=1, source_target_pairs={{0,48},{8,56},{16,0},{24,8},{32,16},{40,24},{48,32},{56,40},{1,49}... | collective-permute-start | bytes 294920 | tf_op jit(solution)/shard_map/ppermute | solution.py:25
  63.2 3.8 %collective-permute-start.6 = (bf16[96,512]{1,0:T(8,128)(2,1)S(1)}, bf16[96,512]{1,0:T(8,128)(2,1)S(1)}, u32[]{:S(2)}, u32[]{:S(2)}) collective-permute-start(bf16[96,512]{1,0:T(8,128)(2,1)S(1)} %get-tuple-element.14), channel_id=1, source_target_pairs={{0,56},{8,0},{16,8},{24,16},{32,24},{40,32},{48,40},{56,48},{1,57}... | collective-permute-start | bytes 294920 | tf_op jit(solution)/shard_map/ppermute | solution.py:25
  77.4 28.9 %all_to_all.25 = bf16[4,192,1536]{2,1,0:T(8,128)(2,1)S(1)} all-to-all(bf16[4,192,1536]{2,1,0:T(8,128)(2,1)S(1)} %bitcast.165), channel_id=1, replica_groups=mesh['req'=8,'gx'=8,'gyy'=4,'gyz'=2] {'gyy'}, dimensions={0} | all-to-all | bytes 4718592 | tf_op jit(solution)/shard_map/all_to_all | solution.py:59
  109.7 27.4 %collective-permute-done.7 = bf16[192,1536]{1,0:T(8,128)(2,1)S(1)} collective-permute-done((bf16[192,1536]{1,0:T(8,128)(2,1)S(1)}, bf16[192,1536]{1,0:T(8,128)(2,1)S(1)}, u32[]{:S(2)}, u32[]{:S(2)}) %collective-permute-start.7) | collective-permute-done | bytes 589856 | tf_op jit(solution)/shard_map/ppermute | solution.py:25
  138.8 3.8 %all-to-all-start.2 = ((bf16[4,192,1536]{2,1,0:T(8,128)(2,1)}), bf16[4,192,1536]{2,1,0:T(8,128)(2,1)S(1)}, u32[]{:S(2)}, u32[]{:S(2)}) async-start(bf16[4,192,1536]{2,1,0:T(8,128)(2,1)} %broadcast_in_dim.119), calls=%async_computation.2 | async-start | bytes 4718592 | tf_op jit(solution)/shard_map/all_to_all | solution.py:65
  152.0 12.8 %all-to-all-done.2 = bf16[4,192,1536]{2,1,0:T(8,128)(2,1)S(1)} async-done(((bf16[4,192,1536]{2,1,0:T(8,128)(2,1)}), bf16[4,192,1536]{2,1,0:T(8,128)(2,1)S(1)}, u32[]{:S(2)}, u32[]{:S(2)}) %all-to-all-start.2) | async-done | bytes 2359328 | tf_op jit(solution)/shard_map/all_to_all | solution.py:65
  172.4 3.5 %copy.92 = bf16[2,384,1,512]{3,2,1,0:T(2,128)(2,1)S(1)} copy(bf16[2,384,1,512]{1,3,0,2:T(8,128)(2,1)} %bitcast.163) | data formatting | bytes 1572864 | tf_op jit(solution)/shard_map/stack;reshape | solution.py:180
  177.2 4.8 %copy.91 = bf16[2,384,1,512]{3,2,1,0:T(2,128)(2,1)} copy(bf16[2,384,1,512]{1,3,0,2:T(8,128)(2,1)} %bitcast.164) | data formatting | bytes 1572864 | tf_op jit(solution)/shard_map/stack;reshape | solution.py:180
  181.9 5.4 %fusion.18 = (bf16[384,2,512]{2,1,0:T(2,128)(2,1)}, bf16[384,2,512]{2,1,0:T(2,128)(2,1)S(1)}) fusion(bf16[2,384,1,512]{3,2,1,0:T(2,128)(2,1)S(1)} %copy.92, bf16[2,384,1,512]{3,2,1,0:T(2,128)(2,1)} %copy.91), kind=kLoop, calls=%fused_computation.37 | loop fusion | flops 3145728 | bytes 3145728 | tf_op jit(solution)/shard_map/squeeze | solution.py:189
  190.4 3.9 %gather_fusion.2 = bf16[272,2,512]{2,1,0:T(2,128)(2,1)} fusion(bf16[384,2,512]{2,1,0:T(2,128)(2,1)S(1)} %get-tuple-element.16, s32[1024]{0:T(1024)S(1)} %pad_clamp_fusion), kind=kCustom, calls=%fused_computation.1.clone | custom fusion | bytes 1115200 | tf_op jit(solution)/shard_map/jit(_take)/gather | solution.py:143
  194.3 5.7 %broadcast_select_fusion.1 = (bf16[272,2,512]{2,1,0:T(2,128)(2,1)S(1)}, bf16[272,2,512]{2,1,0:T(2,128)(2,1)S(1)}) fusion(pred[272]{0:T(512)(128)(4,1)S(1)} %copy-done.18, bf16[272,2,512]{2,1,0:T(2,128)(2,1)S(1)} %gather_fusion.1, pred[272]{0:T(512)(128)(4,1)S(1)} %copy-done.20, bf16[2,272,2,512]{3,2,1,0:T(2,128)(2,1)} %param.12, ...), kind=kLoop, calls=%fused_computation.24 | loop fusion | flops 1114112 | bytes 3343424 | tf_op jit(solution)/shard_map/jit(_where)/select_n | solution.py:144
  219.2 12.9 %all_to_all.26 = bf16[4,192,528]{2,1,0:T(8,128)(2,1)S(1)} all-to-all(bf16[4,192,528]{2,1,0:T(8,128)(2,1)S(1)} %concatenate.29), channel_id=1, replica_groups=mesh['req'=8,'gx'=8,'gyy'=4,'gyz'=2] {'gyy'}, dimensions={0} | all-to-all | bytes 1622016 | tf_op jit(solution)/shard_map/all_to_all | solution.py:101
  236.8 14.7 %collective-permute-done.8 = bf16[192,528]{1,0:T(8,128)(2,1)S(1)} collective-permute-done((bf16[192,528]{1,0:T(8,128)(2,1)S(1)}, bf16[192,528]{1,0:T(8,128)(2,1)S(1)}, u32[]{:S(2)}, u32[]{:S(2)}) %collective-permute-start.8) | collective-permute-done | bytes 202784 | tf_op jit(solution)/shard_map/ppermute | solution.py:25
  257.4 9.3 %all-to-all-done.4 = bf16[4,192,512]{2,1,0:T(8,128)(2,1)S(1)} async-done(((bf16[4,192,512]{2,1,0:T(8,128)(2,1)}), bf16[4,192,512]{2,1,0:T(8,128)(2,1)S(1)}, u32[]{:S(2)}, u32[]{:S(2)}) %all-to-all-start.4) | async-done | bytes 786464 | tf_op jit(solution)/shard_map/all_to_all | solution.py:65
  267.4 27.8 %collective-permute-start.15 = (bf16[96,512]{1,0:T(8,128)(2,1)S(1)}, bf16[96,512]{1,0:T(8,128)(2,1)S(1)}, u32[]{:S(2)}, u32[]{:S(2)}) collective-permute-start(bf16[96,512]{1,0:T(8,128)(2,1)S(1)} %get-tuple-element.28), channel_id=1, source_target_pairs={{0,56},{8,0},{16,8},{24,16},{32,24},{40,32},{48,40},{56,48},{1,57}... | collective-permute-start | bytes 294920 | tf_op jit(solution)/shard_map/ppermute | solution.py:25
  295.2 10.5 %collective-permute-start.14 = (bf16[96,512]{1,0:T(8,128)(2,1)S(1)}, bf16[96,512]{1,0:T(8,128)(2,1)S(1)}, u32[]{:S(2)}, u32[]{:S(2)}) collective-permute-start(bf16[96,512]{1,0:T(8,128)(2,1)S(1)} %get-tuple-element.29), channel_id=1, source_target_pairs={{0,48},{8,56},{16,0},{24,8},{32,16},{40,24},{48,32},{56,40},{1,49}... | collective-permute-start | bytes 294920 | tf_op jit(solution)/shard_map/ppermute | solution.py:25
  305.8 15.1 %collective-permute-start.13 = (bf16[96,512]{1,0:T(8,128)(2,1)S(1)}, bf16[96,512]{1,0:T(8,128)(2,1)S(1)}, u32[]{:S(2)}, u32[]{:S(2)}) collective-permute-start(bf16[96,512]{1,0:T(8,128)(2,1)S(1)} %get-tuple-element.30), channel_id=1, source_target_pairs={{0,40},{8,48},{16,56},{24,0},{32,8},{40,16},{48,24},{56,32},{1,41}... | collective-permute-start | bytes 294920 | tf_op jit(solution)/shard_map/ppermute | solution.py:25
  322.9 4.8 %collective-permute-start.11 = (bf16[96,512]{1,0:T(8,128)(2,1)S(1)}, bf16[96,512]{1,0:T(8,128)(2,1)S(1)}, u32[]{:S(2)}, u32[]{:S(2)}) collective-permute-start(bf16[96,512]{1,0:T(8,128)(2,1)S(1)} %get-tuple-element.32), channel_id=1, source_target_pairs={{0,24},{8,32},{16,40},{24,48},{32,56},{40,0},{48,8},{56,16},{1,25}... | collective-permute-start | bytes 294920 | tf_op jit(solution)/shard_map/ppermute | solution.py:25
  327.7 6.9 %collective-permute-start.10 = (bf16[96,512]{1,0:T(8,128)(2,1)S(1)}, bf16[96,512]{1,0:T(8,128)(2,1)S(1)}, u32[]{:S(2)}, u32[]{:S(2)}) collective-permute-start(bf16[96,512]{1,0:T(8,128)(2,1)S(1)} %get-tuple-element.33), channel_id=1, source_target_pairs={{0,16},{8,24},{16,32},{24,40},{32,48},{40,56},{48,0},{56,8},{1,17}... | collective-permute-start | bytes 294920 | tf_op jit(solution)/shard_map/ppermute | solution.py:25
  339.2 7.0 %collective-permute-done.12 = bf16[96,512]{1,0:T(8,128)(2,1)S(1)} collective-permute-done((bf16[96,512]{1,0:T(8,128)(2,1)S(1)}, bf16[96,512]{1,0:T(8,128)(2,1)S(1)}, u32[]{:S(2)}, u32[]{:S(2)}) %collective-permute-start.12) | collective-permute-done | bytes 98336 | tf_op jit(solution)/shard_map/ppermute | solution.py:25
  (164 shorter events, 89.5 us)
Async XLA Ops:
  0.6 266.1 %copy-start = (bf16[512,512]{1,0:T(8,128)(2,1)S(1)}, bf16[512,512]{1,0:T(8,128)(2,1)}, u32[]{:S(2)}) copy-start(bf16[512,512]{1,0:T(8,128)(2,1)} %param.11) | copy-start | bytes 1572868
  0.6 34.4 %copy-start.2 = (bf16[96,512]{1,0:T(8,128)(2,1)S(1)}, bf16[96,512]{1,0:T(8,128)(2,1)}, u32[]{:S(2)}) copy-start(bf16[96,512]{1,0:T(8,128)(2,1)} %param.8) | copy-start | bytes 294916
  0.7 34.4 %copy-start.16 = (f32[512]{0:T(512)S(1)}, f32[512]{0:T(512)}, u32[]{:S(2)}) copy-start(f32[512]{0:T(512)} %param.9) | copy-start | bytes 6148
  2.4 32.6 %all-to-all-start = ((f32[8,2,96]{2,1,0:T(2,128)}), f32[8,2,96]{2,1,0:T(2,128)S(1)}, u32[]{:S(2)}, u32[]{:S(2)}) async-start(f32[8,2,96]{2,1,0:T(2,128)} %broadcast_in_dim.117), calls=%async_computation | async-start | bytes 16384 | tf_op jit(solution)/shard_map/all_to_all | solution.py:114
  35.8 20.4 %collective-permute-start = (bf16[96,512]{1,0:T(8,128)(2,1)S(1)}, bf16[96,512]{1,0:T(8,128)(2,1)S(1)}, u32[]{:S(2)}, u32[]{:S(2)}) collective-permute-start(bf16[96,512]{1,0:T(8,128)(2,1)S(1)} %get-tuple-element.14), channel_id=1, source_target_pairs={{0,8},{8,16},{16,24},{24,32},{32,40},{40,48},{48,56},{56,0},{1,9},... | collective-permute-start | bytes 294920 | tf_op jit(solution)/shard_map/ppermute | solution.py:25
  38.7 24.5 %collective-permute-start.1 = (bf16[96,512]{1,0:T(8,128)(2,1)S(1)}, bf16[96,512]{1,0:T(8,128)(2,1)S(1)}, u32[]{:S(2)}, u32[]{:S(2)}) collective-permute-start(bf16[96,512]{1,0:T(8,128)(2,1)S(1)} %get-tuple-element.14), channel_id=1, source_target_pairs={{0,16},{8,24},{16,32},{24,40},{32,48},{40,56},{48,0},{56,8},{1,17}... | collective-permute-start | bytes 294920 | tf_op jit(solution)/shard_map/ppermute | solution.py:25
  42.1 25.6 %collective-permute-start.2 = (bf16[96,512]{1,0:T(8,128)(2,1)S(1)}, bf16[96,512]{1,0:T(8,128)(2,1)S(1)}, u32[]{:S(2)}, u32[]{:S(2)}) collective-permute-start(bf16[96,512]{1,0:T(8,128)(2,1)S(1)} %get-tuple-element.14), channel_id=1, source_target_pairs={{0,24},{8,32},{16,40},{24,48},{32,56},{40,0},{48,8},{56,16},{1,25}... | collective-permute-start | bytes 294920 | tf_op jit(solution)/shard_map/ppermute | solution.py:25
  46.0 22.4 %collective-permute-start.3 = (bf16[96,512]{1,0:T(8,128)(2,1)S(1)}, bf16[96,512]{1,0:T(8,128)(2,1)S(1)}, u32[]{:S(2)}, u32[]{:S(2)}) collective-permute-start(bf16[96,512]{1,0:T(8,128)(2,1)S(1)} %get-tuple-element.14), channel_id=1, source_target_pairs={{0,32},{8,40},{16,48},{24,56},{32,0},{40,8},{48,16},{56,24},{1,33}... | collective-permute-start | bytes 294920 | tf_op jit(solution)/shard_map/ppermute | solution.py:25
  53.2 15.8 %collective-permute-start.4 = (bf16[96,512]{1,0:T(8,128)(2,1)S(1)}, bf16[96,512]{1,0:T(8,128)(2,1)S(1)}, u32[]{:S(2)}, u32[]{:S(2)}) collective-permute-start(bf16[96,512]{1,0:T(8,128)(2,1)S(1)} %get-tuple-element.14), channel_id=1, source_target_pairs={{0,40},{8,48},{16,56},{24,0},{32,8},{40,16},{48,24},{56,32},{1,41}... | collective-permute-start | bytes 294920 | tf_op jit(solution)/shard_map/ppermute | solution.py:25
  56.2 16.6 %collective-permute-start.5 = (bf16[96,512]{1,0:T(8,128)(2,1)S(1)}, bf16[96,512]{1,0:T(8,128)(2,1)S(1)}, u32[]{:S(2)}, u32[]{:S(2)}) collective-permute-start(bf16[96,512]{1,0:T(8,128)(2,1)S(1)} %get-tuple-element.14), channel_id=1, source_target_pairs={{0,48},{8,56},{16,0},{24,8},{32,16},{40,24},{48,32},{56,40},{1,49}... | collective-permute-start | bytes 294920 | tf_op jit(solution)/shard_map/ppermute | solution.py:25
  63.2 10.2 %collective-permute-start.6 = (bf16[96,512]{1,0:T(8,128)(2,1)S(1)}, bf16[96,512]{1,0:T(8,128)(2,1)S(1)}, u32[]{:S(2)}, u32[]{:S(2)}) collective-permute-start(bf16[96,512]{1,0:T(8,128)(2,1)S(1)} %get-tuple-element.14), channel_id=1, source_target_pairs={{0,56},{8,0},{16,8},{24,16},{32,24},{40,32},{48,40},{56,48},{1,57}... | collective-permute-start | bytes 294920 | tf_op jit(solution)/shard_map/ppermute | solution.py:25
  106.9 30.2 %collective-permute-start.7 = (bf16[192,1536]{1,0:T(8,128)(2,1)S(1)}, bf16[192,1536]{1,0:T(8,128)(2,1)S(1)}, u32[]{:S(2)}, u32[]{:S(2)}) collective-permute-start(bf16[192,1536]{1,0:T(8,128)(2,1)S(1)} %reduce_sum.60), channel_id=1, source_target_pairs={{0,1},{1,0},{2,3},{3,2},{4,5},{5,4},{6,7},{7,6},{8,9},{9,8},{10,11... | collective-permute-start | bytes 1769480 | tf_op jit(solution)/shard_map/ppermute | solution.py:25
  138.8 25.9 %all-to-all-start.2 = ((bf16[4,192,1536]{2,1,0:T(8,128)(2,1)}), bf16[4,192,1536]{2,1,0:T(8,128)(2,1)S(1)}, u32[]{:S(2)}, u32[]{:S(2)}) async-start(bf16[4,192,1536]{2,1,0:T(8,128)(2,1)} %broadcast_in_dim.119), calls=%async_computation.2 | async-start | bytes 4718592 | tf_op jit(solution)/shard_map/all_to_all | solution.py:65
  187.4 6.9 %copy-start.20 = (pred[272]{0:T(512)(128)(4,1)S(1)}, pred[272]{0:T(512)(128)(4,1)}, u32[]{:S(2)}) copy-start(pred[272]{0:T(512)(128)(4,1)} %get-tuple-element.57) | copy-start | bytes 820
  234.7 16.8 %collective-permute-start.8 = (bf16[192,528]{1,0:T(8,128)(2,1)S(1)}, bf16[192,528]{1,0:T(8,128)(2,1)S(1)}, u32[]{:S(2)}, u32[]{:S(2)}) collective-permute-start(bf16[192,528]{1,0:T(8,128)(2,1)S(1)} %pad_maximum_fusion.3), channel_id=1, source_target_pairs={{0,1},{1,0},{2,3},{3,2},{4,5},{5,4},{6,7},{7,6},{8,9},{9,8},{10,11... | collective-permute-start | bytes 608264 | tf_op jit(solution)/shard_map/ppermute | solution.py:25
  253.8 13.0 %all-to-all-start.4 = ((bf16[4,192,512]{2,1,0:T(8,128)(2,1)}), bf16[4,192,512]{2,1,0:T(8,128)(2,1)S(1)}, u32[]{:S(2)}, u32[]{:S(2)}) async-start(bf16[4,192,512]{2,1,0:T(8,128)(2,1)} %broadcast_in_dim.131), calls=%async_computation.4 | async-start | bytes 1572864 | tf_op jit(solution)/shard_map/all_to_all | solution.py:65
  267.3 80.4 %copy-start.3 = (bf16[96,512]{1,0:T(8,128)(2,1)S(1)}, bf16[96,512]{1,0:T(8,128)(2,1)}, u32[]{:S(2)}) copy-start(bf16[96,512]{1,0:T(8,128)(2,1)} %param.8) | copy-start | bytes 294916
  267.4 60.3 %collective-permute-start.15 = (bf16[96,512]{1,0:T(8,128)(2,1)S(1)}, bf16[96,512]{1,0:T(8,128)(2,1)S(1)}, u32[]{:S(2)}, u32[]{:S(2)}) collective-permute-start(bf16[96,512]{1,0:T(8,128)(2,1)S(1)} %get-tuple-element.28), channel_id=1, source_target_pairs={{0,56},{8,0},{16,8},{24,16},{32,24},{40,32},{48,40},{56,48},{1,57}... | collective-permute-start | bytes 294920 | tf_op jit(solution)/shard_map/ppermute | solution.py:25
  295.2 39.4 %collective-permute-start.14 = (bf16[96,512]{1,0:T(8,128)(2,1)S(1)}, bf16[96,512]{1,0:T(8,128)(2,1)S(1)}, u32[]{:S(2)}, u32[]{:S(2)}) collective-permute-start(bf16[96,512]{1,0:T(8,128)(2,1)S(1)} %get-tuple-element.29), channel_id=1, source_target_pairs={{0,48},{8,56},{16,0},{24,8},{32,16},{40,24},{48,32},{56,40},{1,49}... | collective-permute-start | bytes 294920 | tf_op jit(solution)/shard_map/ppermute | solution.py:25
  305.8 33.4 %collective-permute-start.13 = (bf16[96,512]{1,0:T(8,128)(2,1)S(1)}, bf16[96,512]{1,0:T(8,128)(2,1)S(1)}, u32[]{:S(2)}, u32[]{:S(2)}) collective-permute-start(bf16[96,512]{1,0:T(8,128)(2,1)S(1)} %get-tuple-element.30), channel_id=1, source_target_pairs={{0,40},{8,48},{16,56},{24,0},{32,8},{40,16},{48,24},{56,32},{1,41}... | collective-permute-start | bytes 294920 | tf_op jit(solution)/shard_map/ppermute | solution.py:25
  320.9 25.3 %collective-permute-start.12 = (bf16[96,512]{1,0:T(8,128)(2,1)S(1)}, bf16[96,512]{1,0:T(8,128)(2,1)S(1)}, u32[]{:S(2)}, u32[]{:S(2)}) collective-permute-start(bf16[96,512]{1,0:T(8,128)(2,1)S(1)} %get-tuple-element.31), channel_id=1, source_target_pairs={{0,32},{8,40},{16,48},{24,56},{32,0},{40,8},{48,16},{56,24},{1,33}... | collective-permute-start | bytes 294920 | tf_op jit(solution)/shard_map/ppermute | solution.py:25
  322.9 23.3 %collective-permute-start.11 = (bf16[96,512]{1,0:T(8,128)(2,1)S(1)}, bf16[96,512]{1,0:T(8,128)(2,1)S(1)}, u32[]{:S(2)}, u32[]{:S(2)}) collective-permute-start(bf16[96,512]{1,0:T(8,128)(2,1)S(1)} %get-tuple-element.32), channel_id=1, source_target_pairs={{0,24},{8,32},{16,40},{24,48},{32,56},{40,0},{48,8},{56,16},{1,25}... | collective-permute-start | bytes 294920 | tf_op jit(solution)/shard_map/ppermute | solution.py:25
  327.7 18.5 %collective-permute-start.10 = (bf16[96,512]{1,0:T(8,128)(2,1)S(1)}, bf16[96,512]{1,0:T(8,128)(2,1)S(1)}, u32[]{:S(2)}, u32[]{:S(2)}) collective-permute-start(bf16[96,512]{1,0:T(8,128)(2,1)S(1)} %get-tuple-element.33), channel_id=1, source_target_pairs={{0,16},{8,24},{16,32},{24,40},{32,48},{40,56},{48,0},{56,8},{1,17}... | collective-permute-start | bytes 294920 | tf_op jit(solution)/shard_map/ppermute | solution.py:25
  334.7 13.1 %collective-permute-start.9 = (bf16[96,512]{1,0:T(8,128)(2,1)S(1)}, bf16[96,512]{1,0:T(8,128)(2,1)S(1)}, u32[]{:S(2)}, u32[]{:S(2)}) collective-permute-start(bf16[96,512]{1,0:T(8,128)(2,1)S(1)} %get-tuple-element.27), channel_id=1, source_target_pairs={{0,8},{8,16},{16,24},{24,32},{32,40},{40,48},{48,56},{56,0},{1,9},... | collective-permute-start | bytes 294920 | tf_op jit(solution)/shard_map/ppermute | solution.py:25
  (18 other events, 64.3 us)

commit v7 on v6

--- a/solution.py
+++ b/solution.py
@@ -146,17 +146,19 @@
 
 def shards(hidden, ln_gain, w_qkv, w_out, kv_cache, cache_len):
     hidden_f = hidden.astype(jnp.float32)
-    sums = gy_sum(jnp.stack([jnp.sum(hidden_f, axis=1), jnp.sum(hidden_f * hidden_f, axis=1)]))
-    mean = sums[0] / D
-    var = sums[1] / D - mean * mean
+    gathered = ring_gather(hidden, "gx").astype(jnp.float32)
+    sums = gy_sum(jnp.stack([jnp.sum(hidden_f, axis=1), jnp.sum(hidden_f * hidden_f, axis=1)], axis=1))
+    sums = exchange_gather(sums, "gx")
+    mean = sums[:, 0] / D
+    var = sums[:, 1] / D - mean * mean
     normed = (
-        (hidden_f - mean[:, None]) * lax.rsqrt(var + norm_eps)[:, None] * ln_gain[None, :]
+        (gathered - mean[:, None]) * lax.rsqrt(var + norm_eps)[:, None] * ln_gain[None, :]
     ).astype(jnp.bfloat16)
     local_heads = w_qkv.shape[1]
     head_size = w_qkv.shape[2] // 3
     weight_flat = w_qkv.reshape(w_qkv.shape[0], local_heads * 3 * head_size)
     partial_value = jnp.dot(
-        ring_gather(normed, "gx"),
+        normed,
         weight_flat,
         preferred_element_type=jnp.float32,
     )

time: 350 us -> 354 us (1.011)
  waiting for transfers between devices: 89.1 us -> 106 us
  starting transfers between devices: 129 us -> 116 us
    ppermute x16, starting transfers between devices: 104 us -> 92.5 us  [shift(): return lax.ppermute(x, axis, [(i, (i + step) % n) for i in range(n)])]
    ppermute x16, waiting for transfers between devices: 53.8 us -> 64.1 us  [shift(): return lax.ppermute(x, axis, [(i, (i + step) % n) for i in range(n)])]
    all_to_all x1, starting transfers between devices: 17.7 us -> 10.2 us  [gy_sum(): return jnp.sum(lax.all_to_all(copies, GY, 0, 0), axis=0)]
    all_to_all x2 -> x3, starting transfers between devices: 7.26 us -> 13.4 us  [exchange_gather(): lax.all_to_all(copies, axis, 0, 0).reshape((n * x.shape[0],) + x.shape[1:])]
    all_to_all x2 -> x3, waiting for transfers between devices: 22.1 us -> 28.2 us  [exchange_gather(): lax.all_to_all(copies, axis, 0, 0).reshape((n * x.shape[0],) + x.shape[1:])]
    unnamed x59 -> x60, local copies, waits for them, and re-layouts: 7.22 us -> 8.76 us
  transfers between devices with their start and end apart: 19 -> 20, of which waited for: 9 -> 7; matrix products, arithmetic and copies ran while one was open for 5% -> 6% of each run, Pallas kernels for 0% -> 0%
where the time goes in v7:
time: 354 us; the launch traced here: 352 us
  starting transfers between devices  116 us (33%)
  waiting for transfers between devices  106 us (30%)
  local copies, waits for them, and re-layouts  53.4 us (15%)
  blocking collectives  40.3 us (11%)
  other arithmetic  29.9 us (8%)
  matrix products  5.28 us (1%)
    ppermute x16, starting transfers between devices, shift(): return lax.ppermute(x, axis, [(i, (i + step) % n) for i in range(n)])  92.5 us
    ppermute x16, waiting for transfers between devices, shift(): return lax.ppermute(x, axis, [(i, (i + step) % n) for i in range(n)])  64.1 us
    all_to_all x3, waiting for transfers between devices, exchange_gather(): lax.all_to_all(copies, axis, 0, 0).reshape((n * x.shape[0],) + x.shape[1:])  28.2 us
    all_to_all x1, blocking collectives, exchange_scatter_sum(): lax.all_to_all(split, axis, 0, 0).astype(jnp.float32)  27.4 us
    all_to_all x3, starting transfers between devices, exchange_gather(): lax.all_to_all(copies, axis, 0, 0).reshape((n * x.shape[0],) + x.shape[1:])  13.4 us
    all_to_all x1, waiting for transfers between devices, gy_sum(): return jnp.sum(lax.all_to_all(copies, GY, 0, 0), axis=0)  13.3 us
    all_to_all x1, blocking collectives, attend_combine(): received = lax.all_to_all(split, 'gyy', 0, 0)  12.9 us
    all_to_all x1, starting transfers between devices, gy_sum(): return jnp.sum(lax.all_to_all(copies, GY, 0, 0), axis=0)  10.2 us
  transfers between devices with their start and end apart: 20, of which 7 were waited for; matrix products, arithmetic and copies ran while one was open for 6% of the time, Pallas kernels for 0%

profile of v7, /device:TPU:6, one launch (start us, length us, event | category | flops | bytes accessed | tf_op | source)
XLA Modules:
  0.0 352.2 jit_solution(13096739341666147082)
XLA Ops:
  0.6 4.0 %collective-permute-start = (bf16[96,512]{1,0:T(8,128)(2,1)}, bf16[96,512]{1,0:T(8,128)(2,1)S(1)}, u32[]{:S(2)}, u32[]{:S(2)}) collective-permute-start(bf16[96,512]{1,0:T(8,128)(2,1)} %param.8), channel_id=1, source_target_pairs={{0,8},{8,16},{16,24},{24,32},{32,40},{40,48},{48,56},{56,0},{1,9},... | collective-permute-start | bytes 294920 | tf_op jit(solution)/shard_map/ppermute | solution.py:25
  4.6 5.2 %collective-permute-start.1 = (bf16[96,512]{1,0:T(8,128)(2,1)}, bf16[96,512]{1,0:T(8,128)(2,1)S(1)}, u32[]{:S(2)}, u32[]{:S(2)}) collective-permute-start(bf16[96,512]{1,0:T(8,128)(2,1)} %param.8), channel_id=1, source_target_pairs={{0,16},{8,24},{16,32},{24,40},{32,48},{40,56},{48,0},{56,8},{1,17}... | collective-permute-start | bytes 294920 | tf_op jit(solution)/shard_map/ppermute | solution.py:25
  9.8 7.7 %collective-permute-start.2 = (bf16[96,512]{1,0:T(8,128)(2,1)}, bf16[96,512]{1,0:T(8,128)(2,1)S(1)}, u32[]{:S(2)}, u32[]{:S(2)}) collective-permute-start(bf16[96,512]{1,0:T(8,128)(2,1)} %param.8), channel_id=1, source_target_pairs={{0,24},{8,32},{16,40},{24,48},{32,56},{40,0},{48,8},{56,16},{1,25}... | collective-permute-start | bytes 294920 | tf_op jit(solution)/shard_map/ppermute | solution.py:25
  20.8 7.8 %collective-permute-start.4 = (bf16[96,512]{1,0:T(8,128)(2,1)}, bf16[96,512]{1,0:T(8,128)(2,1)S(1)}, u32[]{:S(2)}, u32[]{:S(2)}) collective-permute-start(bf16[96,512]{1,0:T(8,128)(2,1)} %param.8), channel_id=1, source_target_pairs={{0,40},{8,48},{16,56},{24,0},{32,8},{40,16},{48,24},{56,32},{1,41}... | collective-permute-start | bytes 294920 | tf_op jit(solution)/shard_map/ppermute | solution.py:25
  30.3 10.2 %all-to-all-start = ((f32[8,96,2]{1,2,0:T(2,128)}), f32[8,96,2]{1,2,0:T(2,128)S(1)}, u32[]{:S(2)}, u32[]{:S(2)}) async-start(f32[8,96,2]{1,2,0:T(2,128)} %broadcast_in_dim.124), calls=%async_computation | async-start | bytes 16384 | tf_op jit(solution)/shard_map/all_to_all | solution.py:114
  42.1 13.3 %all-to-all-done = f32[8,96,2]{1,2,0:T(2,128)S(1)} async-done(((f32[8,96,2]{1,2,0:T(2,128)}), f32[8,96,2]{1,2,0:T(2,128)S(1)}, u32[]{:S(2)}, u32[]{:S(2)}) %all-to-all-start) | async-done | bytes 6176 | tf_op jit(solution)/shard_map/all_to_all | solution.py:114
  56.1 6.2 %all-to-all-start.1 = ((f32[8,96,2]{1,2,0:T(2,128)}), f32[8,96,2]{1,2,0:T(2,128)S(1)}, u32[]{:S(2)}, u32[]{:S(2)}) async-start(f32[8,96,2]{1,2,0:T(2,128)} %broadcast_in_dim.125), calls=%async_computation.1 | async-start | bytes 16384 | tf_op jit(solution)/shard_map/all_to_all | solution.py:65
  63.9 8.7 %all-to-all-done.1 = f32[8,96,2]{1,2,0:T(2,128)S(1)} async-done(((f32[8,96,2]{1,2,0:T(2,128)}), f32[8,96,2]{1,2,0:T(2,128)S(1)}, u32[]{:S(2)}, u32[]{:S(2)}) %all-to-all-start.1) | async-done | bytes 6176 | tf_op jit(solution)/shard_map/all_to_all | solution.py:65
  76.0 4.3 %collective-permute-start.6 = (bf16[96,512]{1,0:T(8,128)(2,1)S(1)}, bf16[96,512]{1,0:T(8,128)(2,1)S(1)}, u32[]{:S(2)}, u32[]{:S(2)}) collective-permute-start(bf16[96,512]{1,0:T(8,128)(2,1)S(1)} %copy-done.2), channel_id=1, source_target_pairs={{0,56},{8,0},{16,8},{24,16},{32,24},{40,32},{48,40},{56,48},{1,57}... | collective-permute-start | bytes 294920 | tf_op jit(solution)/shard_map/ppermute | solution.py:25
  87.7 27.4 %all_to_all.30 = bf16[4,192,1536]{2,1,0:T(8,128)(2,1)S(1)} all-to-all(bf16[4,192,1536]{2,1,0:T(8,128)(2,1)S(1)} %bitcast.157), channel_id=1, replica_groups=mesh['req'=8,'gx'=8,'gyy'=4,'gyz'=2] {'gyy'}, dimensions={0} | all-to-all | bytes 4718592 | tf_op jit(solution)/shard_map/all_to_all | solution.py:59
  118.5 38.5 %collective-permute-done.7 = bf16[192,1536]{1,0:T(8,128)(2,1)S(1)} collective-permute-done((bf16[192,1536]{1,0:T(8,128)(2,1)S(1)}, bf16[192,1536]{1,0:T(8,128)(2,1)S(1)}, u32[]{:S(2)}, u32[]{:S(2)}) %collective-permute-start.7) | collective-permute-done | bytes 589856 | tf_op jit(solution)/shard_map/ppermute | solution.py:25
  171.9 10.2 %all-to-all-done.3 = bf16[4,192,1536]{2,1,0:T(8,128)(2,1)S(1)} async-done(((bf16[4,192,1536]{2,1,0:T(8,128)(2,1)}), bf16[4,192,1536]{2,1,0:T(8,128)(2,1)S(1)}, u32[]{:S(2)}, u32[]{:S(2)}) %all-to-all-start.3) | async-done | bytes 2359328 | tf_op jit(solution)/shard_map/all_to_all | solution.py:65
  194.5 4.8 %copy.101 = bf16[2,384,1,512]{3,2,1,0:T(2,128)(2,1)} copy(bf16[2,384,1,512]{1,3,0,2:T(8,128)(2,1)} %bitcast.156) | data formatting | bytes 1572864 | tf_op jit(solution)/shard_map/stack;reshape | solution.py:182
  199.3 5.4 %fusion.18 = (bf16[384,2,512]{2,1,0:T(2,128)(2,1)}, bf16[384,2,512]{2,1,0:T(2,128)(2,1)S(1)}) fusion(bf16[2,384,1,512]{3,2,1,0:T(2,128)(2,1)S(1)} %copy.102, bf16[2,384,1,512]{3,2,1,0:T(2,128)(2,1)} %copy.101), kind=kLoop, calls=%fused_computation.38 | loop fusion | flops 3145728 | bytes 3145728 | tf_op jit(solution)/shard_map/squeeze | solution.py:191
  207.7 3.9 %gather_fusion.2 = bf16[272,2,512]{2,1,0:T(2,128)(2,1)} fusion(bf16[384,2,512]{2,1,0:T(2,128)(2,1)S(1)} %get-tuple-element.16, s32[1024]{0:T(1024)S(1)} %pad_clamp_fusion), kind=kCustom, calls=%fused_computation.1.clone | custom fusion | bytes 1115200 | tf_op jit(solution)/shard_map/jit(_take)/gather | solution.py:143
  211.7 5.7 %broadcast_select_fusion.1 = (bf16[272,2,512]{2,1,0:T(2,128)(2,1)S(1)}, bf16[272,2,512]{2,1,0:T(2,128)(2,1)S(1)}) fusion(pred[272]{0:T(512)(128)(4,1)S(1)} %copy-done.18, bf16[272,2,512]{2,1,0:T(2,128)(2,1)S(1)} %gather_fusion.1, pred[272]{0:T(512)(128)(4,1)S(1)} %copy-done.20, bf16[2,272,2,512]{3,2,1,0:T(2,128)(2,1)} %param.12, ...), kind=kLoop, calls=%fused_computation.25 | loop fusion | flops 1114112 | bytes 3343424 | tf_op jit(solution)/shard_map/jit(_where)/select_n | solution.py:144
  236.6 12.9 %all_to_all.31 = bf16[4,192,528]{2,1,0:T(8,128)(2,1)S(1)} all-to-all(bf16[4,192,528]{2,1,0:T(8,128)(2,1)S(1)} %concatenate.29), channel_id=1, replica_groups=mesh['req'=8,'gx'=8,'gyy'=4,'gyz'=2] {'gyy'}, dimensions={0} | all-to-all | bytes 1622016 | tf_op jit(solution)/shard_map/all_to_all | solution.py:101
  254.5 17.1 %collective-permute-done.8 = bf16[192,528]{1,0:T(8,128)(2,1)S(1)} collective-permute-done((bf16[192,528]{1,0:T(8,128)(2,1)S(1)}, bf16[192,528]{1,0:T(8,128)(2,1)S(1)}, u32[]{:S(2)}, u32[]{:S(2)}) %collective-permute-start.8) | collective-permute-done | bytes 202784 | tf_op jit(solution)/shard_map/ppermute | solution.py:25
  277.5 9.3 %all-to-all-done.5 = bf16[4,192,512]{2,1,0:T(8,128)(2,1)S(1)} async-done(((bf16[4,192,512]{2,1,0:T(8,128)(2,1)}), bf16[4,192,512]{2,1,0:T(8,128)(2,1)S(1)}, u32[]{:S(2)}, u32[]{:S(2)}) %all-to-all-start.5) | async-done | bytes 786464 | tf_op jit(solution)/shard_map/all_to_all | solution.py:65
  287.5 30.0 %collective-permute-start.15 = (bf16[96,512]{1,0:T(8,128)(2,1)S(1)}, bf16[96,512]{1,0:T(8,128)(2,1)S(1)}, u32[]{:S(2)}, u32[]{:S(2)}) collective-permute-start(bf16[96,512]{1,0:T(8,128)(2,1)S(1)} %get-tuple-element.28), channel_id=1, source_target_pairs={{0,56},{8,0},{16,8},{24,16},{32,24},{40,32},{48,40},{56,48},{1,57}... | collective-permute-start | bytes 294920 | tf_op jit(solution)/shard_map/ppermute | solution.py:25
  323.2 5.1 %collective-permute-start.12 = (bf16[96,512]{1,0:T(8,128)(2,1)S(1)}, bf16[96,512]{1,0:T(8,128)(2,1)S(1)}, u32[]{:S(2)}, u32[]{:S(2)}) collective-permute-start(bf16[96,512]{1,0:T(8,128)(2,1)S(1)} %get-tuple-element.31), channel_id=1, source_target_pairs={{0,32},{8,40},{16,48},{24,56},{32,0},{40,8},{48,16},{56,24},{1,33}... | collective-permute-start | bytes 294920 | tf_op jit(solution)/shard_map/ppermute | solution.py:25
  330.3 6.1 %collective-permute-start.10 = (bf16[96,512]{1,0:T(8,128)(2,1)S(1)}, bf16[96,512]{1,0:T(8,128)(2,1)S(1)}, u32[]{:S(2)}, u32[]{:S(2)}) collective-permute-start(bf16[96,512]{1,0:T(8,128)(2,1)S(1)} %get-tuple-element.33), channel_id=1, source_target_pairs={{0,16},{8,24},{16,32},{24,40},{32,48},{40,56},{48,0},{56,8},{1,17}... | collective-permute-start | bytes 294920 | tf_op jit(solution)/shard_map/ppermute | solution.py:25
  336.4 3.9 %collective-permute-start.9 = (bf16[96,512]{1,0:T(8,128)(2,1)S(1)}, bf16[96,512]{1,0:T(8,128)(2,1)S(1)}, u32[]{:S(2)}, u32[]{:S(2)}) collective-permute-start(bf16[96,512]{1,0:T(8,128)(2,1)S(1)} %get-tuple-element.27), channel_id=1, source_target_pairs={{0,8},{8,16},{16,24},{24,32},{32,40},{40,48},{48,56},{56,0},{1,9},... | collective-permute-start | bytes 294920 | tf_op jit(solution)/shard_map/ppermute | solution.py:25
  342.9 8.5 %collective-permute-done.12 = bf16[96,512]{1,0:T(8,128)(2,1)S(1)} collective-permute-done((bf16[96,512]{1,0:T(8,128)(2,1)S(1)}, bf16[96,512]{1,0:T(8,128)(2,1)S(1)}, u32[]{:S(2)}, u32[]{:S(2)}) %collective-permute-start.12) | collective-permute-done | bytes 98336 | tf_op jit(solution)/shard_map/ppermute | solution.py:25
  (170 shorter events, 94.4 us)
Async XLA Ops:
  0.6 286.2 %copy-start = (bf16[512,512]{1,0:T(8,128)(2,1)S(1)}, bf16[512,512]{1,0:T(8,128)(2,1)}, u32[]{:S(2)}) copy-start(bf16[512,512]{1,0:T(8,128)(2,1)} %param.11) | copy-start | bytes 1572868
  0.6 72.3 %collective-permute-start = (bf16[96,512]{1,0:T(8,128)(2,1)}, bf16[96,512]{1,0:T(8,128)(2,1)S(1)}, u32[]{:S(2)}, u32[]{:S(2)}) collective-permute-start(bf16[96,512]{1,0:T(8,128)(2,1)} %param.8), channel_id=1, source_target_pairs={{0,8},{8,16},{16,24},{24,32},{32,40},{40,48},{48,56},{56,0},{1,9},... | collective-permute-start | bytes 294920 | tf_op jit(solution)/shard_map/ppermute | solution.py:25
  4.6 71.4 %collective-permute-start.1 = (bf16[96,512]{1,0:T(8,128)(2,1)}, bf16[96,512]{1,0:T(8,128)(2,1)S(1)}, u32[]{:S(2)}, u32[]{:S(2)}) collective-permute-start(bf16[96,512]{1,0:T(8,128)(2,1)} %param.8), channel_id=1, source_target_pairs={{0,16},{8,24},{16,32},{24,40},{32,48},{40,56},{48,0},{56,8},{1,17}... | collective-permute-start | bytes 294920 | tf_op jit(solution)/shard_map/ppermute | solution.py:25
  9.8 71.2 %collective-permute-start.2 = (bf16[96,512]{1,0:T(8,128)(2,1)}, bf16[96,512]{1,0:T(8,128)(2,1)S(1)}, u32[]{:S(2)}, u32[]{:S(2)}) collective-permute-start(bf16[96,512]{1,0:T(8,128)(2,1)} %param.8), channel_id=1, source_target_pairs={{0,24},{8,32},{16,40},{24,48},{32,56},{40,0},{48,8},{56,16},{1,25}... | collective-permute-start | bytes 294920 | tf_op jit(solution)/shard_map/ppermute | solution.py:25
  17.6 64.1 %collective-permute-start.3 = (bf16[96,512]{1,0:T(8,128)(2,1)}, bf16[96,512]{1,0:T(8,128)(2,1)S(1)}, u32[]{:S(2)}, u32[]{:S(2)}) collective-permute-start(bf16[96,512]{1,0:T(8,128)(2,1)} %param.8), channel_id=1, source_target_pairs={{0,32},{8,40},{16,48},{24,56},{32,0},{40,8},{48,16},{56,24},{1,33}... | collective-permute-start | bytes 294920 | tf_op jit(solution)/shard_map/ppermute | solution.py:25
  20.8 61.4 %collective-permute-start.4 = (bf16[96,512]{1,0:T(8,128)(2,1)}, bf16[96,512]{1,0:T(8,128)(2,1)S(1)}, u32[]{:S(2)}, u32[]{:S(2)}) collective-permute-start(bf16[96,512]{1,0:T(8,128)(2,1)} %param.8), channel_id=1, source_target_pairs={{0,40},{8,48},{16,56},{24,0},{32,8},{40,16},{48,24},{56,32},{1,41}... | collective-permute-start | bytes 294920 | tf_op jit(solution)/shard_map/ppermute | solution.py:25
  30.3 25.1 %all-to-all-start = ((f32[8,96,2]{1,2,0:T(2,128)}), f32[8,96,2]{1,2,0:T(2,128)S(1)}, u32[]{:S(2)}, u32[]{:S(2)}) async-start(f32[8,96,2]{1,2,0:T(2,128)} %broadcast_in_dim.124), calls=%async_computation | async-start | bytes 16384 | tf_op jit(solution)/shard_map/all_to_all | solution.py:114
  42.1 30.9 %copy-start.2 = (bf16[96,512]{1,0:T(8,128)(2,1)S(1)}, bf16[96,512]{1,0:T(8,128)(2,1)}, u32[]{:S(2)}) copy-start(bf16[96,512]{1,0:T(8,128)(2,1)} %param.8) | copy-start | bytes 294916
  56.1 16.6 %all-to-all-start.1 = ((f32[8,96,2]{1,2,0:T(2,128)}), f32[8,96,2]{1,2,0:T(2,128)S(1)}, u32[]{:S(2)}, u32[]{:S(2)}) async-start(f32[8,96,2]{1,2,0:T(2,128)} %broadcast_in_dim.125), calls=%async_computation.1 | async-start | bytes 16384 | tf_op jit(solution)/shard_map/all_to_all | solution.py:65
  63.9 22.0 %copy-start.16 = (f32[512]{0:T(512)S(1)}, f32[512]{0:T(512)}, u32[]{:S(2)}) copy-start(f32[512]{0:T(512)} %param.9) | copy-start | bytes 6148
  73.0 10.0 %collective-permute-start.5 = (bf16[96,512]{1,0:T(8,128)(2,1)S(1)}, bf16[96,512]{1,0:T(8,128)(2,1)S(1)}, u32[]{:S(2)}, u32[]{:S(2)}) collective-permute-start(bf16[96,512]{1,0:T(8,128)(2,1)S(1)} %copy-done.2), channel_id=1, source_target_pairs={{0,48},{8,56},{16,0},{24,8},{32,16},{40,24},{48,32},{56,40},{1,49}... | collective-permute-start | bytes 294920 | tf_op jit(solution)/shard_map/ppermute | solution.py:25
  76.0 7.5 %collective-permute-start.6 = (bf16[96,512]{1,0:T(8,128)(2,1)S(1)}, bf16[96,512]{1,0:T(8,128)(2,1)S(1)}, u32[]{:S(2)}, u32[]{:S(2)}) collective-permute-start(bf16[96,512]{1,0:T(8,128)(2,1)S(1)} %copy-done.2), channel_id=1, source_target_pairs={{0,56},{8,0},{16,8},{24,16},{32,24},{40,32},{48,40},{56,48},{1,57}... | collective-permute-start | bytes 294920 | tf_op jit(solution)/shard_map/ppermute | solution.py:25
  115.7 41.3 %collective-permute-start.7 = (bf16[192,1536]{1,0:T(8,128)(2,1)S(1)}, bf16[192,1536]{1,0:T(8,128)(2,1)S(1)}, u32[]{:S(2)}, u32[]{:S(2)}) collective-permute-start(bf16[192,1536]{1,0:T(8,128)(2,1)S(1)} %reduce_sum.60), channel_id=1, source_target_pairs={{0,1},{1,0},{2,3},{3,2},{4,5},{5,4},{6,7},{7,6},{8,9},{9,8},{10,11... | collective-permute-start | bytes 1769480 | tf_op jit(solution)/shard_map/ppermute | solution.py:25
  158.8 23.3 %all-to-all-start.3 = ((bf16[4,192,1536]{2,1,0:T(8,128)(2,1)}), bf16[4,192,1536]{2,1,0:T(8,128)(2,1)S(1)}, u32[]{:S(2)}, u32[]{:S(2)}) async-start(bf16[4,192,1536]{2,1,0:T(8,128)(2,1)} %broadcast_in_dim.126), calls=%async_computation.3 | async-start | bytes 4718592 | tf_op jit(solution)/shard_map/all_to_all | solution.py:65
  252.1 19.5 %collective-permute-start.8 = (bf16[192,528]{1,0:T(8,128)(2,1)S(1)}, bf16[192,528]{1,0:T(8,128)(2,1)S(1)}, u32[]{:S(2)}, u32[]{:S(2)}) collective-permute-start(bf16[192,528]{1,0:T(8,128)(2,1)S(1)} %pad_maximum_fusion.3), channel_id=1, source_target_pairs={{0,1},{1,0},{2,3},{3,2},{4,5},{5,4},{6,7},{7,6},{8,9},{9,8},{10,11... | collective-permute-start | bytes 608264 | tf_op jit(solution)/shard_map/ppermute | solution.py:25
  273.9 13.0 %all-to-all-start.5 = ((bf16[4,192,512]{2,1,0:T(8,128)(2,1)}), bf16[4,192,512]{2,1,0:T(8,128)(2,1)S(1)}, u32[]{:S(2)}, u32[]{:S(2)}) async-start(bf16[4,192,512]{2,1,0:T(8,128)(2,1)} %broadcast_in_dim.138), calls=%async_computation.5 | async-start | bytes 1572864 | tf_op jit(solution)/shard_map/all_to_all | solution.py:65
  287.4 64.0 %copy-start.3 = (bf16[96,512]{1,0:T(8,128)(2,1)S(1)}, bf16[96,512]{1,0:T(8,128)(2,1)}, u32[]{:S(2)}) copy-start(bf16[96,512]{1,0:T(8,128)(2,1)} %param.8) | copy-start | bytes 294916
  287.5 42.8 %collective-permute-start.15 = (bf16[96,512]{1,0:T(8,128)(2,1)S(1)}, bf16[96,512]{1,0:T(8,128)(2,1)S(1)}, u32[]{:S(2)}, u32[]{:S(2)}) collective-permute-start(bf16[96,512]{1,0:T(8,128)(2,1)S(1)} %get-tuple-element.28), channel_id=1, source_target_pairs={{0,56},{8,0},{16,8},{24,16},{32,24},{40,32},{48,40},{56,48},{1,57}... | collective-permute-start | bytes 294920 | tf_op jit(solution)/shard_map/ppermute | solution.py:25
  317.5 18.8 %collective-permute-start.14 = (bf16[96,512]{1,0:T(8,128)(2,1)S(1)}, bf16[96,512]{1,0:T(8,128)(2,1)S(1)}, u32[]{:S(2)}, u32[]{:S(2)}) collective-permute-start(bf16[96,512]{1,0:T(8,128)(2,1)S(1)} %get-tuple-element.29), channel_id=1, source_target_pairs={{0,48},{8,56},{16,0},{24,8},{32,16},{40,24},{48,32},{56,40},{1,49}... | collective-permute-start | bytes 294920 | tf_op jit(solution)/shard_map/ppermute | solution.py:25
  319.5 23.5 %collective-permute-start.13 = (bf16[96,512]{1,0:T(8,128)(2,1)S(1)}, bf16[96,512]{1,0:T(8,128)(2,1)S(1)}, u32[]{:S(2)}, u32[]{:S(2)}) collective-permute-start(bf16[96,512]{1,0:T(8,128)(2,1)S(1)} %get-tuple-element.30), channel_id=1, source_target_pairs={{0,40},{8,48},{16,56},{24,0},{32,8},{40,16},{48,24},{56,32},{1,41}... | collective-permute-start | bytes 294920 | tf_op jit(solution)/shard_map/ppermute | solution.py:25
  323.2 28.2 %collective-permute-start.12 = (bf16[96,512]{1,0:T(8,128)(2,1)S(1)}, bf16[96,512]{1,0:T(8,128)(2,1)S(1)}, u32[]{:S(2)}, u32[]{:S(2)}) collective-permute-start(bf16[96,512]{1,0:T(8,128)(2,1)S(1)} %get-tuple-element.31), channel_id=1, source_target_pairs={{0,32},{8,40},{16,48},{24,56},{32,0},{40,8},{48,16},{56,24},{1,33}... | collective-permute-start | bytes 294920 | tf_op jit(solution)/shard_map/ppermute | solution.py:25
  328.3 23.1 %collective-permute-start.11 = (bf16[96,512]{1,0:T(8,128)(2,1)S(1)}, bf16[96,512]{1,0:T(8,128)(2,1)S(1)}, u32[]{:S(2)}, u32[]{:S(2)}) collective-permute-start(bf16[96,512]{1,0:T(8,128)(2,1)S(1)} %get-tuple-element.32), channel_id=1, source_target_pairs={{0,24},{8,32},{16,40},{24,48},{32,56},{40,0},{48,8},{56,16},{1,25}... | collective-permute-start | bytes 294920 | tf_op jit(solution)/shard_map/ppermute | solution.py:25
  330.3 21.1 %collective-permute-start.10 = (bf16[96,512]{1,0:T(8,128)(2,1)S(1)}, bf16[96,512]{1,0:T(8,128)(2,1)S(1)}, u32[]{:S(2)}, u32[]{:S(2)}) collective-permute-start(bf16[96,512]{1,0:T(8,128)(2,1)S(1)} %get-tuple-element.33), channel_id=1, source_target_pairs={{0,16},{8,24},{16,32},{24,40},{32,48},{40,56},{48,0},{56,8},{1,17}... | collective-permute-start | bytes 294920 | tf_op jit(solution)/shard_map/ppermute | solution.py:25
  336.4 15.0 %collective-permute-start.9 = (bf16[96,512]{1,0:T(8,128)(2,1)S(1)}, bf16[96,512]{1,0:T(8,128)(2,1)S(1)}, u32[]{:S(2)}, u32[]{:S(2)}) collective-permute-start(bf16[96,512]{1,0:T(8,128)(2,1)S(1)} %get-tuple-element.27), channel_id=1, source_target_pairs={{0,8},{8,16},{16,24},{24,32},{32,40},{40,48},{48,56},{56,0},{1,9},... | collective-permute-start | bytes 294920 | tf_op jit(solution)/shard_map/ppermute | solution.py:25
  (19 other events, 71.3 us)

commit v8 on v6

--- a/solution.py
+++ b/solution.py
@@ -140,7 +140,10 @@
 def write_cache(fresh_rows, cache_block, positions, length, group):
     offset = positions - length
     inside = (offset >= 0) & (offset < group)
-    taken = jnp.take(fresh_rows, jnp.clip(offset, 0, group - 1), axis=0)
+    block = cache_block.shape[0]
+    padded = jnp.pad(fresh_rows, ((block, block), (0, 0), (0, 0)))
+    start = jnp.clip(offset[0] + block, 0, group + block)
+    taken = lax.dynamic_slice_in_dim(padded, start, block, axis=0)
     return jnp.where(inside[:, None, None], taken, cache_block)
 
 

time: 350 us -> 329 us (0.940)
  other arithmetic: 30.5 us -> 15.9 us
  waiting for transfers between devices: 89.1 us -> 81.5 us
  local copies, waits for them, and re-layouts: 50.9 us -> 44 us
  matrix products: 5.31 us -> 9.2 us
    unnamed x59 -> x50, local copies, waits for them, and re-layouts: 7.22 us -> 15.5 us
    another operation x2 -> x0, local copies, waits for them, and re-layouts: 8.27 us -> none  [shards(): jnp.stack([qkv[:, :, :, head_size:2 * head_size].reshape(requests, group,...]
    gather x2 -> x0, local copies, waits for them, and re-layouts: 6.9 us -> none  [write_cache(): taken = jnp.take(fresh_rows, jnp.clip(offset, 0, group - 1), axis=0)]
    squeeze x1, other arithmetic: 5.44 us -> 0.18 us  [shards(): fresh[request]]
    select_n x1 -> x2, other arithmetic: 5.66 us -> 0.97 us  [write_cache(): return jnp.where(inside[:, None, None], taken, cache_block)]
    all_to_all x2, waiting for transfers between devices: 22.1 us -> 17.5 us  [exchange_gather(): lax.all_to_all(copies, axis, 0, 0).reshape((n * x.shape[0],) + x.shape[1:])]
  transfers between devices with their start and end apart: 19 -> 19, of which waited for: 9 -> 8; matrix products, arithmetic and copies ran while one was open for 5% -> 7% of each run, Pallas kernels for 0% -> 0%
where the time goes in v8:
time: 329 us; the launch traced here: 328 us
  starting transfers between devices  132 us (40%)
  waiting for transfers between devices  81.5 us (25%)
  local copies, waits for them, and re-layouts  44 us (13%)
  blocking collectives  41.8 us (13%)
  other arithmetic  15.9 us (5%)
  matrix products  9.2 us (3%)
    ppermute x16, starting transfers between devices, shift(): return lax.ppermute(x, axis, [(i, (i + step) % n) for i in range(n)])  107 us
    ppermute x16, waiting for transfers between devices, shift(): return lax.ppermute(x, axis, [(i, (i + step) % n) for i in range(n)])  50.9 us
    all_to_all x1, blocking collectives, exchange_scatter_sum(): lax.all_to_all(split, axis, 0, 0).astype(jnp.float32)  28.9 us
    all_to_all x1, starting transfers between devices, gy_sum(): return jnp.sum(lax.all_to_all(copies, GY, 0, 0), axis=0)  17.7 us
    all_to_all x2, waiting for transfers between devices, exchange_gather(): lax.all_to_all(copies, axis, 0, 0).reshape((n * x.shape[0],) + x.shape[1:])  17.5 us
    unnamed x50, local copies, waits for them, and re-layouts  15.5 us
    all_to_all x1, waiting for transfers between devices, gy_sum(): return jnp.sum(lax.all_to_all(copies, GY, 0, 0), axis=0)  13.2 us
    all_to_all x1, blocking collectives, attend_combine(): received = lax.all_to_all(split, 'gyy', 0, 0)  12.9 us
  transfers between devices with their start and end apart: 19, of which 8 were waited for; matrix products, arithmetic and copies ran while one was open for 7% of the time, Pallas kernels for 0%

profile of v8, /device:TPU:6, one launch (start us, length us, event | category | flops | bytes accessed | tf_op | source)
XLA Modules:
  0.0 327.5 jit_solution(14478790042899523737)
XLA Ops:
  2.4 17.7 %all-to-all-start = ((f32[8,2,96]{2,1,0:T(2,128)}), f32[8,2,96]{2,1,0:T(2,128)S(1)}, u32[]{:S(2)}, u32[]{:S(2)}) async-start(f32[8,2,96]{2,1,0:T(2,128)} %broadcast_in_dim.108), calls=%async_computation | async-start | bytes 16384 | tf_op jit(solution)/shard_map/all_to_all | solution.py:114
  21.8 13.2 %all-to-all-done = f32[8,2,96]{2,1,0:T(2,128)S(1)} async-done(((f32[8,2,96]{2,1,0:T(2,128)}), f32[8,2,96]{2,1,0:T(2,128)S(1)}, u32[]{:S(2)}, u32[]{:S(2)}) %all-to-all-start) | async-done | bytes 6176 | tf_op jit(solution)/shard_map/all_to_all | solution.py:114
  38.7 3.4 %collective-permute-start.1 = (bf16[96,512]{1,0:T(8,128)(2,1)S(1)}, bf16[96,512]{1,0:T(8,128)(2,1)S(1)}, u32[]{:S(2)}, u32[]{:S(2)}) collective-permute-start(bf16[96,512]{1,0:T(8,128)(2,1)S(1)} %get-tuple-element.17), channel_id=1, source_target_pairs={{0,16},{8,24},{16,32},{24,40},{32,48},{40,56},{48,0},{56,8},{1,17}... | collective-permute-start | bytes 294920 | tf_op jit(solution)/shard_map/ppermute | solution.py:25
  42.1 3.8 %collective-permute-start.2 = (bf16[96,512]{1,0:T(8,128)(2,1)S(1)}, bf16[96,512]{1,0:T(8,128)(2,1)S(1)}, u32[]{:S(2)}, u32[]{:S(2)}) collective-permute-start(bf16[96,512]{1,0:T(8,128)(2,1)S(1)} %get-tuple-element.17), channel_id=1, source_target_pairs={{0,24},{8,32},{16,40},{24,48},{32,56},{40,0},{48,8},{56,16},{1,25}... | collective-permute-start | bytes 294920 | tf_op jit(solution)/shard_map/ppermute | solution.py:25
  46.0 7.3 %collective-permute-start.3 = (bf16[96,512]{1,0:T(8,128)(2,1)S(1)}, bf16[96,512]{1,0:T(8,128)(2,1)S(1)}, u32[]{:S(2)}, u32[]{:S(2)}) collective-permute-start(bf16[96,512]{1,0:T(8,128)(2,1)S(1)} %get-tuple-element.17), channel_id=1, source_target_pairs={{0,32},{8,40},{16,48},{24,56},{32,0},{40,8},{48,16},{56,24},{1,33}... | collective-permute-start | bytes 294920 | tf_op jit(solution)/shard_map/ppermute | solution.py:25
  53.2 2.9 collective-permute-start.4
  56.2 6.4 %collective-permute-start.5 = (bf16[96,512]{1,0:T(8,128)(2,1)S(1)}, bf16[96,512]{1,0:T(8,128)(2,1)S(1)}, u32[]{:S(2)}, u32[]{:S(2)}) collective-permute-start(bf16[96,512]{1,0:T(8,128)(2,1)S(1)} %get-tuple-element.17), channel_id=1, source_target_pairs={{0,48},{8,56},{16,0},{24,8},{32,16},{40,24},{48,32},{56,40},{1,49}... | collective-permute-start | bytes 294920 | tf_op jit(solution)/shard_map/ppermute | solution.py:25
  63.2 3.8 %collective-permute-start.6 = (bf16[96,512]{1,0:T(8,128)(2,1)S(1)}, bf16[96,512]{1,0:T(8,128)(2,1)S(1)}, u32[]{:S(2)}, u32[]{:S(2)}) collective-permute-start(bf16[96,512]{1,0:T(8,128)(2,1)S(1)} %get-tuple-element.17), channel_id=1, source_target_pairs={{0,56},{8,0},{16,8},{24,16},{32,24},{40,32},{48,40},{56,48},{1,57}... | collective-permute-start | bytes 294920 | tf_op jit(solution)/shard_map/ppermute | solution.py:25
  69.7 3.1 collective-permute-done.5
  77.4 28.9 %all_to_all.25 = bf16[4,192,1536]{2,1,0:T(8,128)(2,1)S(1)} all-to-all(bf16[4,192,1536]{2,1,0:T(8,128)(2,1)S(1)} %bitcast.145), channel_id=1, replica_groups=mesh['req'=8,'gx'=8,'gyy'=4,'gyz'=2] {'gyy'}, dimensions={0} | all-to-all | bytes 4718592 | tf_op jit(solution)/shard_map/all_to_all | solution.py:59
  109.7 27.4 %collective-permute-done.7 = bf16[192,1536]{1,0:T(8,128)(2,1)S(1)} collective-permute-done((bf16[192,1536]{1,0:T(8,128)(2,1)S(1)}, bf16[192,1536]{1,0:T(8,128)(2,1)S(1)}, u32[]{:S(2)}, u32[]{:S(2)}) %collective-permute-start.7) | collective-permute-done | bytes 589856 | tf_op jit(solution)/shard_map/ppermute | solution.py:25
  138.8 3.9 %all-to-all-start.2 = ((bf16[4,192,1536]{2,1,0:T(8,128)(2,1)}), bf16[4,192,1536]{2,1,0:T(8,128)(2,1)S(1)}, u32[]{:S(2)}, u32[]{:S(2)}) async-start(bf16[4,192,1536]{2,1,0:T(8,128)(2,1)} %broadcast_in_dim.110), calls=%async_computation.2 | async-start | bytes 4718592 | tf_op jit(solution)/shard_map/all_to_all | solution.py:65
  156.6 8.1 %all-to-all-done.2 = bf16[4,192,1536]{2,1,0:T(8,128)(2,1)S(1)} async-done(((bf16[4,192,1536]{2,1,0:T(8,128)(2,1)}), bf16[4,192,1536]{2,1,0:T(8,128)(2,1)S(1)}, u32[]{:S(2)}, u32[]{:S(2)}) %all-to-all-start.2) | async-done | bytes 2359328 | tf_op jit(solution)/shard_map/all_to_all | solution.py:65
  193.8 12.9 %all_to_all.26 = bf16[4,192,528]{2,1,0:T(8,128)(2,1)S(1)} all-to-all(bf16[4,192,528]{2,1,0:T(8,128)(2,1)S(1)} %concatenate.29), channel_id=1, replica_groups=mesh['req'=8,'gx'=8,'gyy'=4,'gyz'=2] {'gyy'}, dimensions={0} | all-to-all | bytes 1622016 | tf_op jit(solution)/shard_map/all_to_all | solution.py:101
  211.6 14.5 %collective-permute-done.8 = bf16[192,528]{1,0:T(8,128)(2,1)S(1)} collective-permute-done((bf16[192,528]{1,0:T(8,128)(2,1)S(1)}, bf16[192,528]{1,0:T(8,128)(2,1)S(1)}, u32[]{:S(2)}, u32[]{:S(2)}) %collective-permute-start.8) | collective-permute-done | bytes 202784 | tf_op jit(solution)/shard_map/ppermute | solution.py:25
  228.4 3.5 %all-to-all-start.4 = ((bf16[4,192,512]{2,1,0:T(8,128)(2,1)}), bf16[4,192,512]{2,1,0:T(8,128)(2,1)S(1)}, u32[]{:S(2)}, u32[]{:S(2)}) async-start(bf16[4,192,512]{2,1,0:T(8,128)(2,1)} %broadcast_in_dim.122), calls=%async_computation.4 | async-start | bytes 1572864 | tf_op jit(solution)/shard_map/all_to_all | solution.py:65
  232.0 9.3 %all-to-all-done.4 = bf16[4,192,512]{2,1,0:T(8,128)(2,1)S(1)} async-done(((bf16[4,192,512]{2,1,0:T(8,128)(2,1)}), bf16[4,192,512]{2,1,0:T(8,128)(2,1)S(1)}, u32[]{:S(2)}, u32[]{:S(2)}) %all-to-all-start.4) | async-done | bytes 786464 | tf_op jit(solution)/shard_map/all_to_all | solution.py:65
  242.9 32.7 %collective-permute-start.10 = (bf16[96,512]{1,0:T(8,128)(2,1)S(1)}, bf16[96,512]{1,0:T(8,128)(2,1)S(1)}, u32[]{:S(2)}, u32[]{:S(2)}) collective-permute-start(bf16[96,512]{1,0:T(8,128)(2,1)S(1)} %get-tuple-element.36), channel_id=1, source_target_pairs={{0,16},{8,24},{16,32},{24,40},{32,48},{40,56},{48,0},{56,8},{1,17}... | collective-permute-start | bytes 294920 | tf_op jit(solution)/shard_map/ppermute | solution.py:25
  275.6 15.2 %collective-permute-start.11 = (bf16[96,512]{1,0:T(8,128)(2,1)S(1)}, bf16[96,512]{1,0:T(8,128)(2,1)S(1)}, u32[]{:S(2)}, u32[]{:S(2)}) collective-permute-start(bf16[96,512]{1,0:T(8,128)(2,1)S(1)} %get-tuple-element.35), channel_id=1, source_target_pairs={{0,24},{8,32},{16,40},{24,48},{32,56},{40,0},{48,8},{56,16},{1,25}... | collective-permute-start | bytes 294920 | tf_op jit(solution)/shard_map/ppermute | solution.py:25
  292.8 7.8 %collective-permute-start.13 = (bf16[96,512]{1,0:T(8,128)(2,1)S(1)}, bf16[96,512]{1,0:T(8,128)(2,1)S(1)}, u32[]{:S(2)}, u32[]{:S(2)}) collective-permute-start(bf16[96,512]{1,0:T(8,128)(2,1)S(1)} %get-tuple-element.33), channel_id=1, source_target_pairs={{0,40},{8,48},{16,56},{24,0},{32,8},{40,16},{48,24},{56,32},{1,41}... | collective-permute-start | bytes 294920 | tf_op jit(solution)/shard_map/ppermute | solution.py:25
  300.6 4.8 %collective-permute-start.14 = (bf16[96,512]{1,0:T(8,128)(2,1)S(1)}, bf16[96,512]{1,0:T(8,128)(2,1)S(1)}, u32[]{:S(2)}, u32[]{:S(2)}) collective-permute-start(bf16[96,512]{1,0:T(8,128)(2,1)S(1)} %get-tuple-element.32), channel_id=1, source_target_pairs={{0,48},{8,56},{16,0},{24,8},{32,16},{40,24},{48,32},{56,40},{1,49}... | collective-permute-start | bytes 294920 | tf_op jit(solution)/shard_map/ppermute | solution.py:25
  305.4 7.3 %collective-permute-start.15 = (bf16[96,512]{1,0:T(8,128)(2,1)S(1)}, bf16[96,512]{1,0:T(8,128)(2,1)S(1)}, u32[]{:S(2)}, u32[]{:S(2)}) collective-permute-start(bf16[96,512]{1,0:T(8,128)(2,1)S(1)} %get-tuple-element.31), channel_id=1, source_target_pairs={{0,56},{8,0},{16,8},{24,16},{32,24},{40,32},{48,40},{56,48},{1,57}... | collective-permute-start | bytes 294920 | tf_op jit(solution)/shard_map/ppermute | solution.py:25
  316.1 3.9 %copy.117 = bf16[2,272,2,512]{3,2,1,0:T(2,128)(2,1)} copy(bf16[2,272,2,512]{1,3,2,0:T(8,128)(2,1)} %pad_maximum_fusion) | data formatting | bytes 2228224
  320.1 5.8 %collective-permute-done.9 = bf16[96,512]{1,0:T(8,128)(2,1)S(1)} collective-permute-done((bf16[96,512]{1,0:T(8,128)(2,1)S(1)}, bf16[96,512]{1,0:T(8,128)(2,1)S(1)}, u32[]{:S(2)}, u32[]{:S(2)}) %collective-permute-start.9) | collective-permute-done | bytes 98336 | tf_op jit(solution)/shard_map/ppermute | solution.py:25
  (152 shorter events, 77.0 us)
Async XLA Ops:
  0.6 240.7 %copy-start = (bf16[512,512]{1,0:T(8,128)(2,1)S(1)}, bf16[512,512]{1,0:T(8,128)(2,1)}, u32[]{:S(2)}) copy-start(bf16[512,512]{1,0:T(8,128)(2,1)} %param.9) | copy-start | bytes 1572868
  0.6 34.4 %copy-start.5 = (bf16[96,512]{1,0:T(8,128)(2,1)S(1)}, bf16[96,512]{1,0:T(8,128)(2,1)}, u32[]{:S(2)}) copy-start(bf16[96,512]{1,0:T(8,128)(2,1)} %param.6) | copy-start | bytes 294916
  0.7 34.4 %copy-start.15 = (f32[512]{0:T(512)S(1)}, f32[512]{0:T(512)}, u32[]{:S(2)}) copy-start(f32[512]{0:T(512)} %param.7) | copy-start | bytes 6148
  2.4 32.6 %all-to-all-start = ((f32[8,2,96]{2,1,0:T(2,128)}), f32[8,2,96]{2,1,0:T(2,128)S(1)}, u32[]{:S(2)}, u32[]{:S(2)}) async-start(f32[8,2,96]{2,1,0:T(2,128)} %broadcast_in_dim.108), calls=%async_computation | async-start | bytes 16384 | tf_op jit(solution)/shard_map/all_to_all | solution.py:114
  35.8 20.4 %collective-permute-start = (bf16[96,512]{1,0:T(8,128)(2,1)S(1)}, bf16[96,512]{1,0:T(8,128)(2,1)S(1)}, u32[]{:S(2)}, u32[]{:S(2)}) collective-permute-start(bf16[96,512]{1,0:T(8,128)(2,1)S(1)} %get-tuple-element.17), channel_id=1, source_target_pairs={{0,8},{8,16},{16,24},{24,32},{32,40},{40,48},{48,56},{56,0},{1,9},... | collective-permute-start | bytes 294920 | tf_op jit(solution)/shard_map/ppermute | solution.py:25
  38.7 24.5 %collective-permute-start.1 = (bf16[96,512]{1,0:T(8,128)(2,1)S(1)}, bf16[96,512]{1,0:T(8,128)(2,1)S(1)}, u32[]{:S(2)}, u32[]{:S(2)}) collective-permute-start(bf16[96,512]{1,0:T(8,128)(2,1)S(1)} %get-tuple-element.17), channel_id=1, source_target_pairs={{0,16},{8,24},{16,32},{24,40},{32,48},{40,56},{48,0},{56,8},{1,17}... | collective-permute-start | bytes 294920 | tf_op jit(solution)/shard_map/ppermute | solution.py:25
  42.1 25.6 %collective-permute-start.2 = (bf16[96,512]{1,0:T(8,128)(2,1)S(1)}, bf16[96,512]{1,0:T(8,128)(2,1)S(1)}, u32[]{:S(2)}, u32[]{:S(2)}) collective-permute-start(bf16[96,512]{1,0:T(8,128)(2,1)S(1)} %get-tuple-element.17), channel_id=1, source_target_pairs={{0,24},{8,32},{16,40},{24,48},{32,56},{40,0},{48,8},{56,16},{1,25}... | collective-permute-start | bytes 294920 | tf_op jit(solution)/shard_map/ppermute | solution.py:25
  46.0 22.4 %collective-permute-start.3 = (bf16[96,512]{1,0:T(8,128)(2,1)S(1)}, bf16[96,512]{1,0:T(8,128)(2,1)S(1)}, u32[]{:S(2)}, u32[]{:S(2)}) collective-permute-start(bf16[96,512]{1,0:T(8,128)(2,1)S(1)} %get-tuple-element.17), channel_id=1, source_target_pairs={{0,32},{8,40},{16,48},{24,56},{32,0},{40,8},{48,16},{56,24},{1,33}... | collective-permute-start | bytes 294920 | tf_op jit(solution)/shard_map/ppermute | solution.py:25
  53.2 15.8 %collective-permute-start.4 = (bf16[96,512]{1,0:T(8,128)(2,1)S(1)}, bf16[96,512]{1,0:T(8,128)(2,1)S(1)}, u32[]{:S(2)}, u32[]{:S(2)}) collective-permute-start(bf16[96,512]{1,0:T(8,128)(2,1)S(1)} %get-tuple-element.17), channel_id=1, source_target_pairs={{0,40},{8,48},{16,56},{24,0},{32,8},{40,16},{48,24},{56,32},{1,41}... | collective-permute-start | bytes 294920 | tf_op jit(solution)/shard_map/ppermute | solution.py:25
  56.2 16.6 %collective-permute-start.5 = (bf16[96,512]{1,0:T(8,128)(2,1)S(1)}, bf16[96,512]{1,0:T(8,128)(2,1)S(1)}, u32[]{:S(2)}, u32[]{:S(2)}) collective-permute-start(bf16[96,512]{1,0:T(8,128)(2,1)S(1)} %get-tuple-element.17), channel_id=1, source_target_pairs={{0,48},{8,56},{16,0},{24,8},{32,16},{40,24},{48,32},{56,40},{1,49}... | collective-permute-start | bytes 294920 | tf_op jit(solution)/shard_map/ppermute | solution.py:25
  63.2 10.2 %collective-permute-start.6 = (bf16[96,512]{1,0:T(8,128)(2,1)S(1)}, bf16[96,512]{1,0:T(8,128)(2,1)S(1)}, u32[]{:S(2)}, u32[]{:S(2)}) collective-permute-start(bf16[96,512]{1,0:T(8,128)(2,1)S(1)} %get-tuple-element.17), channel_id=1, source_target_pairs={{0,56},{8,0},{16,8},{24,16},{32,24},{40,32},{48,40},{56,48},{1,57}... | collective-permute-start | bytes 294920 | tf_op jit(solution)/shard_map/ppermute | solution.py:25
  106.9 30.2 %collective-permute-start.7 = (bf16[192,1536]{1,0:T(8,128)(2,1)S(1)}, bf16[192,1536]{1,0:T(8,128)(2,1)S(1)}, u32[]{:S(2)}, u32[]{:S(2)}) collective-permute-start(bf16[192,1536]{1,0:T(8,128)(2,1)S(1)} %reduce_sum.60), channel_id=1, source_target_pairs={{0,1},{1,0},{2,3},{3,2},{4,5},{5,4},{6,7},{7,6},{8,9},{9,8},{10,11... | collective-permute-start | bytes 1769480 | tf_op jit(solution)/shard_map/ppermute | solution.py:25
  138.8 25.9 %all-to-all-start.2 = ((bf16[4,192,1536]{2,1,0:T(8,128)(2,1)}), bf16[4,192,1536]{2,1,0:T(8,128)(2,1)S(1)}, u32[]{:S(2)}, u32[]{:S(2)}) async-start(bf16[4,192,1536]{2,1,0:T(8,128)(2,1)} %broadcast_in_dim.110), calls=%async_computation.2 | async-start | bytes 4718592 | tf_op jit(solution)/shard_map/all_to_all | solution.py:65
  155.7 18.3 %copy-start.11 = (pred[384,272]{0,1:T(8,128)(4,1)}, pred[384,272]{0,1:T(8,128)(4,1)S(1)}, u32[]{:S(2)}) copy-start(pred[384,272]{0,1:T(8,128)(4,1)S(1)} %get-tuple-element.51) | copy-start | bytes 313348
  155.7 22.1 %copy-start.9 = (pred[384,272]{0,1:T(8,128)(4,1)}, pred[384,272]{0,1:T(8,128)(4,1)S(1)}, u32[]{:S(2)}) copy-start(pred[384,272]{0,1:T(8,128)(4,1)S(1)} %get-tuple-element.52) | copy-start | bytes 313348
  209.3 16.8 %collective-permute-start.8 = (bf16[192,528]{1,0:T(8,128)(2,1)S(1)}, bf16[192,528]{1,0:T(8,128)(2,1)S(1)}, u32[]{:S(2)}, u32[]{:S(2)}) collective-permute-start(bf16[192,528]{1,0:T(8,128)(2,1)S(1)} %pad_maximum_fusion.3), channel_id=1, source_target_pairs={{0,1},{1,0},{2,3},{3,2},{4,5},{5,4},{6,7},{7,6},{8,9},{9,8},{10,11... | collective-permute-start | bytes 608264 | tf_op jit(solution)/shard_map/ppermute | solution.py:25
  228.4 13.0 %all-to-all-start.4 = ((bf16[4,192,512]{2,1,0:T(8,128)(2,1)}), bf16[4,192,512]{2,1,0:T(8,128)(2,1)S(1)}, u32[]{:S(2)}, u32[]{:S(2)}) async-start(bf16[4,192,512]{2,1,0:T(8,128)(2,1)} %broadcast_in_dim.122), calls=%async_computation.4 | async-start | bytes 1572864 | tf_op jit(solution)/shard_map/all_to_all | solution.py:65
  242.9 62.6 %collective-permute-start.10 = (bf16[96,512]{1,0:T(8,128)(2,1)S(1)}, bf16[96,512]{1,0:T(8,128)(2,1)S(1)}, u32[]{:S(2)}, u32[]{:S(2)}) collective-permute-start(bf16[96,512]{1,0:T(8,128)(2,1)S(1)} %get-tuple-element.36), channel_id=1, source_target_pairs={{0,16},{8,24},{16,32},{24,40},{32,48},{40,56},{48,0},{56,8},{1,17}... | collective-permute-start | bytes 294920 | tf_op jit(solution)/shard_map/ppermute | solution.py:25
  275.6 37.1 %collective-permute-start.11 = (bf16[96,512]{1,0:T(8,128)(2,1)S(1)}, bf16[96,512]{1,0:T(8,128)(2,1)S(1)}, u32[]{:S(2)}, u32[]{:S(2)}) collective-permute-start(bf16[96,512]{1,0:T(8,128)(2,1)S(1)} %get-tuple-element.35), channel_id=1, source_target_pairs={{0,24},{8,32},{16,40},{24,48},{32,56},{40,0},{48,8},{56,16},{1,25}... | collective-permute-start | bytes 294920 | tf_op jit(solution)/shard_map/ppermute | solution.py:25
  290.8 29.2 %collective-permute-start.12 = (bf16[96,512]{1,0:T(8,128)(2,1)S(1)}, bf16[96,512]{1,0:T(8,128)(2,1)S(1)}, u32[]{:S(2)}, u32[]{:S(2)}) collective-permute-start(bf16[96,512]{1,0:T(8,128)(2,1)S(1)} %get-tuple-element.34), channel_id=1, source_target_pairs={{0,32},{8,40},{16,48},{24,56},{32,0},{40,8},{48,16},{56,24},{1,33}... | collective-permute-start | bytes 294920 | tf_op jit(solution)/shard_map/ppermute | solution.py:25
  292.8 27.3 %collective-permute-start.13 = (bf16[96,512]{1,0:T(8,128)(2,1)S(1)}, bf16[96,512]{1,0:T(8,128)(2,1)S(1)}, u32[]{:S(2)}, u32[]{:S(2)}) collective-permute-start(bf16[96,512]{1,0:T(8,128)(2,1)S(1)} %get-tuple-element.33), channel_id=1, source_target_pairs={{0,40},{8,48},{16,56},{24,0},{32,8},{40,16},{48,24},{56,32},{1,41}... | collective-permute-start | bytes 294920 | tf_op jit(solution)/shard_map/ppermute | solution.py:25
  300.6 19.4 %collective-permute-start.14 = (bf16[96,512]{1,0:T(8,128)(2,1)S(1)}, bf16[96,512]{1,0:T(8,128)(2,1)S(1)}, u32[]{:S(2)}, u32[]{:S(2)}) collective-permute-start(bf16[96,512]{1,0:T(8,128)(2,1)S(1)} %get-tuple-element.32), channel_id=1, source_target_pairs={{0,48},{8,56},{16,0},{24,8},{32,16},{40,24},{48,32},{56,40},{1,49}... | collective-permute-start | bytes 294920 | tf_op jit(solution)/shard_map/ppermute | solution.py:25
  305.4 14.6 %collective-permute-start.15 = (bf16[96,512]{1,0:T(8,128)(2,1)S(1)}, bf16[96,512]{1,0:T(8,128)(2,1)S(1)}, u32[]{:S(2)}, u32[]{:S(2)}) collective-permute-start(bf16[96,512]{1,0:T(8,128)(2,1)S(1)} %get-tuple-element.31), channel_id=1, source_target_pairs={{0,56},{8,0},{16,8},{24,16},{32,24},{40,32},{48,40},{56,48},{1,57}... | collective-permute-start | bytes 294920 | tf_op jit(solution)/shard_map/ppermute | solution.py:25
  312.7 13.1 %collective-permute-start.9 = (bf16[96,512]{1,0:T(8,128)(2,1)S(1)}, bf16[96,512]{1,0:T(8,128)(2,1)S(1)}, u32[]{:S(2)}, u32[]{:S(2)}) collective-permute-start(bf16[96,512]{1,0:T(8,128)(2,1)S(1)} %get-tuple-element.30), channel_id=1, source_target_pairs={{0,8},{8,16},{16,24},{24,32},{32,40},{40,48},{48,56},{56,0},{1,9},... | collective-permute-start | bytes 294920 | tf_op jit(solution)/shard_map/ppermute | solution.py:25
  (12 other events, 32.2 us)
